TPU v7x, 512 devices: a whole 4x4x16 slice. The times are simulated.
512 devices in a mesh: gx: 16 (over y, z_hi, core), gy: 32 (over z_lo, x).
Axes of the slice: x: 4, y: 4, z: 16 (z_hi: 2, z_lo: 8; z = z_hi * 8 + z_lo), core: 2. Of those that a mesh axis runs over, the one named last changes fastest.
Arguments:
- layer_input: bfloat16 [16384, 2048], P('gy', 'gx'), may hold values from -6 to 6
- project_weight: bfloat16 [2048, 3, 2048], P(None, None, 'gx'), may hold values from -0.125 to 0.125
- output_weight: bfloat16 [2048, 2048], P('gx'), may hold values from -0.5 to 0.5
- cache_entries: bfloat16 [32, 3584, 2, 2048], P('gy', None, None, 'gx'), may hold values from -400 to 400, as said below
- cached_lengths: int32 [32], replicated, may hold values from 1 to 3584, as said below
- final_gain: bfloat16 [2048], P('gx'), may hold values from 0.099609375 to 1.8984375
- head_weight: bfloat16 [76032, 2048], P('gy', 'gx'), may hold values from -0.125 to 0.125
Outputs:
- layer_output: bfloat16 [16384, 2048], P('gy', 'gx')
- appended_entries: bfloat16 [16384, 2, 2048], P('gy', None, 'gx')
- logit_scale: float32 [32], P('gx')
- logit_peak: float32 [32], P('gx')
Inputs may be any that keep to these rules, and one draw needn't show every extreme that they name: `cached_lengths`: every request has one cached slot or more; in every draw one request uses all 3584 slots and another exactly one. `cache_entries`: slots at or beyond a request's cached length are never read.
All inputs are finite; a program needn't handle non-finite values.
Results may differ from a plain program's by a relative error of at most 0.015.
Values may be sent and summed in bfloat16 or wider, within the bound.
No kernel may reach another device: no remote copies, remote signals or barrier semaphores. Data moves between devices by JAX's collectives and lax.ppermute only.
A program may use at most 64 MiB of HBM per device.

v0:
```python
import jax
import jax.numpy as jnp
from jax import lax
from jax.sharding import PartitionSpec as P

D = 2048
HEAD_DIM = 128
VOCAB = 76032


NEG_FILL = -1e30


def combined_all(part, axis, combine):
    gathered = jax.tree.map(lambda a: lax.all_gather(a, axis), part)

    def take(source):
        return jax.tree.map(lambda a: lax.dynamic_index_in_dim(a, source, 0, False), gathered)

    return lax.fori_loop(
        1, lax.axis_size(axis), lambda source, state: combine(state, take(source)), take(0)
    )


def fold_scores(carried, queries, key_block, value_block, allowed):
    running_max, mass_sum, weighted = carried
    scores = jnp.einsum(
        "qhd,khd->hqk", queries, key_block, preferred_element_type=jnp.float32
    ) * HEAD_DIM ** (-0.5)
    scores = jnp.where(allowed, scores, NEG_FILL)
    new_max = jnp.maximum(running_max, jnp.max(scores, axis=2))
    weights = jnp.where(allowed, jnp.exp(scores - new_max[:, :, None]), 0.0)
    factor = jnp.exp(running_max - new_max)
    mass_sum = mass_sum * factor + jnp.sum(weights, axis=2)
    weighted = weighted * factor[:, :, None] + jnp.einsum(
        "hqk,khd->hqd", weights, value_block.astype(jnp.float32), precision=lax.Precision.HIGHEST
    )
    return (new_max, mass_sum, weighted)


def cache_pass(queries, cache_part, live_slots, block_rows):
    query_rows, head_count, head_width = queries.shape
    block_count = cache_part.shape[0] // block_rows
    live_slots = jnp.clip(live_slots, 0, cache_part.shape[0])
    initial = (
        jnp.full((head_count, query_rows), NEG_FILL, jnp.float32),
        jnp.zeros((head_count, query_rows), jnp.float32),
        jnp.zeros((head_count, query_rows, head_width), jnp.float32),
    )

    def advance(block_index, carried):
        cache_piece = lax.dynamic_slice_in_dim(cache_part, block_index * block_rows, block_rows, 0)
        key_block = cache_piece[:, 0].reshape(block_rows, head_count, head_width)
        value_block = cache_piece[:, 1].reshape(block_rows, head_count, head_width)
        places = block_index * block_rows + jnp.arange(block_rows, dtype=jnp.int32)
        allowed = (places < live_slots)[None, None, :]
        return fold_scores(carried, queries, key_block, value_block, allowed)

    return lax.fori_loop(0, block_count, advance, initial)


def combine_stats(earlier, other_side):
    return (earlier[0] + other_side[0], jnp.maximum(earlier[1], other_side[1]))


def per_device(
    layer_input,
    project_weight,
    output_weight,
    cache_entries,
    cached_lengths,
    final_gain,
    head_weight,
):
    new_rows = layer_input.shape[0]
    head_count = output_weight.shape[0] // HEAD_DIM
    request = lax.axis_index("gy")
    own_len = lax.dynamic_index_in_dim(cached_lengths, request, 0, keepdims=False)
    features = lax.all_gather(layer_input, "gx", axis=1, tiled=True)
    widened = features.astype(jnp.float32)
    normed = (
        widened * lax.rsqrt(jnp.mean(widened * widened, axis=1, keepdims=True) + 1e-06)
    ).astype(jnp.bfloat16)
    projected = jnp.einsum(
        "td,dcf->tcf", normed, project_weight, preferred_element_type=jnp.float32
    )
    rounded = projected.astype(jnp.bfloat16)
    queries = rounded[:, 0].reshape(new_rows, head_count, HEAD_DIM)
    new_keys = rounded[:, 1].reshape(new_rows, head_count, HEAD_DIM)
    new_values = rounded[:, 2].reshape(new_rows, head_count, HEAD_DIM)
    appended = rounded[:, 1:3]
    cache_local = cache_entries[0]
    cache_slots = cache_local.shape[0]
    block_rows = min(256, cache_slots // 2)
    carried = cache_pass(queries, cache_local, own_len, block_rows)
    causal = (jnp.arange(new_rows)[None, :] <= jnp.arange(new_rows)[:, None])[None]
    carried = fold_scores(carried, queries, new_keys, new_values, causal)
    attended = (carried[2] / carried[1][:, :, None]).astype(jnp.bfloat16)
    attended = jnp.transpose(attended, (1, 0, 2)).reshape(new_rows, head_count * HEAD_DIM)
    partial_out = jnp.dot(attended, output_weight, preferred_element_type=jnp.float32)
    branch_sum = lax.psum_scatter(
        partial_out.astype(jnp.bfloat16), "gx", scatter_dimension=1, tiled=True
    ).astype(jnp.float32)
    layer_output = (layer_input.astype(jnp.float32) + branch_sum).astype(jnp.bfloat16)
    last_row = layer_output[new_rows - 1 :]
    every_last = lax.all_gather(last_row, "gy", axis=0, tiled=True)
    last_wide = every_last.astype(jnp.float32)
    square_part = jnp.sum(last_wide * last_wide, axis=1)
    gained = (last_wide * final_gain.astype(jnp.float32)).astype(jnp.bfloat16)
    logit_part = jnp.einsum("rd,vd->rv", gained, head_weight, preferred_element_type=jnp.float32)
    logit_rows, square_rows = (
        lax.psum_scatter(logit_part, "gx", scatter_dimension=0, tiled=True),
        lax.psum_scatter(square_part, "gx", scatter_dimension=0, tiled=True),
    )
    logits = logit_rows * lax.rsqrt(square_rows / D + 1e-06)[:, None]
    square_sums = jnp.sum(logits * logits, axis=1)
    row_peaks = jnp.max(logits, axis=1)
    total_squares, logit_peak = combined_all((square_sums, row_peaks), "gy", combine_stats)
    logit_scale = jnp.sqrt(total_squares / VOCAB)
    return (layer_output, appended, logit_scale, logit_peak)


def solution(mesh):
    return jax.shard_map(
        per_device,
        mesh=mesh,
        in_specs=(
            P("gy", "gx"),
            P(None, None, "gx"),
            P("gx", None),
            P("gy", None, None, "gx"),
            P(),
            P("gx"),
            P("gy", "gx"),
        ),
        out_specs=(P("gy", "gx"), P("gy", None, "gx"), P("gx"), P("gx")),
        check_vma=False,
    )
```

profile of v0, /device:TPU:0, one launch (start us, length us, event | category | flops | bytes accessed | tf_op | source)
XLA Modules:
  0.0 776.4 jit_solution(6854591349324929596)
XLA Ops:
  8.0 3.0 copy.20
  12.2 88.2 %all-gather.5.cloned.1.call-done = bf16[512,2048]{1,0:T(8,128)(2,1)} async-done(((bf16[512,128]{1,0:T(8,128)(2,1)}), bf16[512,2048]{1,0:T(8,128)(2,1)}) %all-gather.5.cloned.1.call-update) | async-done | bytes 2097168 | tf_op jit(solution)/shard_map/all_gather | solution.py:79
  100.4 2.2 fusion.13
  104.9 57.1 %while.36 = (s32[]{:T(128)}, f32[1,512]{1,0:T(1,128)S(1)}, f32[1,512]{1,0:T(1,128)}, f32[1,512,128]{2,1,0:T(8,128)S(1)}, s32[]{:T(128)}, /*index=5*/bf16[3584,2,...) while((s32[]{:T(128)}, f32[1,512]{1,0:T(1,128)S(1)}, ...), condition=%wide.region_4.5_spmd.clone, body=%wide.region_1.4_spmd.clone.sunk | while | flops 236129280 | bytes 2393295 | solution.py:59
  106.7 1.6 fusion.53
  110.8 1.6 fusion.53
  115.0 1.6 fusion.53
  119.1 1.6 fusion.53
  123.2 1.6 fusion.53
  131.5 1.6 fusion.53
  135.6 1.6 fusion.53
  139.8 1.6 fusion.53
  143.9 1.6 fusion.53
  148.0 1.6 fusion.53
  156.3 1.6 fusion.53
  160.4 1.6 fusion.53
  163.6 1.7 fusion.26
  165.3 2.0 convolution_convert_fusion
  167.3 3.9 copy.17
  171.9 112.6 %reduce-scatter.4.cloned.1.call-done = bf16[128,512]{1,0:T(8,128)(2,1)} async-done(((bf16[2048,512]{1,0:T(8,128)(2,1)}), bf16[128,512]{1,0:T(8,128)(2,1)}) %reduce-scatter.4.cloned.1.call-update) | async-done | bytes 131088
  285.7 112.4 %all-gather.2 = bf16[32,1,128]{2,1,0:T(2,128)(2,1)S(1)} all-gather(bf16[1,1,128]{2,1,0:T(2,128)(2,1)S(1)} %slice_bitcast_fusion.4), channel_id=1, replica_groups=mesh['gx'=16,'gy'=32] {'gy'}, dimensions={0}, use_global_device_ids=true | all-gather | bytes 8448 | tf_op jit(solution)/shard_map/all_gather | solution.py:106
  404.1 62.1 %all-reduce.3 = f32[32]{0:T(128)S(1)} all-reduce(f32[32]{0:T(128)S(1)} %multiply_reduce_fusion.1), channel_id=6, replica_groups=mesh['gx'=16,'gy'=32] {'gx'}, use_global_device_ids=true, to_apply=%region_10.11.clone | all-reduce | flops 32 | bytes 256
  466.2 177.4 %all-reduce.7.cloned.1.call-done = f32[32,2376]{1,0:T(8,128)} async-done(((f32[32,2376]{1,0:T(8,128)}), f32[32,2376]{1,0:T(8,128)}) %all-reduce.7.cloned.1.call-update) | async-done | bytes 304144
  645.3 122.6 %all-reduce.4 = (f32[64]{0:T(128)S(1)}, f32[64]{0:T(128)S(1)}) all-reduce(f32[64]{0:T(128)S(1)} %dynamic-update-slice, f32[64]{0:T(128)S(1)} %dynamic-update-slice.1), channel_id=2, replica_groups=mesh['gx'=16,'gy'=32] {'gy'}, use_global_device_ids=true, to_apply=%add | all-reduce | flops 128 | bytes 1024
  (176 shorter events, 53.4 us)
Async XLA Ops:
  7.2 95.5 %copy-start = (bf16[2048,3,128]{2,0,1:T(8,128)(2,1)S(1)}, bf16[2048,3,128]{2,0,1:T(8,128)(2,1)}, u32[]{:S(2)}) copy-start(bf16[2048,3,128]{2,0,1:T(8,128)(2,1)} %param.12) | copy-start | bytes 4718596
  7.2 3.8 copy-start.8
  7.2 93.2 %all-gather.5.cloned.1.call-start = ((), (), s32[]{:S(2)}) async-start(), calls=%async_computation.1 | async-start | bytes 2228224 | tf_op jit(solution)/shard_map/all_gather | solution.py:79
  7.9 276.6 %reduce-scatter.4.cloned.1.call-start = ((), (), s32[]{:S(2)}) async-start(), calls=%async_computation.2 | async-start | bytes 2228224
  100.4 2.2 copy-start.1
  103.9 0.9 copy-start.2
  162.0 3.3 copy-start.5
  171.2 0.7 copy-start.9
  171.2 114.3 %copy-start.4 = (bf16[512,128]{1,0:T(8,128)(2,1)S(1)}, bf16[512,128]{1,0:T(8,128)(2,1)}, u32[]{:S(2)}) copy-start(bf16[512,128]{1,0:T(8,128)(2,1)} %param.11) | copy-start | bytes 393220
  171.2 226.8 %copy-start.3 = (bf16[2376,128]{1,0:T(8,128)(2,1)S(1)}, bf16[2376,128]{1,0:T(8,128)(2,1)}, u32[]{:S(2)}) copy-start(bf16[2376,128]{1,0:T(8,128)(2,1)} %param.17) | copy-start | bytes 1824772
  171.2 231.7 %slice-start = ((bf16[512,3,128]{2,0,1:T(8,128)(2,1)}), bf16[512,2,128]{2,0,1:T(8,128)(2,1)S(1)}, s32[]{:S(2)}) async-start(bf16[512,3,128]{2,0,1:T(8,128)(2,1)} %copy-done.2), calls=%async_computation.4 | async-start | bytes 524288 | tf_op jit(solution)/shard_map/slice | solution.py:91
  171.3 472.4 %all-reduce.7.cloned.1.call-start = ((), (), s32[]{:S(2)}) async-start(), calls=%async_computation.3 | async-start | bytes 622592
  285.6 484.3 %copy-start.6 = (bf16[512,128]{1,0:T(8,128)(2,1)}, bf16[512,128]{1,0:T(8,128)(2,1)S(1)}, u32[]{:S(2)}) copy-start(bf16[512,128]{1,0:T(8,128)(2,1)S(1)} %add_convert_fusion) | copy-start | bytes 393220
  769.4 0.5 copy-start.7
Sparse Core Ops, SparseCore 0:
  11.2 89.1 all-gather.4
  171.4 113.0 reduce-scatter.3
  399.2 244.3 all-reduce.6
where the time goes:
time: 778 us; the launch traced here: 776 us
  waiting for transfers between devices  379 us (49%)
  blocking collectives  297 us (38%)
  matrix products  44 us (6%)
  other arithmetic  25.5 us (3%)
  between operations  15.9 us (2%)
  local copies, waits for them, and re-layouts  13.4 us (2%)
    unnamed x5, waiting for transfers between devices  291 us
    unnamed x2, blocking collectives  185 us
    all_gather x1, blocking collectives, per_device(): every_last = lax.all_gather(last_row, 'gy', axis=0, tiled=True)  112 us
    all_gather x1, waiting for transfers between devices, per_device(): features = lax.all_gather(layer_input, 'gx', axis=1, tiled=True)  88.2 us
    dot_general x15, matrix products, fold_scores(): jnp.einsum('hqk,khd->hqd', weights, value_block.astype(jnp.float32), prec...  23.6 us
    add x15, other arithmetic, fold_scores(): mass_sum = mass_sum * factor + jnp.sum(weights, axis=2)  17.9 us
    dot_general x15, matrix products, fold_scores(): jnp.einsum('qhd,khd->hqk', queries, key_block, preferred_element_type=jnp...  16.1 us
  transfers between devices with their start and end apart: 3, of which 3 were waited for; matrix products, arithmetic and copies ran while one was open for 1% of the time, Pallas kernels for 0%

commit v1 on v0

v1 whole, which is shorter than its diff:
```python
import jax
import jax.numpy as jnp
import numpy as np
from jax import lax
from jax.sharding import Mesh
from jax.sharding import PartitionSpec as P

D = 2048
HEAD_DIM = 128
VOCAB = 76032

NEG_FILL = -1e30

GX = ("y", "zh", "c")
GY = ("zl", "x")


def fold_scores(carried, queries, key_block, value_block, allowed):
    running_max, mass_sum, weighted = carried
    scores = jnp.einsum(
        "qhd,khd->hqk", queries, key_block, preferred_element_type=jnp.float32
    ) * HEAD_DIM ** (-0.5)
    scores = jnp.where(allowed, scores, NEG_FILL)
    new_max = jnp.maximum(running_max, jnp.max(scores, axis=2))
    weights = jnp.where(allowed, jnp.exp(scores - new_max[:, :, None]), 0.0)
    factor = jnp.exp(running_max - new_max)
    mass_sum = mass_sum * factor + jnp.sum(weights, axis=2)
    weighted = weighted * factor[:, :, None] + jnp.einsum(
        "hqk,khd->hqd", weights, value_block.astype(jnp.float32), precision=lax.Precision.HIGHEST
    )
    return (new_max, mass_sum, weighted)


def cache_pass(queries, cache_part, live_slots, block_rows):
    query_rows, head_count, head_width = queries.shape
    block_count = cache_part.shape[0] // block_rows
    initial = (
        jnp.full((head_count, query_rows), NEG_FILL, jnp.float32),
        jnp.zeros((head_count, query_rows), jnp.float32),
        jnp.zeros((head_count, query_rows, head_width), jnp.float32),
    )

    def advance(block_index, carried):
        cache_piece = lax.dynamic_slice_in_dim(cache_part, block_index * block_rows, block_rows, 0)
        key_block = cache_piece[:, 0].reshape(block_rows, head_count, head_width)
        value_block = cache_piece[:, 1].reshape(block_rows, head_count, head_width)
        places = block_index * block_rows + jnp.arange(block_rows, dtype=jnp.int32)
        allowed = (places < live_slots)[None, None, :]
        return fold_scores(carried, queries, key_block, value_block, allowed)

    return lax.fori_loop(0, block_count, advance, initial)


def last_token_attention(query, cache_local, live_slots, new_keys, new_values):
    slots, head_count, head_width = cache_local.shape[0], query.shape[1], query.shape[2]
    cache_keys = cache_local[:, 0].reshape(slots, head_count, head_width)
    cache_values = cache_local[:, 1].reshape(slots, head_count, head_width)
    scale = HEAD_DIM ** (-0.5)
    cache_scores = jnp.einsum("qhd,khd->hqk", query, cache_keys, preferred_element_type=jnp.float32) * scale
    new_scores = jnp.einsum("qhd,khd->hqk", query, new_keys, preferred_element_type=jnp.float32) * scale
    live = (jnp.arange(slots, dtype=jnp.int32) < live_slots)[None, None, :]
    cache_scores = jnp.where(live, cache_scores, NEG_FILL)
    row_max = jnp.maximum(jnp.max(cache_scores, axis=2), jnp.max(new_scores, axis=2))
    cache_weights = jnp.where(live, jnp.exp(cache_scores - row_max[:, :, None]), 0.0)
    new_weights = jnp.exp(new_scores - row_max[:, :, None])
    mass = jnp.sum(cache_weights, axis=2) + jnp.sum(new_weights, axis=2)
    total = jnp.einsum(
        "hqk,khd->hqd", cache_weights, cache_values.astype(jnp.float32), precision=lax.Precision.HIGHEST
    ) + jnp.einsum(
        "hqk,khd->hqd", new_weights, new_values.astype(jnp.float32), precision=lax.Precision.HIGHEST
    )
    return (total / mass[:, :, None]).astype(jnp.bfloat16)


def per_device(
    layer_input,
    project_weight,
    output_weight,
    cache_entries,
    cached_lengths,
    final_gain,
    head_weight,
):
    new_rows, block_cols = layer_input.shape
    n_y, n_zh, n_c = lax.axis_size("y"), lax.axis_size("zh"), lax.axis_size("c")
    n_gx = n_y * n_zh * n_c
    n_gy = lax.axis_size("zl") * lax.axis_size("x")
    head_count = output_weight.shape[0] // HEAD_DIM
    request = lax.axis_index("zl") * lax.axis_size("x") + lax.axis_index("x")
    own_len = lax.dynamic_index_in_dim(cached_lengths, request, 0, keepdims=False)

    pair = lax.all_gather(layer_input, "zh", axis=1, tiled=True)
    features = lax.all_gather(pair, ("y", "c"), axis=1, tiled=True)
    weight_rows = project_weight.reshape(n_y, n_zh, n_c, block_cols, 3, project_weight.shape[-1])
    weight_rows = jnp.transpose(weight_rows, (0, 2, 1, 3, 4, 5)).reshape(project_weight.shape)

    widened = features.astype(jnp.float32)
    normed = (
        widened * lax.rsqrt(jnp.mean(widened * widened, axis=1, keepdims=True) + 1e-06)
    ).astype(jnp.bfloat16)
    projected = jnp.einsum(
        "td,dcf->tcf", normed, weight_rows, preferred_element_type=jnp.float32
    )
    rounded = projected.astype(jnp.bfloat16)
    queries = rounded[:, 0].reshape(new_rows, head_count, HEAD_DIM)
    new_keys = rounded[:, 1].reshape(new_rows, head_count, HEAD_DIM)
    new_values = rounded[:, 2].reshape(new_rows, head_count, HEAD_DIM)
    appended = rounded[:, 1:3]
    cache_local = cache_entries[0]

    last_attended = last_token_attention(
        queries[new_rows - 1 :], cache_local, own_len, new_keys, new_values
    )
    last_attended = jnp.transpose(last_attended, (1, 0, 2)).reshape(1, head_count * HEAD_DIM)
    last_term = jnp.dot(last_attended, output_weight, preferred_element_type=jnp.float32)
    last_term = last_term.astype(jnp.bfloat16).reshape(n_gx, block_cols)
    last_terms = lax.all_to_all(last_term, GX, 0, 0, tiled=True)
    last_row = (
        layer_input[new_rows - 1].astype(jnp.float32) + jnp.sum(last_terms.astype(jnp.float32), axis=0)
    ).astype(jnp.bfloat16)
    every_last = lax.all_to_all(
        jnp.broadcast_to(last_row[None], (n_gy, block_cols)), GY, 0, 0, tiled=True
    )
    last_wide = every_last.astype(jnp.float32)
    square_part = jnp.sum(last_wide * last_wide, axis=1, keepdims=True)
    gained = (last_wide * final_gain.astype(jnp.float32)).astype(jnp.bfloat16)
    logit_part = jnp.einsum("rd,vd->rv", gained, head_weight, preferred_element_type=jnp.float32)
    packed = jnp.concatenate([logit_part, square_part], axis=1)
    packed = lax.all_to_all(packed, GX, 0, 0, tiled=True)
    own_requests = packed.shape[0] // n_gx
    packed = jnp.sum(packed.reshape(n_gx, own_requests, packed.shape[1]), axis=0)
    vocab_part = logit_part.shape[1]
    logits = packed[:, :vocab_part] * lax.rsqrt(packed[:, vocab_part:] / D + 1e-06)
    stats = jnp.stack([jnp.sum(logits * logits, axis=1), jnp.max(logits, axis=1)], axis=0)
    stats = lax.all_to_all(
        jnp.broadcast_to(stats[None], (n_gy,) + stats.shape), GY, 0, 0, tiled=True
    )
    logit_scale = jnp.sqrt(jnp.sum(stats[:, 0], axis=0) / VOCAB)
    logit_peak = jnp.max(stats[:, 1], axis=0)

    cache_slots = cache_local.shape[0]
    block_rows = min(256, cache_slots // 2)
    carried = cache_pass(queries, cache_local, own_len, block_rows)
    causal = (jnp.arange(new_rows)[None, :] <= jnp.arange(new_rows)[:, None])[None]
    carried = fold_scores(carried, queries, new_keys, new_values, causal)
    attended = (carried[2] / carried[1][:, :, None]).astype(jnp.bfloat16)
    attended = jnp.transpose(attended, (1, 0, 2)).reshape(new_rows, head_count * HEAD_DIM)
    out_cols = output_weight.reshape(-1, n_y, n_zh, n_c, block_cols)
    out_cols = jnp.transpose(out_cols, (0, 1, 3, 2, 4)).reshape(output_weight.shape)
    partial_out = jnp.dot(attended, out_cols, preferred_element_type=jnp.float32).astype(jnp.bfloat16)
    branch = lax.psum_scatter(partial_out, ("y", "c"), scatter_dimension=1, tiled=True)
    branch = lax.psum_scatter(branch, "zh", scatter_dimension=1, tiled=True)
    layer_output = (layer_input.astype(jnp.float32) + branch.astype(jnp.float32)).astype(jnp.bfloat16)
    return (layer_output, appended, logit_scale, logit_peak)


def solution(mesh):
    devices = np.asarray(mesh.devices)
    n_gx, n_gy = devices.shape
    fine = Mesh(devices.reshape(n_gx // 4, 2, 2, n_gy // 4, 4), GX + GY)
    return jax.shard_map(
        per_device,
        mesh=fine,
        in_specs=(
            P(GY, GX),
            P(None, None, GX),
            P(GX, None),
            P(GY, None, None, GX),
            P(),
            P(GX),
            P(GY, GX),
        ),
        out_specs=(P(GY, GX), P(GY, None, GX), P(GX), P(GX)),
        check_vma=False,
    )
```

time: 778 us -> 232 us (0.30)
  the two profiles are of different devices: /device:TPU:0 before, /device:TPU:8 now
where the time goes in v1:
time: 232 us; the launch traced here: 231 us
  waiting for transfers between devices  69.2 us (30%)
  blocking collectives  68.2 us (29%)
  matrix products  23.5 us (10%)
  other arithmetic  21.2 us (9%)
  starting transfers between devices  17.9 us (8%)
  between operations  16.6 us (7%)
  local copies, waits for them, and re-layouts  13.7 us (6%)
    all_gather x1, waiting for transfers between devices, per_device(): features = lax.all_gather(pair, ('y', 'c'), axis=1, tiled=True)  33.7 us
    all_to_all x1, blocking collectives, per_device(): last_terms = lax.all_to_all(last_term, GX, 0, 0, tiled=True)  28.6 us
    all_gather x1, blocking collectives, per_device(): pair = lax.all_gather(layer_input, 'zh', axis=1, tiled=True)  20.3 us
    all_to_all x1, blocking collectives, per_device(): packed = lax.all_to_all(packed, GX, 0, 0, tiled=True)  19.3 us
    all_to_all x1, starting transfers between devices, per_device(): lax.all_to_all(jnp.broadcast_to(stats[None], (n_gy,) + stats.shape), GY,...  12.5 us
    all_to_all x1, waiting for transfers between devices, per_device(): lax.all_to_all(jnp.broadcast_to(last_row[None], (n_gy, block_cols)), GY,...  12.4 us
    dot_general x15, matrix products, fold_scores(): jnp.einsum('hqk,khd->hqd', weights, value_block.astype(jnp.float32), prec...  12.3 us
    all_to_all x1, waiting for transfers between devices, per_device(): lax.all_to_all(jnp.broadcast_to(stats[None], (n_gy,) + stats.shape), GY,...  11.8 us
  transfers between devices with their start and end apart: 5, of which 4 were waited for; matrix products, arithmetic and copies ran while one was open for 7% of the time, Pallas kernels for 0%

profile of v1, /device:TPU:8, one launch (start us, length us, event | category | flops | bytes accessed | tf_op | source)
XLA Modules:
  0.0 231.1 jit_solution(5513581570870723583)
XLA Ops:
  7.2 20.3 %all_gather.6 = bf16[512,256]{1,0:T(8,128)(2,1)} all-gather(bf16[512,128]{1,0:T(8,128)(2,1)} %param.9), channel_id=1, replica_groups=mesh['y'=4,'zh'=2,'c'=2,'zl'=8,'x'=4] {'zh'}, dimensions={1}, use_global_device_ids=true | all-gather | bytes 393216 | tf_op jit(solution)/shard_map/all_gather | solution.py:92
  27.6 2.9 %copy.74 = bf16[4,2,2,128,3,128]{5,3,2,1,0,4:T(8,128)(2,1)} copy(bf16[4,2,2,128,3,128]{5,3,1,2,0,4:T(8,128)(2,1)} %bitcast.144) | data formatting | bytes 3145728 | tf_op jit(solution)/shard_map/transpose | solution.py:95
  31.5 1.0 copy.75
  32.5 1.9 copy.76
  35.0 33.7 %all-gather.2.cloned.1.call-done = bf16[512,2048]{1,0:T(8,128)(2,1)} async-done(((bf16[512,256]{1,0:T(8,128)(2,1)}), bf16[512,2048]{1,0:T(8,128)(2,1)}) %all-gather.2.cloned.1.call-update) | async-done | bytes 2097168 | tf_op jit(solution)/shard_map/all_gather | solution.py:93
  68.7 2.2 fusion.13
  70.9 2.7 %fusion.20 = bf16[512,3,128]{2,0,1:T(8,128)(2,1)S(1)} fusion(bf16[2048,3,128]{2,0,1:T(8,128)(2,1)} %bitcast.145, bf16[512,2048]{1,0:T(8,128)(2,1)S(1)} %copy-done.1, f32[512]{0:T(512)S(1)} %add_rsqrt_fusion), kind=kOutput, calls=%fused_computation.34 | convolution fusion | flops 808648704 | bytes 4065280 | tf_op jit(solution)/shard_map/td,dcf->tcf/dot_general | solution.py:101
  74.4 1.3 fusion.53
  75.7 25.9 %while.18 = (s32[]{:T(128)}, f32[1,512]{1,0:T(1,128)S(1)}, f32[1,512]{1,0:T(1,128)S(1)}, f32[1,512,128]{2,1,0:T(8,128)S(1)}, s32[]{:T(128)}, /*index=5*/bf16[358...) while((s32[]{:T(128)}, f32[1,512]{1,0:T(1,128)S(1)}, ...), condition=%wide.region_4.5_spmd.clone, body=%wide.region_1.0_spmd.clone.sunk | while | flops 236129280 | bytes 2393807 | solution.py:51
  101.6 1.4 fusion.31
  103.0 2.0 fusion.26
  105.1 2.1 convolution_convert_fusion
  108.3 1.2 fusion.39
  110.9 1.3 fusion.51
  114.9 28.6 %all_to_all.26 = bf16[16,1,128]{2,1,0:T(2,128)(2,1)S(1)} all-to-all(bf16[16,1,128]{2,1,0:T(2,128)(2,1)S(1)} %copy.77), channel_id=1, replica_groups=mesh['y'=4,'zh'=2,'c'=2,'zl'=8,'x'=4] {'y','zh','c'}, dimensions={0} | all-to-all | bytes 8192 | tf_op jit(solution)/shard_map/all_to_all | solution.py:117
  144.2 5.3 %all-to-all-start.1 = ((bf16[32,1,128]{2,1,0:T(2,128)(2,1)}), bf16[32,1,128]{2,1,0:T(2,128)(2,1)S(1)}, u32[]{:S(2)}, u32[]{:S(2)}) async-start(bf16[32,1,128]{2,1,0:T(2,128)(2,1)} %broadcast_in_dim.94), calls=%async_computation.2 | async-start | bytes 32768 | tf_op jit(solution)/shard_map/all_to_all | solution.py:121
  149.6 12.4 %all-to-all-done.1 = bf16[32,1,128]{2,1,0:T(2,128)(2,1)S(1)} async-done(((bf16[32,1,128]{2,1,0:T(2,128)(2,1)}), bf16[32,1,128]{2,1,0:T(2,128)(2,1)S(1)}, u32[]{:S(2)}, u32[]{:S(2)}) %all-to-all-start.1) | async-done | bytes 8224 | tf_op jit(solution)/shard_map/all_to_all | solution.py:121
  163.0 19.3 %all_to_all.27 = f32[16,2,2377]{2,1,0:T(2,128)S(1)} all-to-all(f32[16,2,2377]{2,1,0:T(2,128)S(1)} %copy.81), channel_id=1, replica_groups=mesh['y'=4,'zh'=2,'c'=2,'zl'=8,'x'=4] {'y','zh','c'}, dimensions={0} | all-to-all | bytes 608512 | tf_op jit(solution)/shard_map/all_to_all | solution.py:129
  182.6 1.8 copy.86
  185.3 12.5 %all-to-all-start.3 = ((f32[32,2,2]{2,1,0:T(2,128)}), f32[32,2,2]{2,1,0:T(2,128)S(1)}, u32[]{:S(2)}, u32[]{:S(2)}) async-start(f32[32,2,2]{2,1,0:T(2,128)} %broadcast_in_dim.95), calls=%async_computation.4 | async-start | bytes 65536 | tf_op jit(solution)/shard_map/all_to_all | solution.py:135
  197.8 1.0 copy.85
  198.7 11.8 %all-to-all-done.3 = f32[32,2,2]{2,1,0:T(2,128)S(1)} async-done(((f32[32,2,2]{2,1,0:T(2,128)}), f32[32,2,2]{2,1,0:T(2,128)S(1)}, u32[]{:S(2)}, u32[]{:S(2)}) %all-to-all-start.3) | async-done | bytes 544 | tf_op jit(solution)/shard_map/all_to_all | solution.py:135
  211.6 11.3 %reduce-scatter.7.cloned.1.call-done = bf16[128,512]{1,0:T(8,128)(2,1)} async-done(((bf16[256,512]{1,0:T(8,128)(2,1)}), bf16[128,512]{1,0:T(8,128)(2,1)}) %reduce-scatter.7.cloned.1.call-update) | async-done | bytes 131088
  222.9 1.0 copy.87
  (167 shorter events, 34.8 us)
Async XLA Ops:
  7.2 155.2 %copy-start = (bf16[2376,128]{1,0:T(8,128)(2,1)S(1)}, bf16[2376,128]{1,0:T(8,128)(2,1)}, u32[]{:S(2)}) copy-start(bf16[2376,128]{1,0:T(8,128)(2,1)} %param.15) | copy-start | bytes 1824772
  7.2 61.5 %all-gather.2.cloned.1.call-start = ((), (), s32[]{:S(2)}) async-start(), calls=%async_computation.6 | async-start | bytes 2359296 | tf_op jit(solution)/shard_map/all_gather | solution.py:93
  27.5 155.1 %reduce-scatter.5.cloned.1.call-start = ((), (), s32[]{:S(2)}) async-start(), calls=%async_computation.7 | async-start | bytes 2359296 | tf_op jit(solution)/shard_map/reduce_scatter | solution.py:151
  27.6 2.9 %copy-start.5 = (bf16[1,3584,2,128]{3,2,1,0:T(2,128)(2,1)S(1)}, bf16[1,3584,2,128]{3,2,1,0:T(2,128)(2,1)}, u32[]{:S(2)}) copy-start(bf16[1,3584,2,128]{3,2,1,0:T(2,128)(2,1)} %param.12) | copy-start | bytes 5505028
  30.5 1.0 copy-start.2
  31.5 2.9 %copy-start.9 = (s32[32]{0:T(128)S(1)}, s32[32]{0:T(128)}, u32[]{:S(2)}) copy-start(s32[32]{0:T(128)} %param.13) | copy-start | bytes 388
  68.7 2.2 copy-start.1
  73.6 0.8 copy-start.6
  101.6 3.5 %copy-start.4 = (bf16[128,4,2,2,128]{0,4,3,2,1:T(8,128)(2,1)S(1)}, bf16[128,4,2,2,128]{0,4,3,2,1:T(8,128)(2,1)}, u32[]{:S(2)}) copy-start(bf16[128,4,2,2,128]{0,4,3,2,1:T(8,128)(2,1)} %copy.76) | copy-start | bytes 1572868
  105.1 2.1 copy-start.7
  107.2 7.6 %copy-start.3 = (bf16[128,2048]{1,0:T(8,128)(2,1)S(1)}, bf16[128,2048]{1,0:T(8,128)(2,1)}, u32[]{:S(2)}) copy-start(bf16[128,2048]{1,0:T(8,128)(2,1)} %param.11) | copy-start | bytes 1572868
  107.2 36.4 %copy-start.8 = (bf16[512,128]{1,0:T(8,128)(2,1)S(1)}, bf16[512,128]{1,0:T(8,128)(2,1)}, u32[]{:S(2)}) copy-start(bf16[512,128]{1,0:T(8,128)(2,1)} %param.9) | copy-start | bytes 393220
  107.2 42.3 %copy-start.10 = (bf16[128]{0:T(256)(128)(2,1)S(1)}, bf16[128]{0:T(256)(128)(2,1)}, u32[]{:S(2)}) copy-start(bf16[128]{0:T(256)(128)(2,1)} %param.14) | copy-start | bytes 772
  144.2 17.8 %all-to-all-start.1 = ((bf16[32,1,128]{2,1,0:T(2,128)(2,1)}), bf16[32,1,128]{2,1,0:T(2,128)(2,1)S(1)}, u32[]{:S(2)}, u32[]{:S(2)}) async-start(bf16[32,1,128]{2,1,0:T(2,128)(2,1)} %broadcast_in_dim.94), calls=%async_computation.2 | async-start | bytes 32768 | tf_op jit(solution)/shard_map/all_to_all | solution.py:121
  149.5 73.4 %reduce-scatter.7.cloned.1.call-start = ((), (), s32[]{:S(2)}) async-start(), calls=%async_computation.8 | async-start | bytes 393216
  162.7 35.0 %slice-start = ((bf16[512,3,128]{2,0,1:T(8,128)(2,1)}), bf16[512,2,128]{2,0,1:T(8,128)(2,1)S(1)}, s32[]{:S(2)}) async-start(bf16[512,3,128]{2,0,1:T(8,128)(2,1)} %copy-done.6), calls=%async_computation.9 | async-start | bytes 524288 | tf_op jit(solution)/shard_map/slice | solution.py:108
  185.3 25.2 %all-to-all-start.3 = ((f32[32,2,2]{2,1,0:T(2,128)}), f32[32,2,2]{2,1,0:T(2,128)S(1)}, u32[]{:S(2)}, u32[]{:S(2)}) async-start(f32[32,2,2]{2,1,0:T(2,128)} %broadcast_in_dim.95), calls=%async_computation.4 | async-start | bytes 65536 | tf_op jit(solution)/shard_map/all_to_all | solution.py:135
Sparse Core Ops, SparseCore 0:
  27.6 41.0 all-gather.1
  107.3 39.8 reduce-scatter.4
  184.5 38.2 reduce-scatter.6

commit v2 on v1

--- a/solution.py
+++ b/solution.py
@@ -108,12 +108,25 @@
     appended = rounded[:, 1:3]
     cache_local = cache_entries[0]
 
+    out_cols = output_weight.reshape(-1, n_y, n_zh, n_c, block_cols)
+    out_cols = jnp.transpose(out_cols, (0, 1, 3, 2, 4)).reshape(output_weight.shape)
+
+    cache_slots = cache_local.shape[0]
+    block_rows = min(256, cache_slots // 2)
+    carried = cache_pass(queries, cache_local, own_len, block_rows)
+    causal = (jnp.arange(new_rows)[None, :] <= jnp.arange(new_rows)[:, None])[None]
+    carried = fold_scores(carried, queries, new_keys, new_values, causal)
+    attended = (carried[2] / carried[1][:, :, None]).astype(jnp.bfloat16)
+    attended = jnp.transpose(attended, (1, 0, 2)).reshape(new_rows, head_count * HEAD_DIM)
+    partial_out = jnp.dot(attended, out_cols, preferred_element_type=jnp.float32).astype(jnp.bfloat16)
+    branch = lax.psum_scatter(partial_out, ("y", "c"), scatter_dimension=1, tiled=True)
     last_attended = last_token_attention(
         queries[new_rows - 1 :], cache_local, own_len, new_keys, new_values
     )
     last_attended = jnp.transpose(last_attended, (1, 0, 2)).reshape(1, head_count * HEAD_DIM)
-    last_term = jnp.dot(last_attended, output_weight, preferred_element_type=jnp.float32)
-    last_term = last_term.astype(jnp.bfloat16).reshape(n_gx, block_cols)
+    last_term = jnp.dot(last_attended, out_cols, preferred_element_type=jnp.float32)
+    last_term = last_term.astype(jnp.bfloat16).reshape(n_y, n_c, n_zh, block_cols)
+    last_term = jnp.transpose(last_term, (0, 2, 1, 3)).reshape(n_gx, block_cols)
     last_terms = lax.all_to_all(last_term, GX, 0, 0, tiled=True)
     last_row = (
         layer_input[new_rows - 1].astype(jnp.float32) + jnp.sum(last_terms.astype(jnp.float32), axis=0)
@@ -132,25 +145,20 @@
     vocab_part = logit_part.shape[1]
     logits = packed[:, :vocab_part] * lax.rsqrt(packed[:, vocab_part:] / D + 1e-06)
     stats = jnp.stack([jnp.sum(logits * logits, axis=1), jnp.max(logits, axis=1)], axis=0)
-    stats = lax.all_to_all(
-        jnp.broadcast_to(stats[None], (n_gy,) + stats.shape), GY, 0, 0, tiled=True
-    )
+    spread = jnp.broadcast_to(stats[None], (n_gy,) + stats.shape)
+    spread, branch = lax.optimization_barrier((spread, branch))
+    branch = branch.reshape(new_rows, n_zh, block_cols)
+    zh = lax.axis_index("zh")
+    mine = lax.dynamic_index_in_dim(branch, zh, 1, keepdims=False)
+    theirs = lax.dynamic_index_in_dim(branch, 1 - zh, 1, keepdims=False)
+    from_partner = lax.ppermute(theirs, "zh", [(0, 1), (1, 0)])
+    stats = lax.all_to_all(spread, GY, 0, 0, tiled=True)
     logit_scale = jnp.sqrt(jnp.sum(stats[:, 0], axis=0) / VOCAB)
     logit_peak = jnp.max(stats[:, 1], axis=0)
 
-    cache_slots = cache_local.shape[0]
-    block_rows = min(256, cache_slots // 2)
-    carried = cache_pass(queries, cache_local, own_len, block_rows)
-    causal = (jnp.arange(new_rows)[None, :] <= jnp.arange(new_rows)[:, None])[None]
-    carried = fold_scores(carried, queries, new_keys, new_values, causal)
-    attended = (carried[2] / carried[1][:, :, None]).astype(jnp.bfloat16)
-    attended = jnp.transpose(attended, (1, 0, 2)).reshape(new_rows, head_count * HEAD_DIM)
-    out_cols = output_weight.reshape(-1, n_y, n_zh, n_c, block_cols)
-    out_cols = jnp.transpose(out_cols, (0, 1, 3, 2, 4)).reshape(output_weight.shape)
-    partial_out = jnp.dot(attended, out_cols, preferred_element_type=jnp.float32).astype(jnp.bfloat16)
-    branch = lax.psum_scatter(partial_out, ("y", "c"), scatter_dimension=1, tiled=True)
-    branch = lax.psum_scatter(branch, "zh", scatter_dimension=1, tiled=True)
-    layer_output = (layer_input.astype(jnp.float32) + branch.astype(jnp.float32)).astype(jnp.bfloat16)
+    layer_output = (
+        layer_input.astype(jnp.float32) + mine.astype(jnp.float32) + from_partner.astype(jnp.float32)
+    ).astype(jnp.bfloat16)
     return (layer_output, appended, logit_scale, logit_peak)
 
 

time: 232 us -> 236 us (1.017)
  the two profiles are of different devices: /device:TPU:8 before, /device:TPU:2 now
where the time goes in v2:
time: 236 us; the launch traced here: 235 us
  waiting for transfers between devices  86.1 us (36%)
  blocking collectives  49.4 us (21%)
  matrix products  26 us (11%)
  starting transfers between devices  23.3 us (10%)
  other arithmetic  21.2 us (9%)
  between operations  16.9 us (7%)
  local copies, waits for them, and re-layouts  11.7 us (5%)
    all_gather x1, waiting for transfers between devices, per_device(): features = lax.all_gather(pair, ('y', 'c'), axis=1, tiled=True)  35.8 us
    all_to_all x1, blocking collectives, per_device(): last_terms = lax.all_to_all(last_term, GX, 0, 0, tiled=True)  29.1 us
    all_gather x1, blocking collectives, per_device(): pair = lax.all_gather(layer_input, 'zh', axis=1, tiled=True)  20.3 us
    all_to_all x1, waiting for transfers between devices, per_device(): packed = lax.all_to_all(packed, GX, 0, 0, tiled=True)  18.2 us
    dot_general x15, matrix products, fold_scores(): jnp.einsum('hqk,khd->hqd', weights, value_block.astype(jnp.float32), prec...  12.3 us
    all_to_all x1, starting transfers between devices, per_device(): stats = lax.all_to_all(spread, GY, 0, 0, tiled=True)  12.1 us
    ppermute x1, waiting for transfers between devices, per_device(): from_partner = lax.ppermute(theirs, 'zh', [(0, 1), (1, 0)])  11.7 us
    all_to_all x1, waiting for transfers between devices, per_device(): lax.all_to_all(jnp.broadcast_to(last_row[None], (n_gy, block_cols)), GY,...  11.3 us
  transfers between devices with their start and end apart: 6, of which 5 were waited for; matrix products, arithmetic and copies ran while one was open for 8% of the time, Pallas kernels for 0%

profile of v2, /device:TPU:2, one launch (start us, length us, event | category | flops | bytes accessed | tf_op | source)
XLA Modules:
  0.0 235.5 jit_solution(10708358941711489006)
XLA Ops:
  7.2 20.3 %all_gather.6 = bf16[512,256]{1,0:T(8,128)(2,1)} all-gather(bf16[512,128]{1,0:T(8,128)(2,1)} %param.9), channel_id=1, replica_groups=mesh['y'=4,'zh'=2,'c'=2,'zl'=8,'x'=4] {'zh'}, dimensions={1}, use_global_device_ids=true | all-gather | bytes 393216 | tf_op jit(solution)/shard_map/all_gather | solution.py:92
  27.6 2.9 %copy.91 = bf16[4,2,2,128,3,128]{5,3,2,1,0,4:T(8,128)(2,1)} copy(bf16[4,2,2,128,3,128]{5,3,1,2,0,4:T(8,128)(2,1)} %bitcast.153) | data formatting | bytes 3145728 | tf_op jit(solution)/shard_map/transpose | solution.py:95
  30.8 1.3 copy.93
  33.5 35.8 %all-gather.2.cloned.1.call-done = bf16[512,2048]{1,0:T(8,128)(2,1)} async-done(((bf16[512,256]{1,0:T(8,128)(2,1)}), bf16[512,2048]{1,0:T(8,128)(2,1)}) %all-gather.2.cloned.1.call-update) | async-done | bytes 2097168 | tf_op jit(solution)/shard_map/all_gather | solution.py:93
  69.3 2.2 fusion.13
  71.5 2.7 %fusion.20 = bf16[512,3,128]{2,0,1:T(8,128)(2,1)S(1)} fusion(bf16[2048,3,128]{2,0,1:T(8,128)(2,1)} %bitcast.154, bf16[512,2048]{1,0:T(8,128)(2,1)S(1)} %copy-done.2, f32[512]{0:T(512)S(1)} %add_rsqrt_fusion), kind=kOutput, calls=%fused_computation.34 | convolution fusion | flops 808648704 | bytes 4065280 | tf_op jit(solution)/shard_map/td,dcf->tcf/dot_general | solution.py:101
  75.0 1.3 fusion.55
  76.3 25.9 %while.18 = (s32[]{:T(128)}, f32[1,512]{1,0:T(1,128)S(1)}, f32[1,512]{1,0:T(1,128)S(1)}, f32[1,512,128]{2,1,0:T(8,128)S(1)}, s32[]{:T(128)}, /*index=5*/bf16[358...) while((s32[]{:T(128)}, f32[1,512]{1,0:T(1,128)S(1)}, ...), condition=%wide.region_13.14_spmd.clone, body=%wide.region_10.13_spmd.clone.sunk | while | flops 236129280 | bytes 2393807 | solution.py:51
  102.2 1.4 fusion.31
  103.6 2.0 fusion.26
  105.7 2.1 convolution_convert_fusion
  107.8 1.1 fusion.39
  110.5 1.2 fusion.41
  113.1 1.3 fusion.53
  116.7 1.1 fusion.30
  118.1 29.1 %all_to_all.26 = bf16[16,1,128]{2,1,0:T(2,128)(2,1)S(1)} all-to-all(bf16[16,1,128]{2,1,0:T(2,128)(2,1)S(1)} %copy.96), channel_id=1, replica_groups=mesh['y'=4,'zh'=2,'c'=2,'zl'=8,'x'=4] {'y','zh','c'}, dimensions={0} | all-to-all | bytes 8192 | tf_op jit(solution)/shard_map/all_to_all | solution.py:130
  147.9 5.6 %all-to-all-start.1 = ((bf16[32,1,128]{2,1,0:T(2,128)(2,1)}), bf16[32,1,128]{2,1,0:T(2,128)(2,1)S(1)}, u32[]{:S(2)}, u32[]{:S(2)}) async-start(bf16[32,1,128]{2,1,0:T(2,128)(2,1)} %broadcast_in_dim.89), calls=%async_computation.1 | async-start | bytes 32768 | tf_op jit(solution)/shard_map/all_to_all | solution.py:134
  153.5 11.3 %all-to-all-done.1 = bf16[32,1,128]{2,1,0:T(2,128)(2,1)S(1)} async-done(((bf16[32,1,128]{2,1,0:T(2,128)(2,1)}), bf16[32,1,128]{2,1,0:T(2,128)(2,1)S(1)}, u32[]{:S(2)}, u32[]{:S(2)}) %all-to-all-start.1) | async-done | bytes 8224 | tf_op jit(solution)/shard_map/all_to_all | solution.py:134
  166.5 3.5 %all-to-all-start.2 = ((f32[16,2,2377]{2,1,0:T(2,128)}), f32[16,2,2377]{2,1,0:T(2,128)S(1)}, u32[]{:S(2)}, u32[]{:S(2)}) async-start(f32[16,2,2377]{2,1,0:T(2,128)} %copy.100), calls=%async_computation.2 | async-start | bytes 622592 | tf_op jit(solution)/shard_map/all_to_all | solution.py:142
  171.0 18.2 %all-to-all-done.2 = f32[16,2,2377]{2,1,0:T(2,128)S(1)} async-done(((f32[16,2,2377]{2,1,0:T(2,128)}), f32[16,2,2377]{2,1,0:T(2,128)S(1)}, u32[]{:S(2)}, u32[]{:S(2)}) %all-to-all-start.2) | async-done | bytes 304288 | tf_op jit(solution)/shard_map/all_to_all | solution.py:142
  191.5 12.1 %all-to-all-start.3 = ((f32[32,2,2]{2,1,0:T(2,128)}), f32[32,2,2]{2,1,0:T(2,128)S(1)}, u32[]{:S(2)}, u32[]{:S(2)}) async-start(f32[32,2,2]{2,1,0:T(2,128)} %broadcast_in_dim.90), calls=%async_computation.4 | async-start | bytes 65536 | tf_op jit(solution)/shard_map/all_to_all | solution.py:155
  204.2 1.9 collective-permute-start
  206.1 9.0 %all-to-all-done.3 = f32[32,2,2]{2,1,0:T(2,128)S(1)} async-done(((f32[32,2,2]{2,1,0:T(2,128)}), f32[32,2,2]{2,1,0:T(2,128)S(1)}, u32[]{:S(2)}, u32[]{:S(2)}) %all-to-all-start.3) | async-done | bytes 544 | tf_op jit(solution)/shard_map/all_to_all | solution.py:155
  216.2 11.7 %collective-permute-done = bf16[512,128]{1,0:T(8,128)(2,1)S(1)} collective-permute-done((bf16[512,128]{1,0:T(8,128)(2,1)S(1)}, bf16[512,128]{1,0:T(8,128)(2,1)S(1)}, u32[]{:S(2)}, u32[]{:S(2)}) %collective-permute-start) | collective-permute-done | bytes 131104 | tf_op jit(solution)/shard_map/ppermute | solution.py:154
  (163 shorter events, 38.5 us)
Async XLA Ops:
  7.2 158.0 %copy-start = (bf16[2376,128]{1,0:T(8,128)(2,1)S(1)}, bf16[2376,128]{1,0:T(8,128)(2,1)}, u32[]{:S(2)}) copy-start(bf16[2376,128]{1,0:T(8,128)(2,1)} %param.15) | copy-start | bytes 1824772
  7.2 62.1 %all-gather.2.cloned.1.call-start = ((), (), s32[]{:S(2)}) async-start(), calls=%async_computation.5 | async-start | bytes 2359296 | tf_op jit(solution)/shard_map/all_gather | solution.py:93
  27.5 162.3 %reduce-scatter.2.cloned.1.call-start = ((), (), s32[]{:S(2)}) async-start(), calls=%async_computation.6 | async-start | bytes 2359296 | tf_op jit(solution)/shard_map/reduce_scatter | solution.py:122
  27.6 2.9 %copy-start.3 = (bf16[1,3584,2,128]{3,2,1,0:T(2,128)(2,1)S(1)}, bf16[1,3584,2,128]{3,2,1,0:T(2,128)(2,1)}, u32[]{:S(2)}) copy-start(bf16[1,3584,2,128]{3,2,1,0:T(2,128)(2,1)} %param.12) | copy-start | bytes 5505028
  30.7 2.2 copy-start.6
  69.3 2.2 copy-start.2
  74.2 0.8 copy-start.4
  102.2 3.5 %copy-start.1 = (bf16[128,4,2,2,128]{0,4,3,2,1:T(8,128)(2,1)S(1)}, bf16[128,4,2,2,128]{0,4,3,2,1:T(8,128)(2,1)}, u32[]{:S(2)}) copy-start(bf16[128,4,2,2,128]{0,4,3,2,1:T(8,128)(2,1)} %copy.94) | copy-start | bytes 1572868
  107.8 39.5 %copy-start.5 = (bf16[512,128]{1,0:T(8,128)(2,1)S(1)}, bf16[512,128]{1,0:T(8,128)(2,1)}, u32[]{:S(2)}) copy-start(bf16[512,128]{1,0:T(8,128)(2,1)} %param.9) | copy-start | bytes 393220
  107.8 45.7 %copy-start.7 = (bf16[128]{0:T(256)(128)(2,1)S(1)}, bf16[128]{0:T(256)(128)(2,1)}, u32[]{:S(2)}) copy-start(bf16[128]{0:T(256)(128)(2,1)} %param.14) | copy-start | bytes 772
  118.0 52.0 %slice-start = ((bf16[512,3,128]{2,0,1:T(8,128)(2,1)}), bf16[512,2,128]{2,0,1:T(8,128)(2,1)S(1)}, s32[]{:S(2)}) async-start(bf16[512,3,128]{2,0,1:T(8,128)(2,1)} %copy-done.4), calls=%async_computation.7 | async-start | bytes 524288 | tf_op jit(solution)/shard_map/slice | solution.py:108
  147.9 16.9 %all-to-all-start.1 = ((bf16[32,1,128]{2,1,0:T(2,128)(2,1)}), bf16[32,1,128]{2,1,0:T(2,128)(2,1)S(1)}, u32[]{:S(2)}, u32[]{:S(2)}) async-start(bf16[32,1,128]{2,1,0:T(2,128)(2,1)} %broadcast_in_dim.89), calls=%async_computation.1 | async-start | bytes 32768 | tf_op jit(solution)/shard_map/all_to_all | solution.py:134
  166.5 22.8 %all-to-all-start.2 = ((f32[16,2,2377]{2,1,0:T(2,128)}), f32[16,2,2377]{2,1,0:T(2,128)S(1)}, u32[]{:S(2)}, u32[]{:S(2)}) async-start(f32[16,2,2377]{2,1,0:T(2,128)} %copy.100), calls=%async_computation.2 | async-start | bytes 622592 | tf_op jit(solution)/shard_map/all_to_all | solution.py:142
  191.5 23.7 %all-to-all-start.3 = ((f32[32,2,2]{2,1,0:T(2,128)}), f32[32,2,2]{2,1,0:T(2,128)S(1)}, u32[]{:S(2)}, u32[]{:S(2)}) async-start(f32[32,2,2]{2,1,0:T(2,128)} %broadcast_in_dim.90), calls=%async_computation.4 | async-start | bytes 65536 | tf_op jit(solution)/shard_map/all_to_all | solution.py:155
  204.2 23.7 %collective-permute-start = (bf16[512,128]{1,0:T(8,128)(2,1)S(1)}, bf16[512,128]{1,0:T(8,128)(2,1)S(1)}, u32[]{:S(2)}, u32[]{:S(2)}) collective-permute-start(bf16[512,128]{1,0:T(8,128)(2,1)S(1)} %bitcast.160), channel_id=1, source_target_pairs={{0,64},{64,0},{1,65},{65,1},{2,66},{66,2},{3,67},{67,3},{4,68},{68... | collective-permute-start | bytes 393224 | tf_op jit(solution)/shard_map/ppermute | solution.py:154
Sparse Core Ops, SparseCore 0:
  27.7 41.6 all-gather.1
  107.9 42.5 reduce-scatter.1

commit v3 on v2

--- a/solution.py
+++ b/solution.py
@@ -51,27 +51,6 @@
     return lax.fori_loop(0, block_count, advance, initial)
 
 
-def last_token_attention(query, cache_local, live_slots, new_keys, new_values):
-    slots, head_count, head_width = cache_local.shape[0], query.shape[1], query.shape[2]
-    cache_keys = cache_local[:, 0].reshape(slots, head_count, head_width)
-    cache_values = cache_local[:, 1].reshape(slots, head_count, head_width)
-    scale = HEAD_DIM ** (-0.5)
-    cache_scores = jnp.einsum("qhd,khd->hqk", query, cache_keys, preferred_element_type=jnp.float32) * scale
-    new_scores = jnp.einsum("qhd,khd->hqk", query, new_keys, preferred_element_type=jnp.float32) * scale
-    live = (jnp.arange(slots, dtype=jnp.int32) < live_slots)[None, None, :]
-    cache_scores = jnp.where(live, cache_scores, NEG_FILL)
-    row_max = jnp.maximum(jnp.max(cache_scores, axis=2), jnp.max(new_scores, axis=2))
-    cache_weights = jnp.where(live, jnp.exp(cache_scores - row_max[:, :, None]), 0.0)
-    new_weights = jnp.exp(new_scores - row_max[:, :, None])
-    mass = jnp.sum(cache_weights, axis=2) + jnp.sum(new_weights, axis=2)
-    total = jnp.einsum(
-        "hqk,khd->hqd", cache_weights, cache_values.astype(jnp.float32), precision=lax.Precision.HIGHEST
-    ) + jnp.einsum(
-        "hqk,khd->hqd", new_weights, new_values.astype(jnp.float32), precision=lax.Precision.HIGHEST
-    )
-    return (total / mass[:, :, None]).astype(jnp.bfloat16)
-
-
 def per_device(
     layer_input,
     project_weight,
@@ -120,12 +99,7 @@
     attended = jnp.transpose(attended, (1, 0, 2)).reshape(new_rows, head_count * HEAD_DIM)
     partial_out = jnp.dot(attended, out_cols, preferred_element_type=jnp.float32).astype(jnp.bfloat16)
     branch = lax.psum_scatter(partial_out, ("y", "c"), scatter_dimension=1, tiled=True)
-    last_attended = last_token_attention(
-        queries[new_rows - 1 :], cache_local, own_len, new_keys, new_values
-    )
-    last_attended = jnp.transpose(last_attended, (1, 0, 2)).reshape(1, head_count * HEAD_DIM)
-    last_term = jnp.dot(last_attended, out_cols, preferred_element_type=jnp.float32)
-    last_term = last_term.astype(jnp.bfloat16).reshape(n_y, n_c, n_zh, block_cols)
+    last_term = partial_out[new_rows - 1].reshape(n_y, n_c, n_zh, block_cols)
     last_term = jnp.transpose(last_term, (0, 2, 1, 3)).reshape(n_gx, block_cols)
     last_terms = lax.all_to_all(last_term, GX, 0, 0, tiled=True)
     last_row = (
@@ -139,6 +113,12 @@
     gained = (last_wide * final_gain.astype(jnp.float32)).astype(jnp.bfloat16)
     logit_part = jnp.einsum("rd,vd->rv", gained, head_weight, preferred_element_type=jnp.float32)
     packed = jnp.concatenate([logit_part, square_part], axis=1)
+    packed, branch = lax.optimization_barrier((packed, branch))
+    branch = branch.reshape(new_rows, n_zh, block_cols)
+    zh = lax.axis_index("zh")
+    mine = lax.dynamic_index_in_dim(branch, zh, 1, keepdims=False)
+    theirs = lax.dynamic_index_in_dim(branch, 1 - zh, 1, keepdims=False)
+    from_partner = lax.ppermute(theirs, "zh", [(0, 1), (1, 0)])
     packed = lax.all_to_all(packed, GX, 0, 0, tiled=True)
     own_requests = packed.shape[0] // n_gx
     packed = jnp.sum(packed.reshape(n_gx, own_requests, packed.shape[1]), axis=0)
@@ -146,12 +126,6 @@
     logits = packed[:, :vocab_part] * lax.rsqrt(packed[:, vocab_part:] / D + 1e-06)
     stats = jnp.stack([jnp.sum(logits * logits, axis=1), jnp.max(logits, axis=1)], axis=0)
     spread = jnp.broadcast_to(stats[None], (n_gy,) + stats.shape)
-    spread, branch = lax.optimization_barrier((spread, branch))
-    branch = branch.reshape(new_rows, n_zh, block_cols)
-    zh = lax.axis_index("zh")
-    mine = lax.dynamic_index_in_dim(branch, zh, 1, keepdims=False)
-    theirs = lax.dynamic_index_in_dim(branch, 1 - zh, 1, keepdims=False)
-    from_partner = lax.ppermute(theirs, "zh", [(0, 1), (1, 0)])
     stats = lax.all_to_all(spread, GY, 0, 0, tiled=True)
     logit_scale = jnp.sqrt(jnp.sum(stats[:, 0], axis=0) / VOCAB)
     logit_peak = jnp.max(stats[:, 1], axis=0)

time: 236 us -> 223 us (0.945)
  waiting for transfers between devices: 86.1 us -> 61.5 us
  starting transfers between devices: 23.3 us -> 45.8 us
  matrix products: 26 us -> 22.1 us
  other arithmetic: 21.2 us -> 17.5 us
  between operations: 16.9 us -> 14.3 us
    all_to_all x1, waiting for transfers between devices: 18.2 us -> 3.64 us  [per_device(): packed = lax.all_to_all(packed, GX, 0, 0, tiled=True)]
    ppermute x1, waiting for transfers between devices: 11.7 us -> 0.01 us  [per_device(): from_partner = lax.ppermute(theirs, 'zh', [(0, 1), (1, 0)])]
    ppermute x1, starting transfers between devices: 1.92 us -> 12.5 us  [per_device(): from_partner = lax.ppermute(theirs, 'zh', [(0, 1), (1, 0)])]
    all_to_all x1, starting transfers between devices: 12.1 us -> 20.6 us  [per_device(): stats = lax.all_to_all(spread, GY, 0, 0, tiled=True)]
    dot_general x5 -> x0, matrix products: 3.89 us -> none  [the longest x1 1.08 us: last_token_attention(): jnp.einsum('hqk,khd->hqd', new_weights, new_values.astype(jnp.float32), p...]
    all_to_all x1, starting transfers between devices: 3.54 us -> 6.95 us  [per_device(): packed = lax.all_to_all(packed, GX, 0, 0, tiled=True)]
  transfers between devices with their start and end apart: 6 -> 6, of which waited for: 5 -> 4; matrix products, arithmetic and copies ran while one was open for 8% -> 5% of each run, Pallas kernels for 0% -> 0%
where the time goes in v3:
time: 223 us
  waiting for transfers between devices  61.5 us (28%)
  blocking collectives  49.3 us (22%)
  starting transfers between devices  45.8 us (21%)
  matrix products  22.1 us (10%)
  other arithmetic  17.5 us (8%)
  between operations  14.3 us (6%)
  local copies, waits for them, and re-layouts  11.4 us (5%)
    all_gather x1, waiting for transfers between devices, per_device(): features = lax.all_gather(pair, ('y', 'c'), axis=1, tiled=True)  35.8 us
    all_to_all x1, blocking collectives, per_device(): last_terms = lax.all_to_all(last_term, GX, 0, 0, tiled=True)  29 us
    all_to_all x1, starting transfers between devices, per_device(): stats = lax.all_to_all(spread, GY, 0, 0, tiled=True)  20.6 us
    all_gather x1, blocking collectives, per_device(): pair = lax.all_gather(layer_input, 'zh', axis=1, tiled=True)  20.3 us
    ppermute x1, starting transfers between devices, per_device(): from_partner = lax.ppermute(theirs, 'zh', [(0, 1), (1, 0)])  12.5 us
    dot_general x15, matrix products, fold_scores(): jnp.einsum('hqk,khd->hqd', weights, value_block.astype(jnp.float32), prec...  12.3 us
    all_to_all x1, waiting for transfers between devices, per_device(): lax.all_to_all(jnp.broadcast_to(last_row[None], (n_gy, block_cols)), GY,...  11.3 us
    all_to_all x1, waiting for transfers between devices, per_device(): stats = lax.all_to_all(spread, GY, 0, 0, tiled=True)  10.8 us
  transfers between devices with their start and end apart: 6, of which 4 were waited for; matrix products, arithmetic and copies ran while one was open for 5% of the time, Pallas kernels for 0%

profile of v3, /device:TPU:2, one launch (start us, length us, event | category | flops | bytes accessed | tf_op | source)
XLA Modules:
  0.0 222.7 jit_solution(16598998124366209928)
XLA Ops:
  7.2 20.3 %all_gather.6 = bf16[512,256]{1,0:T(8,128)(2,1)} all-gather(bf16[512,128]{1,0:T(8,128)(2,1)} %param.9), channel_id=1, replica_groups=mesh['y'=4,'zh'=2,'c'=2,'zl'=8,'x'=4] {'zh'}, dimensions={1}, use_global_device_ids=true | all-gather | bytes 393216 | tf_op jit(solution)/shard_map/all_gather | solution.py:71
  27.6 2.9 %copy.63 = bf16[4,2,2,128,3,128]{5,3,2,1,0,4:T(8,128)(2,1)} copy(bf16[4,2,2,128,3,128]{5,3,1,2,0,4:T(8,128)(2,1)} %bitcast.115) | data formatting | bytes 3145728 | tf_op jit(solution)/shard_map/transpose | solution.py:74
  30.7 1.3 copy.64
  32.1 0.9 copy.65
  33.5 35.8 %all-gather.2.cloned.1.call-done = bf16[512,2048]{1,0:T(8,128)(2,1)} async-done(((bf16[512,256]{1,0:T(8,128)(2,1)}), bf16[512,2048]{1,0:T(8,128)(2,1)}) %all-gather.2.cloned.1.call-update) | async-done | bytes 2097168 | tf_op jit(solution)/shard_map/all_gather | solution.py:72
  69.3 2.2 fusion.13
  71.5 2.7 %fusion.20 = bf16[512,3,128]{2,0,1:T(8,128)(2,1)S(1)} fusion(bf16[2048,3,128]{2,0,1:T(8,128)(2,1)} %bitcast.116, bf16[512,2048]{1,0:T(8,128)(2,1)S(1)} %copy-done.1, f32[512]{0:T(512)S(1)} %add_rsqrt_fusion), kind=kOutput, calls=%fused_computation.34 | convolution fusion | flops 808648704 | bytes 4065280 | tf_op jit(solution)/shard_map/td,dcf->tcf/dot_general | solution.py:80
  74.3 0.7 copy-done.4
  75.0 1.3 fusion.44
  76.3 25.9 %while.18 = (s32[]{:T(128)}, f32[1,512]{1,0:T(1,128)S(1)}, f32[1,512]{1,0:T(1,128)S(1)}, f32[1,512,128]{2,1,0:T(8,128)S(1)}, s32[]{:T(128)}, /*index=5*/bf16[358...) while((s32[]{:T(128)}, f32[1,512]{1,0:T(1,128)S(1)}, ...), condition=%wide.region_4.5_spmd.clone, body=%wide.region_1.4_spmd.clone.sunk | while | flops 236129280 | bytes 2393807 | solution.py:51
  102.2 1.4 fusion.27
  103.6 2.0 fusion.26
  105.7 2.1 convolution_convert_fusion
  107.8 0.8 slice_reduce_fusion.2
  108.7 29.0 %all_to_all.29 = bf16[16,1,128]{2,1,0:T(2,128)(2,1)S(1)} all-to-all(bf16[16,1,128]{2,1,0:T(2,128)(2,1)S(1)} %copy.67), channel_id=1, replica_groups=mesh['y'=4,'zh'=2,'c'=2,'zl'=8,'x'=4] {'y','zh','c'}, dimensions={0} | all-to-all | bytes 8192 | tf_op jit(solution)/shard_map/all_to_all | solution.py:104
  138.3 5.6 %all-to-all-start.1 = ((bf16[32,1,128]{2,1,0:T(2,128)(2,1)}), bf16[32,1,128]{2,1,0:T(2,128)(2,1)S(1)}, u32[]{:S(2)}, u32[]{:S(2)}) async-start(bf16[32,1,128]{2,1,0:T(2,128)(2,1)} %broadcast_in_dim.83), calls=%async_computation.1 | async-start | bytes 32768 | tf_op jit(solution)/shard_map/all_to_all | solution.py:108
  144.0 11.3 %all-to-all-done.1 = bf16[32,1,128]{2,1,0:T(2,128)(2,1)S(1)} async-done(((bf16[32,1,128]{2,1,0:T(2,128)(2,1)}), bf16[32,1,128]{2,1,0:T(2,128)(2,1)S(1)}, u32[]{:S(2)}, u32[]{:S(2)}) %all-to-all-start.1) | async-done | bytes 8224 | tf_op jit(solution)/shard_map/all_to_all | solution.py:108
  155.8 0.9 all_to_all.22
  156.7 7.0 %all-to-all-start.2 = ((f32[16,2,2377]{2,1,0:T(2,128)}), f32[16,2,2377]{2,1,0:T(2,128)S(1)}, u32[]{:S(2)}, u32[]{:S(2)}) async-start(f32[16,2,2377]{2,1,0:T(2,128)} %all_to_all.22), calls=%async_computation.3 | async-start | bytes 622592 | tf_op jit(solution)/shard_map/all_to_all | solution.py:122
  163.7 1.0 copy.73
  165.3 12.5 %collective-permute-start = (bf16[512,128]{1,0:T(8,128)(2,1)S(1)}, bf16[512,128]{1,0:T(8,128)(2,1)S(1)}, u32[]{:S(2)}, u32[]{:S(2)}) collective-permute-start(bf16[512,128]{1,0:T(8,128)(2,1)S(1)} %bitcast.124), channel_id=1, source_target_pairs={{0,64},{64,0},{1,65},{65,1},{2,66},{66,2},{3,67},{67,3},{4,68},{68... | collective-permute-start | bytes 393224 | tf_op jit(solution)/shard_map/ppermute | solution.py:121
  177.9 3.6 %all-to-all-done.2 = f32[16,2,2377]{2,1,0:T(2,128)S(1)} async-done(((f32[16,2,2377]{2,1,0:T(2,128)}), f32[16,2,2377]{2,1,0:T(2,128)S(1)}, u32[]{:S(2)}, u32[]{:S(2)}) %all-to-all-start.2) | async-done | bytes 304288 | tf_op jit(solution)/shard_map/all_to_all | solution.py:122
  182.7 20.6 %all-to-all-start.3 = ((f32[32,2,2]{2,1,0:T(2,128)}), f32[32,2,2]{2,1,0:T(2,128)S(1)}, u32[]{:S(2)}, u32[]{:S(2)}) async-start(f32[32,2,2]{2,1,0:T(2,128)} %broadcast_in_dim.85), calls=%async_computation.4 | async-start | bytes 65536 | tf_op jit(solution)/shard_map/all_to_all | solution.py:129
  204.0 10.8 %all-to-all-done.3 = f32[32,2,2]{2,1,0:T(2,128)S(1)} async-done(((f32[32,2,2]{2,1,0:T(2,128)}), f32[32,2,2]{2,1,0:T(2,128)S(1)}, u32[]{:S(2)}, u32[]{:S(2)}) %all-to-all-start.3) | async-done | bytes 544 | tf_op jit(solution)/shard_map/all_to_all | solution.py:129
  (154 shorter events, 30.9 us)
Async XLA Ops:
  7.2 148.3 %copy-start = (bf16[2376,128]{1,0:T(8,128)(2,1)S(1)}, bf16[2376,128]{1,0:T(8,128)(2,1)}, u32[]{:S(2)}) copy-start(bf16[2376,128]{1,0:T(8,128)(2,1)} %param.15) | copy-start | bytes 1824772
  7.2 62.1 %all-gather.2.cloned.1.call-start = ((), (), s32[]{:S(2)}) async-start(), calls=%async_computation.5 | async-start | bytes 2359296 | tf_op jit(solution)/shard_map/all_gather | solution.py:72
  27.5 128.3 %reduce-scatter.2.cloned.1.call-start = ((), (), s32[]{:S(2)}) async-start(), calls=%async_computation.6 | async-start | bytes 2359296 | tf_op jit(solution)/shard_map/reduce_scatter | solution.py:101
  27.6 2.9 %copy-start.3 = (bf16[1,3584,2,128]{3,2,1,0:T(2,128)(2,1)S(1)}, bf16[1,3584,2,128]{3,2,1,0:T(2,128)(2,1)}, u32[]{:S(2)}) copy-start(bf16[1,3584,2,128]{3,2,1,0:T(2,128)(2,1)} %param.12) | copy-start | bytes 5505028
  30.5 2.4 %copy-start.7 = (s32[32]{0:T(128)S(1)}, s32[32]{0:T(128)}, u32[]{:S(2)}) copy-start(s32[32]{0:T(128)} %param.13) | copy-start | bytes 388
  69.3 2.2 %copy-start.1 = (bf16[512,2048]{1,0:T(8,128)(2,1)S(1)}, bf16[512,2048]{1,0:T(8,128)(2,1)}, u32[]{:S(2)}) copy-start(bf16[512,2048]{1,0:T(8,128)(2,1)} %all-gather.2.cloned.1.call-done) | copy-start | bytes 6291460
  74.2 0.8 copy-start.4
  102.2 3.5 %copy-start.2 = (bf16[128,4,2,2,128]{0,4,3,2,1:T(8,128)(2,1)S(1)}, bf16[128,4,2,2,128]{0,4,3,2,1:T(8,128)(2,1)}, u32[]{:S(2)}) copy-start(bf16[128,4,2,2,128]{0,4,3,2,1:T(8,128)(2,1)} %copy.65) | copy-start | bytes 1572868
  105.7 32.1 %copy-start.5 = (bf16[512,128]{1,0:T(8,128)(2,1)S(1)}, bf16[512,128]{1,0:T(8,128)(2,1)}, u32[]{:S(2)}) copy-start(bf16[512,128]{1,0:T(8,128)(2,1)} %param.9) | copy-start | bytes 393220
  105.7 38.3 %copy-start.8 = (bf16[128]{0:T(256)(128)(2,1)S(1)}, bf16[128]{0:T(256)(128)(2,1)}, u32[]{:S(2)}) copy-start(bf16[128]{0:T(256)(128)(2,1)} %param.14) | copy-start | bytes 772
  107.8 55.9 %slice-start = ((bf16[512,3,128]{2,0,1:T(8,128)(2,1)}), bf16[512,2,128]{2,0,1:T(8,128)(2,1)S(1)}, s32[]{:S(2)}) async-start(bf16[512,3,128]{2,0,1:T(8,128)(2,1)} %copy-done.4), calls=%async_computation.7 | async-start | bytes 524288 | tf_op jit(solution)/shard_map/slice | solution.py:87
  138.3 16.9 %all-to-all-start.1 = ((bf16[32,1,128]{2,1,0:T(2,128)(2,1)}), bf16[32,1,128]{2,1,0:T(2,128)(2,1)S(1)}, u32[]{:S(2)}, u32[]{:S(2)}) async-start(bf16[32,1,128]{2,1,0:T(2,128)(2,1)} %broadcast_in_dim.83), calls=%async_computation.1 | async-start | bytes 32768 | tf_op jit(solution)/shard_map/all_to_all | solution.py:108
  155.8 8.8 %copy-start.6 = (bf16[512,256]{1,0:T(8,128)(2,1)S(1)}, bf16[512,256]{1,0:T(8,128)(2,1)}, u32[]{:S(2)}) copy-start(bf16[512,256]{1,0:T(8,128)(2,1)} %reduce-scatter.2.cloned.1.call-done) | copy-start | bytes 786436
  156.7 24.8 %all-to-all-start.2 = ((f32[16,2,2377]{2,1,0:T(2,128)}), f32[16,2,2377]{2,1,0:T(2,128)S(1)}, u32[]{:S(2)}, u32[]{:S(2)}) async-start(f32[16,2,2377]{2,1,0:T(2,128)} %all_to_all.22), calls=%async_computation.3 | async-start | bytes 622592 | tf_op jit(solution)/shard_map/all_to_all | solution.py:122
  165.3 37.9 %collective-permute-start = (bf16[512,128]{1,0:T(8,128)(2,1)S(1)}, bf16[512,128]{1,0:T(8,128)(2,1)S(1)}, u32[]{:S(2)}, u32[]{:S(2)}) collective-permute-start(bf16[512,128]{1,0:T(8,128)(2,1)S(1)} %bitcast.124), channel_id=1, source_target_pairs={{0,64},{64,0},{1,65},{65,1},{2,66},{66,2},{3,67},{67,3},{4,68},{68... | collective-permute-start | bytes 393224 | tf_op jit(solution)/shard_map/ppermute | solution.py:121
  182.7 32.1 %all-to-all-start.3 = ((f32[32,2,2]{2,1,0:T(2,128)}), f32[32,2,2]{2,1,0:T(2,128)S(1)}, u32[]{:S(2)}, u32[]{:S(2)}) async-start(f32[32,2,2]{2,1,0:T(2,128)} %broadcast_in_dim.85), calls=%async_computation.4 | async-start | bytes 65536 | tf_op jit(solution)/shard_map/all_to_all | solution.py:129
Sparse Core Ops, SparseCore 0:
  27.7 41.6 all-gather.1
  107.9 42.4 reduce-scatter.1

commit v4 on v3

--- a/solution.py
+++ b/solution.py
@@ -25,8 +25,11 @@
     weights = jnp.where(allowed, jnp.exp(scores - new_max[:, :, None]), 0.0)
     factor = jnp.exp(running_max - new_max)
     mass_sum = mass_sum * factor + jnp.sum(weights, axis=2)
-    weighted = weighted * factor[:, :, None] + jnp.einsum(
-        "hqk,khd->hqd", weights, value_block.astype(jnp.float32), precision=lax.Precision.HIGHEST
+    high = weights.astype(jnp.bfloat16)
+    low = (weights - high.astype(jnp.float32)).astype(jnp.bfloat16)
+    weighted = weighted * factor[:, :, None] + (
+        jnp.einsum("hqk,khd->hqd", high, value_block, preferred_element_type=jnp.float32)
+        + jnp.einsum("hqk,khd->hqd", low, value_block, preferred_element_type=jnp.float32)
     )
     return (new_max, mass_sum, weighted)
 
@@ -91,7 +94,7 @@
     out_cols = jnp.transpose(out_cols, (0, 1, 3, 2, 4)).reshape(output_weight.shape)
 
     cache_slots = cache_local.shape[0]
-    block_rows = min(256, cache_slots // 2)
+    block_rows = min(512, cache_slots // 2)
     carried = cache_pass(queries, cache_local, own_len, block_rows)
     causal = (jnp.arange(new_rows)[None, :] <= jnp.arange(new_rows)[:, None])[None]
     carried = fold_scores(carried, queries, new_keys, new_values, causal)

time: 223 us -> 227 us (1.018)
  matrix products: 22.1 us -> 33 us
  other arithmetic: 17.5 us -> 11.2 us
    dot_general x15, matrix products: 12.3 us -> 20.2 us  [the longest x7 10.2 us: fold_scores(): jnp.einsum('hqk,khd->hqd', low, value_block, preferred_element_type=jnp.f...]
    lt x14 -> x7, other arithmetic: 9.14 us -> 4.57 us  [advance(): allowed = (places < live_slots)[None, None, :]]
    dot_general x15 -> x8, matrix products: 4.78 us -> 8.91 us  [fold_scores(): jnp.einsum('qhd,khd->hqk', queries, key_block, preferred_element_type=jnp...]
where the time goes in v4:
time: 227 us
  waiting for transfers between devices  61.4 us (27%)
  blocking collectives  49.3 us (22%)
  starting transfers between devices  45.7 us (20%)
  matrix products  33 us (15%)
  between operations  14.3 us (6%)
  local copies, waits for them, and re-layouts  11.2 us (5%)
  other arithmetic  11.2 us (5%)
    all_gather x1, waiting for transfers between devices, per_device(): features = lax.all_gather(pair, ('y', 'c'), axis=1, tiled=True)  35.7 us
    all_to_all x1, blocking collectives, per_device(): last_terms = lax.all_to_all(last_term, GX, 0, 0, tiled=True)  29 us
    all_to_all x1, starting transfers between devices, per_device(): stats = lax.all_to_all(spread, GY, 0, 0, tiled=True)  20.6 us
    all_gather x1, blocking collectives, per_device(): pair = lax.all_gather(layer_input, 'zh', axis=1, tiled=True)  20.3 us
    ppermute x1, starting transfers between devices, per_device(): from_partner = lax.ppermute(theirs, 'zh', [(0, 1), (1, 0)])  12.5 us
    all_to_all x1, waiting for transfers between devices, per_device(): lax.all_to_all(jnp.broadcast_to(last_row[None], (n_gy, block_cols)), GY,...  11.3 us
    all_to_all x1, waiting for transfers between devices, per_device(): stats = lax.all_to_all(spread, GY, 0, 0, tiled=True)  10.8 us
    dot_general x7, matrix products, fold_scores(): jnp.einsum('hqk,khd->hqd', low, value_block, preferred_element_type=jnp.f...  10.2 us
  transfers between devices with their start and end apart: 6, of which 4 were waited for; matrix products, arithmetic and copies ran while one was open for 5% of the time, Pallas kernels for 0%

profile of v4, /device:TPU:2, one launch (start us, length us, event | category | flops | bytes accessed | tf_op | source)
XLA Modules:
  0.0 226.5 jit_solution(13220793343712434298)
XLA Ops:
  7.2 20.3 %all_gather.6 = bf16[512,256]{1,0:T(8,128)(2,1)} all-gather(bf16[512,128]{1,0:T(8,128)(2,1)} %param.9), channel_id=1, replica_groups=mesh['y'=4,'zh'=2,'c'=2,'zl'=8,'x'=4] {'zh'}, dimensions={1}, use_global_device_ids=true | all-gather | bytes 393216 | tf_op jit(solution)/shard_map/all_gather | solution.py:74
  27.6 2.7 %copy.63 = bf16[4,2,2,128,3,128]{5,3,2,1,0,4:T(8,128)(2,1)} copy(bf16[4,2,2,128,3,128]{5,3,1,2,0,4:T(8,128)(2,1)} %bitcast.139) | data formatting | bytes 3145728 | tf_op jit(solution)/shard_map/transpose | solution.py:77
  30.4 1.5 copy.83
  33.6 35.7 %all-gather.2.cloned.1.call-done = bf16[512,2048]{1,0:T(8,128)(2,1)} async-done(((bf16[512,256]{1,0:T(8,128)(2,1)}), bf16[512,2048]{1,0:T(8,128)(2,1)}) %all-gather.2.cloned.1.call-update) | async-done | bytes 2097168 | tf_op jit(solution)/shard_map/all_gather | solution.py:75
  69.3 2.2 fusion.22
  73.2 35.2 %while.18 = (s32[]{:T(128)}, f32[1,512]{1,0:T(1,128)S(1)}, f32[1,512]{1,0:T(1,128)S(1)}, f32[1,512,128]{2,1,0:T(8,128)S(1)}, s32[]{:T(128)}, /*index=5*/bf16[358...) while((s32[]{:T(128)}, f32[1,512]{1,0:T(1,128)S(1)}, ...), condition=%wide.region_4.5_spmd.clone, body=%wide.region_1.4_spmd.clone.sunk | while | flops 205524480 | bytes 5804759 | solution.py:54
  75.1 1.4 fusion.82
  76.7 1.5 fusion.83
  80.2 1.4 fusion.82
  81.8 1.5 fusion.83
  86.8 1.5 fusion.83
  91.8 1.5 fusion.83
  96.9 1.5 fusion.83
  101.9 1.5 fusion.83
  106.9 1.5 fusion.83
  109.4 2.2 convolution_convert_fusion
  112.6 29.0 %all_to_all.29 = bf16[16,1,128]{2,1,0:T(2,128)(2,1)S(1)} all-to-all(bf16[16,1,128]{2,1,0:T(2,128)(2,1)S(1)} %copy.67), channel_id=1, replica_groups=mesh['y'=4,'zh'=2,'c'=2,'zl'=8,'x'=4] {'y','zh','c'}, dimensions={0} | all-to-all | bytes 8192 | tf_op jit(solution)/shard_map/all_to_all | solution.py:107
  142.3 5.6 %all-to-all-start.1 = ((bf16[32,1,128]{2,1,0:T(2,128)(2,1)}), bf16[32,1,128]{2,1,0:T(2,128)(2,1)S(1)}, u32[]{:S(2)}, u32[]{:S(2)}) async-start(bf16[32,1,128]{2,1,0:T(2,128)(2,1)} %broadcast_in_dim.83), calls=%async_computation.1 | async-start | bytes 32768 | tf_op jit(solution)/shard_map/all_to_all | solution.py:111
  147.9 11.3 %all-to-all-done.1 = bf16[32,1,128]{2,1,0:T(2,128)(2,1)S(1)} async-done(((bf16[32,1,128]{2,1,0:T(2,128)(2,1)}), bf16[32,1,128]{2,1,0:T(2,128)(2,1)S(1)}, u32[]{:S(2)}, u32[]{:S(2)}) %all-to-all-start.1) | async-done | bytes 8224 | tf_op jit(solution)/shard_map/all_to_all | solution.py:111
  160.7 6.9 %all-to-all-start.2 = ((f32[16,2,2377]{2,1,0:T(2,128)}), f32[16,2,2377]{2,1,0:T(2,128)S(1)}, u32[]{:S(2)}, u32[]{:S(2)}) async-start(f32[16,2,2377]{2,1,0:T(2,128)} %all_to_all.22), calls=%async_computation.3 | async-start | bytes 622592 | tf_op jit(solution)/shard_map/all_to_all | solution.py:125
  169.3 12.5 %collective-permute-start = (bf16[512,128]{1,0:T(8,128)(2,1)S(1)}, bf16[512,128]{1,0:T(8,128)(2,1)S(1)}, u32[]{:S(2)}, u32[]{:S(2)}) collective-permute-start(bf16[512,128]{1,0:T(8,128)(2,1)S(1)} %bitcast.146), channel_id=1, source_target_pairs={{0,64},{64,0},{1,65},{65,1},{2,66},{66,2},{3,67},{67,3},{4,68},{68... | collective-permute-start | bytes 393224 | tf_op jit(solution)/shard_map/ppermute | solution.py:124
  181.8 3.6 %all-to-all-done.2 = f32[16,2,2377]{2,1,0:T(2,128)S(1)} async-done(((f32[16,2,2377]{2,1,0:T(2,128)}), f32[16,2,2377]{2,1,0:T(2,128)S(1)}, u32[]{:S(2)}, u32[]{:S(2)}) %all-to-all-start.2) | async-done | bytes 304288 | tf_op jit(solution)/shard_map/all_to_all | solution.py:125
  186.6 20.6 %all-to-all-start.3 = ((f32[32,2,2]{2,1,0:T(2,128)}), f32[32,2,2]{2,1,0:T(2,128)S(1)}, u32[]{:S(2)}, u32[]{:S(2)}) async-start(f32[32,2,2]{2,1,0:T(2,128)} %broadcast_in_dim.85), calls=%async_computation.4 | async-start | bytes 65536 | tf_op jit(solution)/shard_map/all_to_all | solution.py:132
  207.8 10.8 %all-to-all-done.3 = f32[32,2,2]{2,1,0:T(2,128)S(1)} async-done(((f32[32,2,2]{2,1,0:T(2,128)}), f32[32,2,2]{2,1,0:T(2,128)S(1)}, u32[]{:S(2)}, u32[]{:S(2)}) %all-to-all-start.3) | async-done | bytes 544 | tf_op jit(solution)/shard_map/all_to_all | solution.py:132
  (113 shorter events, 33.9 us)
Async XLA Ops:
  7.2 152.2 %copy-start = (bf16[2376,128]{1,0:T(8,128)(2,1)S(1)}, bf16[2376,128]{1,0:T(8,128)(2,1)}, u32[]{:S(2)}) copy-start(bf16[2376,128]{1,0:T(8,128)(2,1)} %param.15) | copy-start | bytes 1824772
  7.2 23.2 %copy-start.3 = (bf16[1,3584,2,128]{3,2,1,0:T(2,128)(2,1)S(1)}, bf16[1,3584,2,128]{3,2,1,0:T(2,128)(2,1)}, u32[]{:S(2)}) copy-start(bf16[1,3584,2,128]{3,2,1,0:T(2,128)(2,1)} %param.12) | copy-start | bytes 5505028
  7.2 62.1 %all-gather.2.cloned.1.call-start = ((), (), s32[]{:S(2)}) async-start(), calls=%async_computation.5 | async-start | bytes 2359296 | tf_op jit(solution)/shard_map/all_gather | solution.py:75
  27.5 132.2 %reduce-scatter.2.cloned.1.call-start = ((), (), s32[]{:S(2)}) async-start(), calls=%async_computation.6 | async-start | bytes 2359296 | tf_op jit(solution)/shard_map/reduce_scatter | solution.py:104
  30.4 1.5 copy-start.6
  30.4 2.6 %copy-start.8 = (s32[32]{0:T(128)S(1)}, s32[32]{0:T(128)}, u32[]{:S(2)}) copy-start(s32[32]{0:T(128)} %param.13) | copy-start | bytes 388
  31.9 39.7 %copy-start.4 = (bf16[4,2,2,128,3,128]{5,3,2,1,0,4:T(8,128)(2,1)S(1)}, bf16[4,2,2,128,3,128]{5,3,2,1,0,4:T(8,128)(2,1)}, u32[]{:S(2)}) copy-start(bf16[4,2,2,128,3,128]{5,3,2,1,0,4:T(8,128)(2,1)} %copy.63) | copy-start | bytes 4718596
  69.3 2.2 copy-start.2
  108.4 1.0 copy-start.1
  111.7 30.0 %copy-start.5 = (bf16[512,128]{1,0:T(8,128)(2,1)S(1)}, bf16[512,128]{1,0:T(8,128)(2,1)}, u32[]{:S(2)}) copy-start(bf16[512,128]{1,0:T(8,128)(2,1)} %param.9) | copy-start | bytes 393220
  111.7 36.2 %copy-start.9 = (bf16[128]{0:T(256)(128)(2,1)S(1)}, bf16[128]{0:T(256)(128)(2,1)}, u32[]{:S(2)}) copy-start(bf16[128]{0:T(256)(128)(2,1)} %param.14) | copy-start | bytes 772
  142.3 16.9 %all-to-all-start.1 = ((bf16[32,1,128]{2,1,0:T(2,128)(2,1)}), bf16[32,1,128]{2,1,0:T(2,128)(2,1)S(1)}, u32[]{:S(2)}, u32[]{:S(2)}) async-start(bf16[32,1,128]{2,1,0:T(2,128)(2,1)} %broadcast_in_dim.83), calls=%async_computation.1 | async-start | bytes 32768 | tf_op jit(solution)/shard_map/all_to_all | solution.py:111
  159.8 8.8 %copy-start.7 = (bf16[512,256]{1,0:T(8,128)(2,1)S(1)}, bf16[512,256]{1,0:T(8,128)(2,1)}, u32[]{:S(2)}) copy-start(bf16[512,256]{1,0:T(8,128)(2,1)} %reduce-scatter.2.cloned.1.call-done) | copy-start | bytes 786436
  160.7 24.8 %all-to-all-start.2 = ((f32[16,2,2377]{2,1,0:T(2,128)}), f32[16,2,2377]{2,1,0:T(2,128)S(1)}, u32[]{:S(2)}, u32[]{:S(2)}) async-start(f32[16,2,2377]{2,1,0:T(2,128)} %all_to_all.22), calls=%async_computation.3 | async-start | bytes 622592 | tf_op jit(solution)/shard_map/all_to_all | solution.py:125
  169.3 37.9 %collective-permute-start = (bf16[512,128]{1,0:T(8,128)(2,1)S(1)}, bf16[512,128]{1,0:T(8,128)(2,1)S(1)}, u32[]{:S(2)}, u32[]{:S(2)}) collective-permute-start(bf16[512,128]{1,0:T(8,128)(2,1)S(1)} %bitcast.146), channel_id=1, source_target_pairs={{0,64},{64,0},{1,65},{65,1},{2,66},{66,2},{3,67},{67,3},{4,68},{68... | collective-permute-start | bytes 393224 | tf_op jit(solution)/shard_map/ppermute | solution.py:124
  186.6 32.0 %all-to-all-start.3 = ((f32[32,2,2]{2,1,0:T(2,128)}), f32[32,2,2]{2,1,0:T(2,128)S(1)}, u32[]{:S(2)}, u32[]{:S(2)}) async-start(f32[32,2,2]{2,1,0:T(2,128)} %broadcast_in_dim.85), calls=%async_computation.4 | async-start | bytes 65536 | tf_op jit(solution)/shard_map/all_to_all | solution.py:132
Sparse Core Ops, SparseCore 0:
  27.7 41.6 all-gather.1
  111.8 42.5 reduce-scatter.1

commit v5 on v3

--- a/solution.py
+++ b/solution.py
@@ -1,7 +1,11 @@
+import functools
+
 import jax
 import jax.numpy as jnp
 import numpy as np
 from jax import lax
+from jax.experimental import pallas as pl
+from jax.experimental.pallas import tpu as pltpu
 from jax.sharding import Mesh
 from jax.sharding import PartitionSpec as P
 
@@ -15,40 +19,64 @@
 GY = ("zl", "x")
 
 
-def fold_scores(carried, queries, key_block, value_block, allowed):
-    running_max, mass_sum, weighted = carried
-    scores = jnp.einsum(
-        "qhd,khd->hqk", queries, key_block, preferred_element_type=jnp.float32
-    ) * HEAD_DIM ** (-0.5)
-    scores = jnp.where(allowed, scores, NEG_FILL)
-    new_max = jnp.maximum(running_max, jnp.max(scores, axis=2))
-    weights = jnp.where(allowed, jnp.exp(scores - new_max[:, :, None]), 0.0)
-    factor = jnp.exp(running_max - new_max)
-    mass_sum = mass_sum * factor + jnp.sum(weights, axis=2)
-    weighted = weighted * factor[:, :, None] + jnp.einsum(
-        "hqk,khd->hqd", weights, value_block.astype(jnp.float32), precision=lax.Precision.HIGHEST
-    )
-    return (new_max, mass_sum, weighted)
+def attention_kernel(cache_slots, key_rows, len_ref, q_ref, k_ref, v_ref, o_ref, m_sc, l_sc, acc_sc):
+    step = pl.program_id(0)
+
+    @pl.when(step == 0)
+    def _():
+        m_sc[...] = jnp.full(m_sc.shape, NEG_FILL, jnp.float32)
+        l_sc[...] = jnp.zeros(l_sc.shape, jnp.float32)
+        acc_sc[...] = jnp.zeros(acc_sc.shape, jnp.float32)
+
+    q = q_ref[...]
+    k = k_ref[...]
+    s = lax.dot_general(q, k, (((1,), (1,)), ((), ())), preferred_element_type=jnp.float32) * HEAD_DIM ** (-0.5)
+    rows = q.shape[0]
+    slot = step * key_rows + lax.broadcasted_iota(jnp.int32, (rows, key_rows), 1)
+    place = lax.broadcasted_iota(jnp.int32, (rows, key_rows), 0)
+    limit = jnp.where(slot < cache_slots, len_ref[0], cache_slots + place + 1)
+    allowed = slot < limit
+    s = jnp.where(allowed, s, NEG_FILL)
+    m_old = m_sc[...]
+    m_new = jnp.maximum(m_old, jnp.max(s, axis=1, keepdims=True))
+    p = jnp.where(allowed, jnp.exp(s - m_new), 0.0)
+    factor = jnp.exp(m_old - m_new)
+    l_sc[...] = l_sc[...] * factor + jnp.sum(p, axis=1, keepdims=True)
+    v = v_ref[...]
+    high = p.astype(jnp.bfloat16)
+    low = (p - high.astype(jnp.float32)).astype(jnp.bfloat16)
+    pv = jnp.dot(high, v, preferred_element_type=jnp.float32) + jnp.dot(low, v, preferred_element_type=jnp.float32)
+    acc_sc[...] = acc_sc[...] * factor + pv
+    m_sc[...] = m_new
+
+    @pl.when(step == pl.num_programs(0) - 1)
+    def _():
+        o_ref[...] = (acc_sc[...] / l_sc[...]).astype(o_ref.dtype)
 
 
-def cache_pass(queries, cache_part, live_slots, block_rows):
-    query_rows, head_count, head_width = queries.shape
-    block_count = cache_part.shape[0] // block_rows
-    initial = (
-        jnp.full((head_count, query_rows), NEG_FILL, jnp.float32),
-        jnp.zeros((head_count, query_rows), jnp.float32),
-        jnp.zeros((head_count, query_rows, head_width), jnp.float32),
-    )
-
-    def advance(block_index, carried):
-        cache_piece = lax.dynamic_slice_in_dim(cache_part, block_index * block_rows, block_rows, 0)
-        key_block = cache_piece[:, 0].reshape(block_rows, head_count, head_width)
-        value_block = cache_piece[:, 1].reshape(block_rows, head_count, head_width)
-        places = block_index * block_rows + jnp.arange(block_rows, dtype=jnp.int32)
-        allowed = (places < live_slots)[None, None, :]
-        return fold_scores(carried, queries, key_block, value_block, allowed)
-
-    return lax.fori_loop(0, block_count, advance, initial)
+def attend(queries, keys, values, live_slots, cache_slots, key_rows=512):
+    rows, width = queries.shape
+    steps = keys.shape[0] // key_rows
+    return pl.pallas_call(
+        functools.partial(attention_kernel, cache_slots, key_rows),
+        grid_spec=pltpu.PrefetchScalarGridSpec(
+            num_scalar_prefetch=1,
+            grid=(steps,),
+            in_specs=[
+                pl.BlockSpec((rows, width), lambda i, n: (0, 0)),
+                pl.BlockSpec((key_rows, width), lambda i, n: (i, 0)),
+                pl.BlockSpec((key_rows, width), lambda i, n: (i, 0)),
+            ],
+            out_specs=pl.BlockSpec((rows, width), lambda i, n: (0, 0)),
+            scratch_shapes=[
+                pltpu.VMEM((rows, 1), jnp.float32),
+                pltpu.VMEM((rows, 1), jnp.float32),
+                pltpu.VMEM((rows, width), jnp.float32),
+            ],
+        ),
+        out_shape=jax.ShapeDtypeStruct((rows, width), jnp.bfloat16),
+        compiler_params=pltpu.CompilerParams(dimension_semantics=("arbitrary",)),
+    )(live_slots, queries, keys, values)
 
 
 def per_device(
@@ -91,12 +119,14 @@
     out_cols = jnp.transpose(out_cols, (0, 1, 3, 2, 4)).reshape(output_weight.shape)
 
     cache_slots = cache_local.shape[0]
-    block_rows = min(256, cache_slots // 2)
-    carried = cache_pass(queries, cache_local, own_len, block_rows)
-    causal = (jnp.arange(new_rows)[None, :] <= jnp.arange(new_rows)[:, None])[None]
-    carried = fold_scores(carried, queries, new_keys, new_values, causal)
-    attended = (carried[2] / carried[1][:, :, None]).astype(jnp.bfloat16)
-    attended = jnp.transpose(attended, (1, 0, 2)).reshape(new_rows, head_count * HEAD_DIM)
+    live = jnp.reshape(own_len, (1,)).astype(jnp.int32)
+    heads = []
+    for h in range(head_count):
+        cols = slice(h * HEAD_DIM, (h + 1) * HEAD_DIM)
+        keys_all = jnp.concatenate([cache_local[:, 0, cols], new_keys[:, h]], axis=0)
+        values_all = jnp.concatenate([cache_local[:, 1, cols], new_values[:, h]], axis=0)
+        heads.append(attend(queries[:, h], keys_all, values_all, live, cache_slots))
+    attended = jnp.concatenate(heads, axis=1)
     partial_out = jnp.dot(attended, out_cols, preferred_element_type=jnp.float32).astype(jnp.bfloat16)
     branch = lax.psum_scatter(partial_out, ("y", "c"), scatter_dimension=1, tiled=True)
     last_term = partial_out[new_rows - 1].reshape(n_y, n_c, n_zh, block_cols)

time: 223 us -> 207 us (0.928)
  matrix products: 22.1 us -> 6.09 us
  Pallas kernels: 0 us -> 11.9 us
  other arithmetic: 17.5 us -> 6.27 us
    dot_general x30 -> x0, matrix products: 17 us -> none  [the longest x15 12.3 us: fold_scores(): jnp.einsum('hqk,khd->hqd', weights, value_block.astype(jnp.float32), prec...]
    pallas_call x0 -> x1, Pallas kernels: none -> 11.9 us  [attend(): pl.pallas_call(functools.partial(attention_kernel, cache_slots, key_rows)...]
    lt x14 -> x0, other arithmetic: 9.14 us -> none  [advance(): allowed = (places < live_slots)[None, None, :]]
    reduce_sum x15 -> x0, other arithmetic: 3.19 us -> none  [fold_scores(): mass_sum = mass_sum * factor + jnp.sum(weights, axis=2)]
  transfers between devices with their start and end apart: 6 -> 6, of which waited for: 4 -> 4; matrix products, arithmetic and copies ran while one was open for 5% -> 6% of each run, Pallas kernels for 0% -> 0%
where the time goes in v5:
time: 207 us; the launch traced here: 206 us
  waiting for transfers between devices  60.5 us (29%)
  blocking collectives  49.3 us (24%)
  starting transfers between devices  45.8 us (22%)
  between operations  14.2 us (7%)
  local copies, waits for them, and re-layouts  12.3 us (6%)
  Pallas kernels  11.9 us (6%)
  other arithmetic  6.27 us (3%)
  matrix products  6.09 us (3%)
    all_gather x1, waiting for transfers between devices, per_device(): features = lax.all_gather(pair, ('y', 'c'), axis=1, tiled=True)  34.8 us
    all_to_all x1, blocking collectives, per_device(): last_terms = lax.all_to_all(last_term, GX, 0, 0, tiled=True)  29 us
    all_to_all x1, starting transfers between devices, per_device(): stats = lax.all_to_all(spread, GY, 0, 0, tiled=True)  20.6 us
    all_gather x1, blocking collectives, per_device(): pair = lax.all_gather(layer_input, 'zh', axis=1, tiled=True)  20.3 us
    ppermute x1, starting transfers between devices, per_device(): from_partner = lax.ppermute(theirs, 'zh', [(0, 1), (1, 0)])  12.5 us
    pallas_call x1, Pallas kernels, attend(): pl.pallas_call(functools.partial(attention_kernel, cache_slots, key_rows)...  11.9 us
    all_to_all x1, waiting for transfers between devices, per_device(): lax.all_to_all(jnp.broadcast_to(last_row[None], (n_gy, block_cols)), GY,...  11.3 us
    all_to_all x1, waiting for transfers between devices, per_device(): stats = lax.all_to_all(spread, GY, 0, 0, tiled=True)  10.8 us
  transfers between devices with their start and end apart: 6, of which 4 were waited for; matrix products, arithmetic and copies ran while one was open for 6% of the time, Pallas kernels for 0%

profile of v5, /device:TPU:2, one launch (start us, length us, event | category | flops | bytes accessed | tf_op | source)
XLA Modules:
  0.0 206.4 jit_solution(11211898911778272612)
XLA Ops:
  7.2 20.3 %all_gather.6 = bf16[512,256]{1,0:T(8,128)(2,1)} all-gather(bf16[512,128]{1,0:T(8,128)(2,1)} %param.7), channel_id=1, replica_groups=mesh['y'=4,'zh'=2,'c'=2,'zl'=8,'x'=4] {'zh'}, dimensions={1}, use_global_device_ids=true | all-gather | bytes 393216 | tf_op jit(solution)/shard_map/all_gather | solution.py:99
  27.6 2.9 %copy.62 = bf16[4,2,2,128,3,128]{5,3,2,1,0,4:T(8,128)(2,1)} copy(bf16[4,2,2,128,3,128]{5,3,1,2,0,4:T(8,128)(2,1)} %bitcast.57) | data formatting | bytes 3145728 | tf_op jit(solution)/shard_map/transpose | solution.py:102
  30.7 1.3 copy.64
  32.0 0.8 copy.65
  33.5 1.0 slice_bitcast_fusion
  34.5 34.8 %all-gather.2.cloned.1.call-done = bf16[512,2048]{1,0:T(8,128)(2,1)} async-done(((bf16[512,256]{1,0:T(8,128)(2,1)}), bf16[512,2048]{1,0:T(8,128)(2,1)}) %all-gather.2.cloned.1.call-update) | async-done | bytes 2097168 | tf_op jit(solution)/shard_map/all_gather | solution.py:100
  69.3 2.2 %fusion = f32[512]{0:T(512)S(1)} fusion(bf16[512,2048]{1,0:T(8,128)(2,1)} %all-gather.2.cloned.1.call-done), kind=kLoop, calls=%fused_computation.2 | loop fusion | flops 3145216 | bytes 2099200 | tf_op jit(solution)/shard_map/reduce_sum | solution.py:106
  71.6 2.8 %fusion.6 = bf16[512,3,128]{2,0,1:T(8,128)(2,1)S(1)} fusion(bf16[2048,3,128]{2,0,1:T(8,128)(2,1)} %bitcast.58, bf16[512,2048]{1,0:T(8,128)(2,1)S(1)} %copy-done.2, f32[512]{0:T(512)S(1)} %add_rsqrt_fusion), kind=kOutput, calls=%fused_computation.9 | convolution fusion | flops 808648704 | bytes 4065280 | tf_op jit(solution)/shard_map/td,dcf->tcf/dot_general | solution.py:108
  74.3 0.7 slice_bitcast_fusion.2
  75.0 1.5 pad_maximum_fusion
  76.5 11.9 %shard_map.102 = bf16[512,128]{1,0:T(8,128)(2,1)} custom-call(s32[1]{0:T(128)} %dynamic_slice.11.len_ref, bf16[512,128]{1,0:T(8,128)(2,1)} %get-tuple-element.44.q_ref, bf16[4096,128]{1,0:T(8,128)(2,1)} %get-tuple-element.47.k_ref, bf16[4096,128]{1,0:T(8,128)(2,1)} %get-tuple-element.48.v_ref), custom_call_target="tpu_custom_call" | custom-call | tf_op jit(solution)/shard_map/pallas_call | solution.py:60
  88.4 3.0 %convolution_convert_fusion = bf16[512,2048]{1,0:T(8,128)(2,1)} fusion(bf16[512,128]{1,0:T(8,128)(2,1)} %shard_map.102, bf16[128,2048]{0,1:T(8,128)(2,1)S(1)} %bitcast.56), kind=kOutput, calls=%fused_computation.4 | convolution fusion | flops 269484032 | bytes 2752512 | tf_op jit(solution)/shard_map/dot_general | solution.py:130
  91.5 0.8 slice_reduce_fusion.2
  92.3 29.0 %all_to_all.29 = bf16[16,1,128]{2,1,0:T(2,128)(2,1)S(1)} all-to-all(bf16[16,1,128]{2,1,0:T(2,128)(2,1)S(1)} %copy.67), channel_id=1, replica_groups=mesh['y'=4,'zh'=2,'c'=2,'zl'=8,'x'=4] {'y','zh','c'}, dimensions={0} | all-to-all | bytes 8192 | tf_op jit(solution)/shard_map/all_to_all | solution.py:134
  122.0 5.6 %all-to-all-start.1 = ((bf16[32,1,128]{2,1,0:T(2,128)(2,1)}), bf16[32,1,128]{2,1,0:T(2,128)(2,1)S(1)}, u32[]{:S(2)}, u32[]{:S(2)}) async-start(bf16[32,1,128]{2,1,0:T(2,128)(2,1)} %broadcast_in_dim.6), calls=%async_computation.1 | async-start | bytes 32768 | tf_op jit(solution)/shard_map/all_to_all | solution.py:138
  127.6 11.3 %all-to-all-done.1 = bf16[32,1,128]{2,1,0:T(2,128)(2,1)S(1)} async-done(((bf16[32,1,128]{2,1,0:T(2,128)(2,1)}), bf16[32,1,128]{2,1,0:T(2,128)(2,1)S(1)}, u32[]{:S(2)}, u32[]{:S(2)}) %all-to-all-start.1) | async-done | bytes 8224 | tf_op jit(solution)/shard_map/all_to_all | solution.py:138
  139.5 0.9 all_to_all.22
  140.4 7.0 %all-to-all-start.2 = ((f32[16,2,2377]{2,1,0:T(2,128)}), f32[16,2,2377]{2,1,0:T(2,128)S(1)}, u32[]{:S(2)}, u32[]{:S(2)}) async-start(f32[16,2,2377]{2,1,0:T(2,128)} %all_to_all.22), calls=%async_computation.3 | async-start | bytes 622592 | tf_op jit(solution)/shard_map/all_to_all | solution.py:152
  147.4 1.0 copy.73
  149.1 12.5 %collective-permute-start = (bf16[512,128]{1,0:T(8,128)(2,1)S(1)}, bf16[512,128]{1,0:T(8,128)(2,1)S(1)}, u32[]{:S(2)}, u32[]{:S(2)}) collective-permute-start(bf16[512,128]{1,0:T(8,128)(2,1)S(1)} %bitcast.61), channel_id=1, source_target_pairs={{0,64},{64,0},{1,65},{65,1},{2,66},{66,2},{3,67},{67,3},{4,68},{68... | collective-permute-start | bytes 393224 | tf_op jit(solution)/shard_map/ppermute | solution.py:151
  161.6 3.6 %all-to-all-done.2 = f32[16,2,2377]{2,1,0:T(2,128)S(1)} async-done(((f32[16,2,2377]{2,1,0:T(2,128)}), f32[16,2,2377]{2,1,0:T(2,128)S(1)}, u32[]{:S(2)}, u32[]{:S(2)}) %all-to-all-start.2) | async-done | bytes 304288 | tf_op jit(solution)/shard_map/all_to_all | solution.py:152
  166.4 20.6 %all-to-all-start.3 = ((f32[32,2,2]{2,1,0:T(2,128)}), f32[32,2,2]{2,1,0:T(2,128)S(1)}, u32[]{:S(2)}, u32[]{:S(2)}) async-start(f32[32,2,2]{2,1,0:T(2,128)} %broadcast_in_dim.8), calls=%async_computation.4 | async-start | bytes 65536 | tf_op jit(solution)/shard_map/all_to_all | solution.py:159
  187.0 0.7 fusion.10
  187.7 10.8 %all-to-all-done.3 = f32[32,2,2]{2,1,0:T(2,128)S(1)} async-done(((f32[32,2,2]{2,1,0:T(2,128)}), f32[32,2,2]{2,1,0:T(2,128)S(1)}, u32[]{:S(2)}, u32[]{:S(2)}) %all-to-all-start.3) | async-done | bytes 544 | tf_op jit(solution)/shard_map/all_to_all | solution.py:159
  (49 shorter events, 5.2 us)
Async XLA Ops:
  7.2 131.9 %copy-start = (bf16[2376,128]{1,0:T(8,128)(2,1)S(1)}, bf16[2376,128]{1,0:T(8,128)(2,1)}, u32[]{:S(2)}) copy-start(bf16[2376,128]{1,0:T(8,128)(2,1)} %param.13) | copy-start | bytes 1824772
  7.2 62.1 %all-gather.2.cloned.1.call-start = ((), (), s32[]{:S(2)}) async-start(), calls=%async_computation.5 | async-start | bytes 2359296 | tf_op jit(solution)/shard_map/all_gather | solution.py:100
  27.5 112.0 %reduce-scatter.2.cloned.1.call-start = ((), (), s32[]{:S(2)}) async-start(), calls=%async_computation.6 | async-start | bytes 2359296 | tf_op jit(solution)/shard_map/reduce_scatter | solution.py:131
  27.6 2.9 %copy-start.4 = (bf16[1,3584,2,128]{3,2,1,0:T(2,128)(2,1)S(1)}, bf16[1,3584,2,128]{3,2,1,0:T(2,128)(2,1)}, u32[]{:S(2)}) copy-start(bf16[1,3584,2,128]{3,2,1,0:T(2,128)(2,1)} %param.10) | copy-start | bytes 5505028
  30.5 2.4 %copy-start.7 = (s32[32]{0:T(128)S(1)}, s32[32]{0:T(128)}, u32[]{:S(2)}) copy-start(s32[32]{0:T(128)} %param.11) | copy-start | bytes 388
  69.3 2.2 %copy-start.2 = (bf16[512,2048]{1,0:T(8,128)(2,1)S(1)}, bf16[512,2048]{1,0:T(8,128)(2,1)}, u32[]{:S(2)}) copy-start(bf16[512,2048]{1,0:T(8,128)(2,1)} %all-gather.2.cloned.1.call-done) | copy-start | bytes 6291460
  71.5 3.5 %copy-start.1 = (bf16[3584,128]{1,0:T(8,128)(2,1)S(1)}, bf16[3584,128]{1,0:T(8,128)(2,1)}, u32[]{:S(2)}) copy-start(bf16[3584,128]{1,0:T(8,128)(2,1)} %get-tuple-element.41) | copy-start | bytes 2752516
  76.5 11.9 %copy-start.3 = (bf16[128,4,2,2,128]{0,4,3,2,1:T(8,128)(2,1)S(1)}, bf16[128,4,2,2,128]{0,4,3,2,1:T(8,128)(2,1)}, u32[]{:S(2)}) copy-start(bf16[128,4,2,2,128]{0,4,3,2,1:T(8,128)(2,1)} %copy.65) | copy-start | bytes 1572868
  88.4 32.9 %copy-start.5 = (bf16[512,128]{1,0:T(8,128)(2,1)S(1)}, bf16[512,128]{1,0:T(8,128)(2,1)}, u32[]{:S(2)}) copy-start(bf16[512,128]{1,0:T(8,128)(2,1)} %param.7) | copy-start | bytes 393220
  88.4 39.1 %copy-start.8 = (bf16[128]{0:T(256)(128)(2,1)S(1)}, bf16[128]{0:T(256)(128)(2,1)}, u32[]{:S(2)}) copy-start(bf16[128]{0:T(256)(128)(2,1)} %param.12) | copy-start | bytes 772
  122.0 16.9 %all-to-all-start.1 = ((bf16[32,1,128]{2,1,0:T(2,128)(2,1)}), bf16[32,1,128]{2,1,0:T(2,128)(2,1)S(1)}, u32[]{:S(2)}, u32[]{:S(2)}) async-start(bf16[32,1,128]{2,1,0:T(2,128)(2,1)} %broadcast_in_dim.6), calls=%async_computation.1 | async-start | bytes 32768 | tf_op jit(solution)/shard_map/all_to_all | solution.py:138
  139.5 8.9 %copy-start.6 = (bf16[512,256]{1,0:T(8,128)(2,1)S(1)}, bf16[512,256]{1,0:T(8,128)(2,1)}, u32[]{:S(2)}) copy-start(bf16[512,256]{1,0:T(8,128)(2,1)} %reduce-scatter.2.cloned.1.call-done) | copy-start | bytes 786436
  140.4 24.9 %all-to-all-start.2 = ((f32[16,2,2377]{2,1,0:T(2,128)}), f32[16,2,2377]{2,1,0:T(2,128)S(1)}, u32[]{:S(2)}, u32[]{:S(2)}) async-start(f32[16,2,2377]{2,1,0:T(2,128)} %all_to_all.22), calls=%async_computation.3 | async-start | bytes 622592 | tf_op jit(solution)/shard_map/all_to_all | solution.py:152
  149.1 37.9 %collective-permute-start = (bf16[512,128]{1,0:T(8,128)(2,1)S(1)}, bf16[512,128]{1,0:T(8,128)(2,1)S(1)}, u32[]{:S(2)}, u32[]{:S(2)}) collective-permute-start(bf16[512,128]{1,0:T(8,128)(2,1)S(1)} %bitcast.61), channel_id=1, source_target_pairs={{0,64},{64,0},{1,65},{65,1},{2,66},{66,2},{3,67},{67,3},{4,68},{68... | collective-permute-start | bytes 393224 | tf_op jit(solution)/shard_map/ppermute | solution.py:151
  166.4 32.0 %all-to-all-start.3 = ((f32[32,2,2]{2,1,0:T(2,128)}), f32[32,2,2]{2,1,0:T(2,128)S(1)}, u32[]{:S(2)}, u32[]{:S(2)}) async-start(f32[32,2,2]{2,1,0:T(2,128)} %broadcast_in_dim.8), calls=%async_computation.4 | async-start | bytes 65536 | tf_op jit(solution)/shard_map/all_to_all | solution.py:159
Sparse Core Ops, SparseCore 0:
  27.6 41.6 all-gather.1
  91.6 42.5 reduce-scatter.1

commit v6 on v5

--- a/solution.py
+++ b/solution.py
@@ -144,11 +144,7 @@
     logit_part = jnp.einsum("rd,vd->rv", gained, head_weight, preferred_element_type=jnp.float32)
     packed = jnp.concatenate([logit_part, square_part], axis=1)
     packed, branch = lax.optimization_barrier((packed, branch))
-    branch = branch.reshape(new_rows, n_zh, block_cols)
-    zh = lax.axis_index("zh")
-    mine = lax.dynamic_index_in_dim(branch, zh, 1, keepdims=False)
-    theirs = lax.dynamic_index_in_dim(branch, 1 - zh, 1, keepdims=False)
-    from_partner = lax.ppermute(theirs, "zh", [(0, 1), (1, 0)])
+    branch = lax.psum_scatter(branch, "zh", scatter_dimension=1, tiled=True)
     packed = lax.all_to_all(packed, GX, 0, 0, tiled=True)
     own_requests = packed.shape[0] // n_gx
     packed = jnp.sum(packed.reshape(n_gx, own_requests, packed.shape[1]), axis=0)
@@ -160,9 +156,8 @@
     logit_scale = jnp.sqrt(jnp.sum(stats[:, 0], axis=0) / VOCAB)
     logit_peak = jnp.max(stats[:, 1], axis=0)
 
-    layer_output = (
-        layer_input.astype(jnp.float32) + mine.astype(jnp.float32) + from_partner.astype(jnp.float32)
-    ).astype(jnp.bfloat16)
+    branch, logit_scale, logit_peak = lax.optimization_barrier((branch, logit_scale, logit_peak))
+    layer_output = (layer_input.astype(jnp.float32) + branch.astype(jnp.float32)).astype(jnp.bfloat16)
     return (layer_output, appended, logit_scale, logit_peak)
 
 

time: 207 us -> 203 us (0.981)
  the two profiles are of different devices: /device:TPU:2 before, /device:TPU:1 now
where the time goes in v6:
time: 203 us
  waiting for transfers between devices  74 us (36%)
  blocking collectives  49 us (24%)
  starting transfers between devices  27.2 us (13%)
  local copies, waits for them, and re-layouts  14.2 us (7%)
  between operations  13.9 us (7%)
  Pallas kernels  11.9 us (6%)
  other arithmetic  6.26 us (3%)
  matrix products  6.1 us (3%)
    all_gather x1, waiting for transfers between devices, per_device(): features = lax.all_gather(pair, ('y', 'c'), axis=1, tiled=True)  36.2 us
    all_to_all x1, blocking collectives, per_device(): last_terms = lax.all_to_all(last_term, GX, 0, 0, tiled=True)  28.6 us
    all_gather x1, blocking collectives, per_device(): pair = lax.all_gather(layer_input, 'zh', axis=1, tiled=True)  20.4 us
    all_to_all x1, waiting for transfers between devices, per_device(): packed = lax.all_to_all(packed, GX, 0, 0, tiled=True)  15.1 us
    all_to_all x1, starting transfers between devices, per_device(): stats = lax.all_to_all(spread, GY, 0, 0, tiled=True)  13.9 us
    pallas_call x1, Pallas kernels, attend(): pl.pallas_call(functools.partial(attention_kernel, cache_slots, key_rows)...  11.9 us
    unnamed x4, waiting for transfers between devices  11.4 us
    all_to_all x1, waiting for transfers between devices, per_device(): lax.all_to_all(jnp.broadcast_to(last_row[None], (n_gy, block_cols)), GY,...  11.3 us
  transfers between devices with their start and end apart: 6, of which 4 were waited for; matrix products, arithmetic and copies ran while one was open for 6% of the time, Pallas kernels for 0%

profile of v6, /device:TPU:1, one launch (start us, length us, event | category | flops | bytes accessed | tf_op | source)
XLA Modules:
  0.0 202.6 jit_solution(7216806797140727373)
XLA Ops:
  7.2 20.4 %all_gather.6 = bf16[512,256]{1,0:T(8,128)(2,1)} all-gather(bf16[512,128]{1,0:T(8,128)(2,1)} %param.7), channel_id=1, replica_groups=mesh['y'=4,'zh'=2,'c'=2,'zl'=8,'x'=4] {'zh'}, dimensions={1}, use_global_device_ids=true | all-gather | bytes 393216 | tf_op jit(solution)/shard_map/all_gather | solution.py:99
  27.7 2.9 %copy.51 = bf16[4,2,2,128,3,128]{5,3,2,1,0,4:T(8,128)(2,1)} copy(bf16[4,2,2,128,3,128]{5,3,1,2,0,4:T(8,128)(2,1)} %bitcast.51) | data formatting | bytes 3145728 | tf_op jit(solution)/shard_map/transpose | solution.py:102
  30.8 0.8 copy-done.6
  31.9 0.8 copy.54
  33.3 1.0 slice_bitcast_fusion
  34.4 36.2 %all-gather.2.cloned.1.call-done = bf16[512,2048]{1,0:T(8,128)(2,1)} async-done(((bf16[512,256]{1,0:T(8,128)(2,1)}), bf16[512,2048]{1,0:T(8,128)(2,1)}) %all-gather.2.cloned.1.call-update) | async-done | bytes 2097168 | tf_op jit(solution)/shard_map/all_gather | solution.py:100
  70.6 2.2 %fusion = f32[512]{0:T(512)S(1)} fusion(bf16[512,2048]{1,0:T(8,128)(2,1)} %all-gather.2.cloned.1.call-done), kind=kLoop, calls=%fused_computation.2 | loop fusion | flops 3145216 | bytes 2099200 | tf_op jit(solution)/shard_map/reduce_sum | solution.py:106
  72.8 2.8 %fusion.6 = bf16[512,3,128]{2,0,1:T(8,128)(2,1)S(1)} fusion(bf16[2048,3,128]{2,0,1:T(8,128)(2,1)} %bitcast.52, bf16[512,2048]{1,0:T(8,128)(2,1)S(1)} %copy-done.2, f32[512]{0:T(512)S(1)} %add_rsqrt_fusion), kind=kOutput, calls=%fused_computation.9 | convolution fusion | flops 808648704 | bytes 4065280 | tf_op jit(solution)/shard_map/td,dcf->tcf/dot_general | solution.py:108
  76.3 1.5 pad_maximum_fusion
  77.8 11.9 %shard_map.102 = bf16[512,128]{1,0:T(8,128)(2,1)} custom-call(s32[1]{0:T(128)} %dynamic_slice.4.len_ref, bf16[512,128]{1,0:T(8,128)(2,1)} %get-tuple-element.50.q_ref, bf16[4096,128]{1,0:T(8,128)(2,1)} %get-tuple-element.51.k_ref, bf16[4096,128]{1,0:T(8,128)(2,1)} %get-tuple-element.52.v_ref), custom_call_target="tpu_custom_call" | custom-call | tf_op jit(solution)/shard_map/pallas_call | solution.py:60
  89.7 3.0 %convolution_convert_fusion = bf16[512,2048]{1,0:T(8,128)(2,1)} fusion(bf16[512,128]{1,0:T(8,128)(2,1)} %shard_map.102, bf16[128,2048]{0,1:T(8,128)(2,1)S(1)} %bitcast.50), kind=kOutput, calls=%fused_computation.4 | convolution fusion | flops 269484032 | bytes 2752512 | tf_op jit(solution)/shard_map/dot_general | solution.py:130
  92.7 0.8 slice_reduce_fusion.2
  93.6 28.6 %all_to_all.29 = bf16[16,1,128]{2,1,0:T(2,128)(2,1)S(1)} all-to-all(bf16[16,1,128]{2,1,0:T(2,128)(2,1)S(1)} %copy.56), channel_id=1, replica_groups=mesh['y'=4,'zh'=2,'c'=2,'zl'=8,'x'=4] {'y','zh','c'}, dimensions={0} | all-to-all | bytes 8192 | tf_op jit(solution)/shard_map/all_to_all | solution.py:134
  122.8 5.0 %all-to-all-start.1 = ((bf16[32,1,128]{2,1,0:T(2,128)(2,1)}), bf16[32,1,128]{2,1,0:T(2,128)(2,1)S(1)}, u32[]{:S(2)}, u32[]{:S(2)}) async-start(bf16[32,1,128]{2,1,0:T(2,128)(2,1)} %broadcast_in_dim.6), calls=%async_computation.1 | async-start | bytes 32768 | tf_op jit(solution)/shard_map/all_to_all | solution.py:138
  127.8 11.3 %all-to-all-done.1 = bf16[32,1,128]{2,1,0:T(2,128)(2,1)S(1)} async-done(((bf16[32,1,128]{2,1,0:T(2,128)(2,1)}), bf16[32,1,128]{2,1,0:T(2,128)(2,1)S(1)}, u32[]{:S(2)}, u32[]{:S(2)}) %all-to-all-start.1) | async-done | bytes 8224 | tf_op jit(solution)/shard_map/all_to_all | solution.py:138
  139.8 0.9 all_to_all.22
  140.7 8.1 %all-to-all-start.2 = ((f32[16,2,2377]{2,1,0:T(2,128)}), f32[16,2,2377]{2,1,0:T(2,128)S(1)}, u32[]{:S(2)}, u32[]{:S(2)}) async-start(f32[16,2,2377]{2,1,0:T(2,128)} %all_to_all.22), calls=%async_computation.3 | async-start | bytes 622592 | tf_op jit(solution)/shard_map/all_to_all | solution.py:148
  148.9 1.8 copy.61
  150.7 15.1 %all-to-all-done.2 = f32[16,2,2377]{2,1,0:T(2,128)S(1)} async-done(((f32[16,2,2377]{2,1,0:T(2,128)}), f32[16,2,2377]{2,1,0:T(2,128)S(1)}, u32[]{:S(2)}, u32[]{:S(2)}) %all-to-all-start.2) | async-done | bytes 304288 | tf_op jit(solution)/shard_map/all_to_all | solution.py:148
  166.9 13.9 %all-to-all-start.3 = ((f32[32,2,2]{2,1,0:T(2,128)}), f32[32,2,2]{2,1,0:T(2,128)S(1)}, u32[]{:S(2)}, u32[]{:S(2)}) async-start(f32[32,2,2]{2,1,0:T(2,128)} %broadcast_in_dim.8), calls=%async_computation.4 | async-start | bytes 65536 | tf_op jit(solution)/shard_map/all_to_all | solution.py:155
  180.9 1.0 copy.60
  181.9 11.4 %reduce-scatter.7.cloned.1.call-done = bf16[128,512]{1,0:T(8,128)(2,1)} async-done(((bf16[256,512]{1,0:T(8,128)(2,1)}), bf16[128,512]{1,0:T(8,128)(2,1)}) %reduce-scatter.7.cloned.1.call-update) | async-done | bytes 131088
  193.2 1.0 copy.62
  195.4 0.7 add_convert_fusion
  (49 shorter events, 5.5 us)
Async XLA Ops:
  7.2 132.2 %copy-start = (bf16[2376,128]{1,0:T(8,128)(2,1)S(1)}, bf16[2376,128]{1,0:T(8,128)(2,1)}, u32[]{:S(2)}) copy-start(bf16[2376,128]{1,0:T(8,128)(2,1)} %param.13) | copy-start | bytes 1824772
  7.2 63.4 %all-gather.2.cloned.1.call-start = ((), (), s32[]{:S(2)}) async-start(), calls=%async_computation.6 | async-start | bytes 2359296 | tf_op jit(solution)/shard_map/all_gather | solution.py:100
  27.6 112.2 %reduce-scatter.5.cloned.1.call-start = ((), (), s32[]{:S(2)}) async-start(), calls=%async_computation.7 | async-start | bytes 2359296 | tf_op jit(solution)/shard_map/reduce_scatter | solution.py:131
  27.7 2.9 %copy-start.4 = (bf16[1,3584,2,128]{3,2,1,0:T(2,128)(2,1)S(1)}, bf16[1,3584,2,128]{3,2,1,0:T(2,128)(2,1)}, u32[]{:S(2)}) copy-start(bf16[1,3584,2,128]{3,2,1,0:T(2,128)(2,1)} %param.10) | copy-start | bytes 5505028
  30.6 1.0 copy-start.6
  30.6 2.2 %copy-start.7 = (s32[32]{0:T(128)S(1)}, s32[32]{0:T(128)}, u32[]{:S(2)}) copy-start(s32[32]{0:T(128)} %param.11) | copy-start | bytes 388
  70.6 2.2 %copy-start.2 = (bf16[512,2048]{1,0:T(8,128)(2,1)S(1)}, bf16[512,2048]{1,0:T(8,128)(2,1)}, u32[]{:S(2)}) copy-start(bf16[512,2048]{1,0:T(8,128)(2,1)} %all-gather.2.cloned.1.call-done) | copy-start | bytes 6291460
  72.8 3.5 %copy-start.1 = (bf16[3584,128]{1,0:T(8,128)(2,1)S(1)}, bf16[3584,128]{1,0:T(8,128)(2,1)}, u32[]{:S(2)}) copy-start(bf16[3584,128]{1,0:T(8,128)(2,1)} %get-tuple-element.47) | copy-start | bytes 2752516
  77.8 11.9 %copy-start.3 = (bf16[128,4,2,2,128]{0,4,3,2,1:T(8,128)(2,1)S(1)}, bf16[128,4,2,2,128]{0,4,3,2,1:T(8,128)(2,1)}, u32[]{:S(2)}) copy-start(bf16[128,4,2,2,128]{0,4,3,2,1:T(8,128)(2,1)} %copy.54) | copy-start | bytes 1572868
  89.7 32.5 %copy-start.5 = (bf16[512,128]{1,0:T(8,128)(2,1)S(1)}, bf16[512,128]{1,0:T(8,128)(2,1)}, u32[]{:S(2)}) copy-start(bf16[512,128]{1,0:T(8,128)(2,1)} %param.7) | copy-start | bytes 393220
  89.7 38.1 %copy-start.8 = (bf16[128]{0:T(256)(128)(2,1)S(1)}, bf16[128]{0:T(256)(128)(2,1)}, u32[]{:S(2)}) copy-start(bf16[128]{0:T(256)(128)(2,1)} %param.12) | copy-start | bytes 772
  122.8 16.4 %all-to-all-start.1 = ((bf16[32,1,128]{2,1,0:T(2,128)(2,1)}), bf16[32,1,128]{2,1,0:T(2,128)(2,1)S(1)}, u32[]{:S(2)}, u32[]{:S(2)}) async-start(bf16[32,1,128]{2,1,0:T(2,128)(2,1)} %broadcast_in_dim.6), calls=%async_computation.1 | async-start | bytes 32768 | tf_op jit(solution)/shard_map/all_to_all | solution.py:138
  140.7 25.1 %all-to-all-start.2 = ((f32[16,2,2377]{2,1,0:T(2,128)}), f32[16,2,2377]{2,1,0:T(2,128)S(1)}, u32[]{:S(2)}, u32[]{:S(2)}) async-start(f32[16,2,2377]{2,1,0:T(2,128)} %all_to_all.22), calls=%async_computation.3 | async-start | bytes 622592 | tf_op jit(solution)/shard_map/all_to_all | solution.py:148
  148.8 44.4 %reduce-scatter.7.cloned.1.call-start = ((), (), s32[]{:S(2)}) async-start(), calls=%async_computation.8 | async-start | bytes 393216
  166.9 27.3 %all-to-all-start.3 = ((f32[32,2,2]{2,1,0:T(2,128)}), f32[32,2,2]{2,1,0:T(2,128)S(1)}, u32[]{:S(2)}, u32[]{:S(2)}) async-start(f32[32,2,2]{2,1,0:T(2,128)} %broadcast_in_dim.8), calls=%async_computation.4 | async-start | bytes 65536 | tf_op jit(solution)/shard_map/all_to_all | solution.py:155
Sparse Core Ops, SparseCore 0:
  27.8 42.7 all-gather.1
  92.9 40.2 reduce-scatter.4
  152.4 40.7 reduce-scatter.6

commit v7 on v6

--- a/solution.py
+++ b/solution.py
@@ -117,6 +117,7 @@
 
     out_cols = output_weight.reshape(-1, n_y, n_zh, n_c, block_cols)
     out_cols = jnp.transpose(out_cols, (0, 1, 3, 2, 4)).reshape(output_weight.shape)
+    partner_cols = lax.ppermute(out_cols, "zh", [(0, 1), (1, 0)])
 
     cache_slots = cache_local.shape[0]
     live = jnp.reshape(own_len, (1,)).astype(jnp.int32)
@@ -127,11 +128,19 @@
         values_all = jnp.concatenate([cache_local[:, 1, cols], new_values[:, h]], axis=0)
         heads.append(attend(queries[:, h], keys_all, values_all, live, cache_slots))
     attended = jnp.concatenate(heads, axis=1)
+    pair = [(0, 1), (1, 0)]
+    partner_attended = lax.ppermute(attended, "zh", pair)
     partial_out = jnp.dot(attended, out_cols, preferred_element_type=jnp.float32).astype(jnp.bfloat16)
-    branch = lax.psum_scatter(partial_out, ("y", "c"), scatter_dimension=1, tiled=True)
     last_term = partial_out[new_rows - 1].reshape(n_y, n_c, n_zh, block_cols)
     last_term = jnp.transpose(last_term, (0, 2, 1, 3)).reshape(n_gx, block_cols)
     last_terms = lax.all_to_all(last_term, GX, 0, 0, tiled=True)
+    partner_attended, last_terms = lax.optimization_barrier((partner_attended, last_terms))
+    partner_out = jnp.dot(partner_attended, partner_cols, preferred_element_type=jnp.float32).astype(jnp.bfloat16)
+    pair_out = (partial_out.astype(jnp.float32) + partner_out.astype(jnp.float32)).astype(jnp.bfloat16)
+    branch = lax.psum_scatter(pair_out, ("y", "c"), scatter_dimension=1, tiled=True)
+    branch = lax.dynamic_index_in_dim(
+        branch.reshape(new_rows, n_zh, block_cols), lax.axis_index("zh"), 1, keepdims=False
+    )
     last_row = (
         layer_input[new_rows - 1].astype(jnp.float32) + jnp.sum(last_terms.astype(jnp.float32), axis=0)
     ).astype(jnp.bfloat16)
@@ -143,8 +152,6 @@
     gained = (last_wide * final_gain.astype(jnp.float32)).astype(jnp.bfloat16)
     logit_part = jnp.einsum("rd,vd->rv", gained, head_weight, preferred_element_type=jnp.float32)
     packed = jnp.concatenate([logit_part, square_part], axis=1)
-    packed, branch = lax.optimization_barrier((packed, branch))
-    branch = lax.psum_scatter(branch, "zh", scatter_dimension=1, tiled=True)
     packed = lax.all_to_all(packed, GX, 0, 0, tiled=True)
     own_requests = packed.shape[0] // n_gx
     packed = jnp.sum(packed.reshape(n_gx, own_requests, packed.shape[1]), axis=0)

time: 203 us -> 209 us (1.030)
  waiting for transfers between devices: 74 us -> 45.1 us
  starting transfers between devices: 27.2 us -> 49.5 us
  blocking collectives: 49 us -> 60.6 us
    ppermute x0 -> x2, starting transfers between devices: none -> 25.3 us  [the longest x1 12.8 us: per_device(): partner_cols = lax.ppermute(out_cols, 'zh', [(0, 1), (1, 0)])]
    all_to_all x0 -> x1, blocking collectives: none -> 21.7 us  [per_device(): packed = lax.all_to_all(packed, GX, 0, 0, tiled=True)]
    all_to_all x1 -> x0, waiting for transfers between devices: 15.1 us -> none  [per_device(): packed = lax.all_to_all(packed, GX, 0, 0, tiled=True)]
    all_gather x1, waiting for transfers between devices: 36.2 us -> 23.2 us  [per_device(): features = lax.all_gather(pair, ('y', 'c'), axis=1, tiled=True)]
    unnamed x4 -> x2, waiting for transfers between devices: 11.4 us -> 0.03 us
    all_to_all x1, waiting for transfers between devices: 0.01 us -> 10.5 us  [per_device(): stats = lax.all_to_all(spread, GY, 0, 0, tiled=True)]
    all_to_all x1, blocking collectives: 28.6 us -> 18.5 us  [per_device(): last_terms = lax.all_to_all(last_term, GX, 0, 0, tiled=True)]
    all_to_all x1 -> x0, starting transfers between devices: 8.11 us -> none  [per_device(): packed = lax.all_to_all(packed, GX, 0, 0, tiled=True)]
  transfers between devices with their start and end apart: 6 -> 6, of which waited for: 4 -> 3; matrix products, arithmetic and copies ran while one was open for 6% -> 10% of each run, Pallas kernels for 0% -> 6%
where the time goes in v7:
time: 209 us; the launch traced here: 208 us
  blocking collectives  60.6 us (29%)
  starting transfers between devices  49.5 us (24%)
  waiting for transfers between devices  45.1 us (22%)
  between operations  14.3 us (7%)
  local copies, waits for them, and re-layouts  12.4 us (6%)
  Pallas kernels  11.9 us (6%)
  matrix products  8.02 us (4%)
  other arithmetic  6.24 us (3%)
    all_gather x1, waiting for transfers between devices, per_device(): features = lax.all_gather(pair, ('y', 'c'), axis=1, tiled=True)  23.2 us
    all_to_all x1, blocking collectives, per_device(): packed = lax.all_to_all(packed, GX, 0, 0, tiled=True)  21.7 us
    all_gather x1, blocking collectives, per_device(): pair = lax.all_gather(layer_input, 'zh', axis=1, tiled=True)  20.4 us
    all_to_all x1, blocking collectives, per_device(): last_terms = lax.all_to_all(last_term, GX, 0, 0, tiled=True)  18.5 us
    ppermute x1, starting transfers between devices, per_device(): partner_cols = lax.ppermute(out_cols, 'zh', [(0, 1), (1, 0)])  12.8 us
    ppermute x1, starting transfers between devices, per_device(): partner_attended = lax.ppermute(attended, 'zh', pair)  12.5 us
    all_to_all x1, starting transfers between devices, per_device(): stats = lax.all_to_all(spread, GY, 0, 0, tiled=True)  12.3 us
    pallas_call x1, Pallas kernels, attend(): pl.pallas_call(functools.partial(attention_kernel, cache_slots, key_rows)...  11.9 us
  transfers between devices with their start and end apart: 6, of which 3 were waited for; matrix products, arithmetic and copies ran while one was open for 10% of the time, Pallas kernels for 6%

profile of v7, /device:TPU:1, one launch (start us, length us, event | category | flops | bytes accessed | tf_op | source)
XLA Modules:
  0.0 208.0 jit_solution(12995045348686698605)
XLA Ops:
  7.2 20.4 %all_gather.6 = bf16[512,256]{1,0:T(8,128)(2,1)} all-gather(bf16[512,128]{1,0:T(8,128)(2,1)} %param.7), channel_id=1, replica_groups=mesh['y'=4,'zh'=2,'c'=2,'zl'=8,'x'=4] {'zh'}, dimensions={1}, use_global_device_ids=true | all-gather | bytes 393216 | tf_op jit(solution)/shard_map/all_gather | solution.py:99
  27.7 1.3 copy.87
  29.0 0.8 copy.88
  29.8 12.8 %collective-permute-start.1 = (bf16[128,2048]{0,1:T(8,128)(2,1)}, bf16[128,2048]{0,1:T(8,128)(2,1)}, u32[]{:S(2)}, u32[]{:S(2)}) collective-permute-start(bf16[128,2048]{0,1:T(8,128)(2,1)} %bitcast.12), channel_id=1, source_target_pairs={{0,64},{64,0},{1,65},{65,1},{2,66},{66,2},{3,67},{67,3},{4,68},{68... | collective-permute-start | bytes 1572872 | tf_op jit(solution)/shard_map/ppermute | solution.py:120
  42.7 1.3 copy.85
  43.9 1.8 copy.117
  46.3 1.0 slice_bitcast_fusion
  47.3 23.2 %all-gather.2.cloned.1.call-done = bf16[512,2048]{1,0:T(8,128)(2,1)} async-done(((bf16[512,256]{1,0:T(8,128)(2,1)}), bf16[512,2048]{1,0:T(8,128)(2,1)}) %all-gather.2.cloned.1.call-update) | async-done | bytes 2097168 | tf_op jit(solution)/shard_map/all_gather | solution.py:100
  70.6 2.2 %fusion = f32[512]{0:T(512)S(1)} fusion(bf16[512,2048]{1,0:T(8,128)(2,1)} %all-gather.2.cloned.1.call-done), kind=kLoop, calls=%fused_computation.2 | loop fusion | flops 3145216 | bytes 2099200 | tf_op jit(solution)/shard_map/reduce_sum | solution.py:106
  72.8 2.8 %fusion.6 = bf16[512,3,128]{2,0,1:T(8,128)(2,1)S(1)} fusion(bf16[2048,3,128]{2,0,1:T(8,128)(2,1)} %bitcast.58, bf16[512,2048]{1,0:T(8,128)(2,1)S(1)} %copy-done.2, f32[512]{0:T(512)S(1)} %add_rsqrt_fusion), kind=kOutput, calls=%fused_computation.11 | convolution fusion | flops 808648704 | bytes 4065280 | tf_op jit(solution)/shard_map/td,dcf->tcf/dot_general | solution.py:108
  76.3 1.5 pad_maximum_fusion
  77.8 11.9 %shard_map.102 = bf16[512,128]{1,0:T(8,128)(2,1)} custom-call(s32[1]{0:T(128)} %dynamic_slice.8.len_ref, bf16[512,128]{1,0:T(8,128)(2,1)} %get-tuple-element.54.q_ref, bf16[4096,128]{1,0:T(8,128)(2,1)} %get-tuple-element.55.k_ref, bf16[4096,128]{1,0:T(8,128)(2,1)} %get-tuple-element.56.v_ref), custom_call_target="tpu_custom_call" | custom-call | tf_op jit(solution)/shard_map/pallas_call | solution.py:60
  89.6 12.5 %collective-permute-start = (bf16[512,128]{1,0:T(8,128)(2,1)}, bf16[512,128]{1,0:T(8,128)(2,1)S(1)}, u32[]{:S(2)}, u32[]{:S(2)}) collective-permute-start(bf16[512,128]{1,0:T(8,128)(2,1)} %shard_map.102), channel_id=1, source_target_pairs={{0,64},{64,0},{1,65},{65,1},{2,66},{66,2},{3,67},{67,3},{4,68},{68... | collective-permute-start | bytes 393224 | tf_op jit(solution)/shard_map/ppermute | solution.py:132
  102.2 1.8 convolution_convert_fusion.1
  104.1 18.5 %all_to_all.29 = bf16[16,1,128]{2,1,0:T(2,128)(2,1)S(1)} all-to-all(bf16[16,1,128]{2,1,0:T(2,128)(2,1)S(1)} %copy.90), channel_id=1, replica_groups=mesh['y'=4,'zh'=2,'c'=2,'zl'=8,'x'=4] {'y','zh','c'}, dimensions={0} | all-to-all | bytes 8192 | tf_op jit(solution)/shard_map/all_to_all | solution.py:136
  122.6 3.1 %add_convert_fusion = bf16[512,2048]{1,0:T(8,128)(2,1)} fusion(bf16[512,2048]{1,0:T(8,128)(2,1)S(1)} %convolution_convert_fusion.1, bf16[512,128]{1,0:T(8,128)(2,1)S(1)} %collective-permute-done, bf16[128,2048]{0,1:T(8,128)(2,1)} %collective-permute-done.1), kind=kOutput, calls=%fused_computation.4 | convolution fusion | flops 273678336 | bytes 4849664 | tf_op jit(solution)/shard_map/dot_general | solution.py:138
  125.8 0.9 copy-done.4
  127.2 11.8 %all-to-all-start.1 = ((bf16[32,1,128]{2,1,0:T(2,128)(2,1)}), bf16[32,1,128]{2,1,0:T(2,128)(2,1)S(1)}, u32[]{:S(2)}, u32[]{:S(2)}) async-start(bf16[32,1,128]{2,1,0:T(2,128)(2,1)} %broadcast_in_dim.4), calls=%async_computation.2 | async-start | bytes 32768 | tf_op jit(solution)/shard_map/all_to_all | solution.py:147
  139.1 11.3 %all-to-all-done.1 = bf16[32,1,128]{2,1,0:T(2,128)(2,1)S(1)} async-done(((bf16[32,1,128]{2,1,0:T(2,128)(2,1)}), bf16[32,1,128]{2,1,0:T(2,128)(2,1)S(1)}, u32[]{:S(2)}, u32[]{:S(2)}) %all-to-all-start.1) | async-done | bytes 8224 | tf_op jit(solution)/shard_map/all_to_all | solution.py:147
  151.4 21.7 %all_to_all.30 = f32[16,2,2377]{2,1,0:T(2,128)S(1)} all-to-all(f32[16,2,2377]{2,1,0:T(2,128)S(1)} %copy.95), channel_id=1, replica_groups=mesh['y'=4,'zh'=2,'c'=2,'zl'=8,'x'=4] {'y','zh','c'}, dimensions={0} | all-to-all | bytes 608512 | tf_op jit(solution)/shard_map/all_to_all | solution.py:155
  174.2 12.3 %all-to-all-start.3 = ((f32[32,2,2]{2,1,0:T(2,128)}), f32[32,2,2]{2,1,0:T(2,128)S(1)}, u32[]{:S(2)}, u32[]{:S(2)}) async-start(f32[32,2,2]{2,1,0:T(2,128)} %broadcast_in_dim.5), calls=%async_computation.4 | async-start | bytes 65536 | tf_op jit(solution)/shard_map/all_to_all | solution.py:162
  186.6 1.0 copy.99
  187.6 10.5 %all-to-all-done.3 = f32[32,2,2]{2,1,0:T(2,128)S(1)} async-done(((f32[32,2,2]{2,1,0:T(2,128)}), f32[32,2,2]{2,1,0:T(2,128)S(1)}, u32[]{:S(2)}, u32[]{:S(2)}) %all-to-all-start.3) | async-done | bytes 544 | tf_op jit(solution)/shard_map/all_to_all | solution.py:162
  199.2 1.0 reshape.66
  (49 shorter events, 6.3 us)
Async XLA Ops:
  7.2 143.6 %copy-start = (bf16[2376,128]{1,0:T(8,128)(2,1)S(1)}, bf16[2376,128]{1,0:T(8,128)(2,1)}, u32[]{:S(2)}) copy-start(bf16[2376,128]{1,0:T(8,128)(2,1)} %param.13) | copy-start | bytes 1824772
  7.2 35.5 %copy-start.3 = (bf16[2048,3,128]{2,0,1:T(8,128)(2,1)S(1)}, bf16[2048,3,128]{2,0,1:T(8,128)(2,1)}, u32[]{:S(2)}) copy-start(bf16[2048,3,128]{2,0,1:T(8,128)(2,1)} %param.8) | copy-start | bytes 4718596
  7.2 63.4 %all-gather.2.cloned.1.call-start = ((), (), s32[]{:S(2)}) async-start(), calls=%async_computation.5 | async-start | bytes 2359296 | tf_op jit(solution)/shard_map/all_gather | solution.py:100
  27.7 171.5 %reduce-scatter.2.cloned.1.call-start = ((), (), s32[]{:S(2)}) async-start(), calls=%async_computation.6 | async-start | bytes 2359296 | tf_op jit(solution)/shard_map/reduce_scatter | solution.py:140
  29.8 92.8 %collective-permute-start.1 = (bf16[128,2048]{0,1:T(8,128)(2,1)}, bf16[128,2048]{0,1:T(8,128)(2,1)}, u32[]{:S(2)}, u32[]{:S(2)}) collective-permute-start(bf16[128,2048]{0,1:T(8,128)(2,1)} %bitcast.12), channel_id=1, source_target_pairs={{0,64},{64,0},{1,65},{65,1},{2,66},{66,2},{3,67},{67,3},{4,68},{68... | collective-permute-start | bytes 1572872 | tf_op jit(solution)/shard_map/ppermute | solution.py:120
  43.9 1.8 copy-start.5
  70.6 2.2 %copy-start.2 = (bf16[512,2048]{1,0:T(8,128)(2,1)S(1)}, bf16[512,2048]{1,0:T(8,128)(2,1)}, u32[]{:S(2)}) copy-start(bf16[512,2048]{1,0:T(8,128)(2,1)} %all-gather.2.cloned.1.call-done) | copy-start | bytes 6291460
  72.8 3.5 %copy-start.1 = (bf16[3584,128]{1,0:T(8,128)(2,1)S(1)}, bf16[3584,128]{1,0:T(8,128)(2,1)}, u32[]{:S(2)}) copy-start(bf16[3584,128]{1,0:T(8,128)(2,1)} %get-tuple-element.51) | copy-start | bytes 2752516
  89.6 33.0 %collective-permute-start = (bf16[512,128]{1,0:T(8,128)(2,1)}, bf16[512,128]{1,0:T(8,128)(2,1)S(1)}, u32[]{:S(2)}, u32[]{:S(2)}) collective-permute-start(bf16[512,128]{1,0:T(8,128)(2,1)} %shard_map.102), channel_id=1, source_target_pairs={{0,64},{64,0},{1,65},{65,1},{2,66},{66,2},{3,67},{67,3},{4,68},{68... | collective-permute-start | bytes 393224 | tf_op jit(solution)/shard_map/ppermute | solution.py:132
  125.7 0.9 copy-start.4
  125.7 13.3 %copy-start.6 = (bf16[128]{0:T(256)(128)(2,1)S(1)}, bf16[128]{0:T(256)(128)(2,1)}, u32[]{:S(2)}) copy-start(bf16[128]{0:T(256)(128)(2,1)} %param.12) | copy-start | bytes 772
  127.2 23.1 %all-to-all-start.1 = ((bf16[32,1,128]{2,1,0:T(2,128)(2,1)}), bf16[32,1,128]{2,1,0:T(2,128)(2,1)S(1)}, u32[]{:S(2)}, u32[]{:S(2)}) async-start(bf16[32,1,128]{2,1,0:T(2,128)(2,1)} %broadcast_in_dim.4), calls=%async_computation.2 | async-start | bytes 32768 | tf_op jit(solution)/shard_map/all_to_all | solution.py:147
  174.2 23.9 %all-to-all-start.3 = ((f32[32,2,2]{2,1,0:T(2,128)}), f32[32,2,2]{2,1,0:T(2,128)S(1)}, u32[]{:S(2)}, u32[]{:S(2)}) async-start(f32[32,2,2]{2,1,0:T(2,128)} %broadcast_in_dim.5), calls=%async_computation.4 | async-start | bytes 65536 | tf_op jit(solution)/shard_map/all_to_all | solution.py:162
Sparse Core Ops, SparseCore 0:
  27.8 42.7 all-gather.1
  125.9 36.7 reduce-scatter.1

commit v8 on v6

--- a/solution.py
+++ b/solution.py
@@ -131,13 +131,13 @@
     branch = lax.psum_scatter(partial_out, ("y", "c"), scatter_dimension=1, tiled=True)
     last_term = partial_out[new_rows - 1].reshape(n_y, n_c, n_zh, block_cols)
     last_term = jnp.transpose(last_term, (0, 2, 1, 3)).reshape(n_gx, block_cols)
-    last_terms = lax.all_to_all(last_term, GX, 0, 0, tiled=True)
-    last_row = (
-        layer_input[new_rows - 1].astype(jnp.float32) + jnp.sum(last_terms.astype(jnp.float32), axis=0)
-    ).astype(jnp.bfloat16)
-    every_last = lax.all_to_all(
-        jnp.broadcast_to(last_row[None], (n_gy, block_cols)), GY, 0, 0, tiled=True
+    own_block = (lax.axis_index(GX) == jnp.arange(n_gx))[:, None]
+    terms = last_term.astype(jnp.float32) + jnp.where(
+        own_block, layer_input[new_rows - 1].astype(jnp.float32)[None], 0.0
     )
+    spread = jnp.broadcast_to(terms[:, None], (n_gx, n_gy, block_cols)).reshape(n_gx * n_gy, block_cols)
+    rows_in = lax.all_to_all(spread, GX + GY, 0, 0, tiled=True)
+    every_last = jnp.sum(rows_in.reshape(n_gx, n_gy, block_cols), axis=0).astype(jnp.bfloat16)
     last_wide = every_last.astype(jnp.float32)
     square_part = jnp.sum(last_wide * last_wide, axis=1, keepdims=True)
     gained = (last_wide * final_gain.astype(jnp.float32)).astype(jnp.bfloat16)

time: 203 us -> 204 us (level)
  blocking collectives: 49 us -> 20.4 us
  starting transfers between devices: 27.2 us -> 43.2 us
  waiting for transfers between devices: 74 us -> 87.1 us
    all_to_all x1 -> x0, blocking collectives: 28.6 us -> none  [per_device(): last_terms = lax.all_to_all(last_term, GX, 0, 0, tiled=True)]
    all_to_all x1, starting transfers between devices: 5 us -> 19.6 us  [per_device(): rows_in = lax.all_to_all(spread, GX + GY, 0, 0, tiled=True)]
    all_to_all x1, waiting for transfers between devices: 11.3 us -> 24.5 us  [per_device(): rows_in = lax.all_to_all(spread, GX + GY, 0, 0, tiled=True)]
    unnamed x22 -> x20, local copies, waits for them, and re-layouts: 4.11 us -> 4.36 us
  transfers between devices with their start and end apart: 6 -> 6, of which waited for: 4 -> 4; matrix products, arithmetic and copies ran while one was open for 6% -> 7% of each run, Pallas kernels for 0% -> 0%
where the time goes in v8:
time: 204 us; the launch traced here: 203 us
  waiting for transfers between devices  87.1 us (43%)
  starting transfers between devices  43.2 us (21%)
  blocking collectives  20.4 us (10%)
  between operations  13.9 us (7%)
  local copies, waits for them, and re-layouts  13.8 us (7%)
  Pallas kernels  11.9 us (6%)
  other arithmetic  7.08 us (3%)
  matrix products  6.09 us (3%)
    all_gather x1, waiting for transfers between devices, per_device(): features = lax.all_gather(pair, ('y', 'c'), axis=1, tiled=True)  35.9 us
    all_to_all x1, waiting for transfers between devices, per_device(): rows_in = lax.all_to_all(spread, GX + GY, 0, 0, tiled=True)  24.5 us
    all_gather x1, blocking collectives, per_device(): pair = lax.all_gather(layer_input, 'zh', axis=1, tiled=True)  20.4 us
    all_to_all x1, starting transfers between devices, per_device(): rows_in = lax.all_to_all(spread, GX + GY, 0, 0, tiled=True)  19.6 us
    all_to_all x1, waiting for transfers between devices, per_device(): packed = lax.all_to_all(packed, GX, 0, 0, tiled=True)  15.1 us
    all_to_all x1, starting transfers between devices, per_device(): stats = lax.all_to_all(spread, GY, 0, 0, tiled=True)  13.8 us
    pallas_call x1, Pallas kernels, attend(): pl.pallas_call(functools.partial(attention_kernel, cache_slots, key_rows)...  11.9 us
    unnamed x4, waiting for transfers between devices  11.5 us
  transfers between devices with their start and end apart: 6, of which 4 were waited for; matrix products, arithmetic and copies ran while one was open for 7% of the time, Pallas kernels for 0%

profile of v8, /device:TPU:1, one launch (start us, length us, event | category | flops | bytes accessed | tf_op | source)
XLA Modules:
  0.0 203.4 jit_solution(3235606285652982054)
XLA Ops:
  7.2 20.4 %all_gather.6 = bf16[512,256]{1,0:T(8,128)(2,1)} all-gather(bf16[512,128]{1,0:T(8,128)(2,1)} %param.7), channel_id=1, replica_groups=mesh['y'=4,'zh'=2,'c'=2,'zl'=8,'x'=4] {'zh'}, dimensions={1}, use_global_device_ids=true | all-gather | bytes 393216 | tf_op jit(solution)/shard_map/all_gather | solution.py:99
  27.7 2.9 %copy.48 = bf16[4,2,2,128,3,128]{5,3,2,1,0,4:T(8,128)(2,1)} copy(bf16[4,2,2,128,3,128]{5,3,1,2,0,4:T(8,128)(2,1)} %bitcast.49) | data formatting | bytes 3145728 | tf_op jit(solution)/shard_map/transpose | solution.py:102
  30.8 1.3 copy.50
  32.2 0.8 copy.51
  33.6 1.0 slice_bitcast_fusion
  34.6 35.9 %all-gather.2.cloned.1.call-done = bf16[512,2048]{1,0:T(8,128)(2,1)} async-done(((bf16[512,256]{1,0:T(8,128)(2,1)}), bf16[512,2048]{1,0:T(8,128)(2,1)}) %all-gather.2.cloned.1.call-update) | async-done | bytes 2097168 | tf_op jit(solution)/shard_map/all_gather | solution.py:100
  70.6 2.2 %fusion = f32[512]{0:T(512)S(1)} fusion(bf16[512,2048]{1,0:T(8,128)(2,1)} %all-gather.2.cloned.1.call-done), kind=kLoop, calls=%fused_computation.2 | loop fusion | flops 3145216 | bytes 2099200 | tf_op jit(solution)/shard_map/reduce_sum | solution.py:106
  72.8 2.8 %fusion.6 = bf16[512,3,128]{2,0,1:T(8,128)(2,1)S(1)} fusion(bf16[2048,3,128]{2,0,1:T(8,128)(2,1)} %bitcast.50, bf16[512,2048]{1,0:T(8,128)(2,1)S(1)} %copy-done.2, f32[512]{0:T(512)S(1)} %add_rsqrt_fusion), kind=kOutput, calls=%fused_computation.9 | convolution fusion | flops 808648704 | bytes 4065280 | tf_op jit(solution)/shard_map/td,dcf->tcf/dot_general | solution.py:108
  76.3 1.5 pad_maximum_fusion
  77.8 11.9 %shard_map.102 = bf16[512,128]{1,0:T(8,128)(2,1)} custom-call(s32[1]{0:T(128)} %dynamic_slice.4.len_ref, bf16[512,128]{1,0:T(8,128)(2,1)} %get-tuple-element.50.q_ref, bf16[4096,128]{1,0:T(8,128)(2,1)} %get-tuple-element.51.k_ref, bf16[4096,128]{1,0:T(8,128)(2,1)} %get-tuple-element.52.v_ref), custom_call_target="tpu_custom_call" | custom-call | tf_op jit(solution)/shard_map/pallas_call | solution.py:60
  89.7 3.0 %convolution_convert_fusion = bf16[512,2048]{1,0:T(8,128)(2,1)} fusion(bf16[512,128]{1,0:T(8,128)(2,1)} %shard_map.102, bf16[128,2048]{0,1:T(8,128)(2,1)S(1)} %bitcast.48), kind=kOutput, calls=%fused_computation.4 | convolution fusion | flops 269484032 | bytes 2752512 | tf_op jit(solution)/shard_map/dot_general | solution.py:130
  92.8 0.8 slice_convert_fusion
  93.6 0.7 broadcast_in_dim.48
  94.3 19.6 %all-to-all-start = ((f32[512,1,128]{2,1,0:T(1,128)}), f32[512,1,128]{2,1,0:T(1,128)S(1)}, u32[]{:S(2)}, u32[]{:S(2)}) async-start(f32[512,1,128]{2,1,0:T(1,128)} %bitcast.17), calls=%async_computation | async-start | bytes 524288 | tf_op jit(solution)/shard_map/all_to_all | solution.py:139
  114.0 24.5 %all-to-all-done = f32[512,1,128]{2,1,0:T(1,128)S(1)} async-done(((f32[512,1,128]{2,1,0:T(1,128)}), f32[512,1,128]{2,1,0:T(1,128)S(1)}, u32[]{:S(2)}, u32[]{:S(2)}) %all-to-all-start) | async-done | bytes 262176 | tf_op jit(solution)/shard_map/all_to_all | solution.py:139
  139.2 0.9 all_to_all.17
  140.1 9.6 %all-to-all-start.1 = ((f32[16,2,2377]{2,1,0:T(2,128)}), f32[16,2,2377]{2,1,0:T(2,128)S(1)}, u32[]{:S(2)}, u32[]{:S(2)}) async-start(f32[16,2,2377]{2,1,0:T(2,128)} %all_to_all.17), calls=%async_computation.2 | async-start | bytes 622592 | tf_op jit(solution)/shard_map/all_to_all | solution.py:148
  149.7 1.8 copy.57
  151.6 15.1 %all-to-all-done.1 = f32[16,2,2377]{2,1,0:T(2,128)S(1)} async-done(((f32[16,2,2377]{2,1,0:T(2,128)}), f32[16,2,2377]{2,1,0:T(2,128)S(1)}, u32[]{:S(2)}, u32[]{:S(2)}) %all-to-all-start.1) | async-done | bytes 304288 | tf_op jit(solution)/shard_map/all_to_all | solution.py:148
  167.8 13.8 %all-to-all-start.2 = ((f32[32,2,2]{2,1,0:T(2,128)}), f32[32,2,2]{2,1,0:T(2,128)S(1)}, u32[]{:S(2)}, u32[]{:S(2)}) async-start(f32[32,2,2]{2,1,0:T(2,128)} %broadcast_in_dim.50), calls=%async_computation.3 | async-start | bytes 65536 | tf_op jit(solution)/shard_map/all_to_all | solution.py:155
  181.7 1.0 copy.56
  182.6 11.5 %reduce-scatter.7.cloned.1.call-done = bf16[128,512]{1,0:T(8,128)(2,1)} async-done(((bf16[256,512]{1,0:T(8,128)(2,1)}), bf16[128,512]{1,0:T(8,128)(2,1)}) %reduce-scatter.7.cloned.1.call-update) | async-done | bytes 131088
  194.1 1.0 copy.58
  196.2 0.7 add_convert_fusion
  (46 shorter events, 4.7 us)
Async XLA Ops:
  7.2 131.6 %copy-start = (bf16[2376,128]{1,0:T(8,128)(2,1)S(1)}, bf16[2376,128]{1,0:T(8,128)(2,1)}, u32[]{:S(2)}) copy-start(bf16[2376,128]{1,0:T(8,128)(2,1)} %param.13) | copy-start | bytes 1824772
  7.2 63.4 %all-gather.2.cloned.1.call-start = ((), (), s32[]{:S(2)}) async-start(), calls=%async_computation.5 | async-start | bytes 2359296 | tf_op jit(solution)/shard_map/all_gather | solution.py:100
  27.6 111.5 %reduce-scatter.5.cloned.1.call-start = ((), (), s32[]{:S(2)}) async-start(), calls=%async_computation.6 | async-start | bytes 2359296 | tf_op jit(solution)/shard_map/reduce_scatter | solution.py:131
  27.7 2.9 %copy-start.4 = (bf16[1,3584,2,128]{3,2,1,0:T(2,128)(2,1)S(1)}, bf16[1,3584,2,128]{3,2,1,0:T(2,128)(2,1)}, u32[]{:S(2)}) copy-start(bf16[1,3584,2,128]{3,2,1,0:T(2,128)(2,1)} %param.10) | copy-start | bytes 5505028
  30.6 2.4 %copy-start.6 = (s32[32]{0:T(128)S(1)}, s32[32]{0:T(128)}, u32[]{:S(2)}) copy-start(s32[32]{0:T(128)} %param.11) | copy-start | bytes 388
  70.6 2.2 %copy-start.2 = (bf16[512,2048]{1,0:T(8,128)(2,1)S(1)}, bf16[512,2048]{1,0:T(8,128)(2,1)}, u32[]{:S(2)}) copy-start(bf16[512,2048]{1,0:T(8,128)(2,1)} %all-gather.2.cloned.1.call-done) | copy-start | bytes 6291460
  72.8 3.5 %copy-start.1 = (bf16[3584,128]{1,0:T(8,128)(2,1)S(1)}, bf16[3584,128]{1,0:T(8,128)(2,1)}, u32[]{:S(2)}) copy-start(bf16[3584,128]{1,0:T(8,128)(2,1)} %get-tuple-element.47) | copy-start | bytes 2752516
  77.8 11.9 %copy-start.3 = (bf16[128,4,2,2,128]{0,4,3,2,1:T(8,128)(2,1)S(1)}, bf16[128,4,2,2,128]{0,4,3,2,1:T(8,128)(2,1)}, u32[]{:S(2)}) copy-start(bf16[128,4,2,2,128]{0,4,3,2,1:T(8,128)(2,1)} %copy.51) | copy-start | bytes 1572868
  89.7 3.1 %copy-start.5 = (bf16[512,128]{1,0:T(8,128)(2,1)S(1)}, bf16[512,128]{1,0:T(8,128)(2,1)}, u32[]{:S(2)}) copy-start(bf16[512,128]{1,0:T(8,128)(2,1)} %param.7) | copy-start | bytes 393220
  92.7 21.3 %copy-start.7 = (bf16[128]{0:T(256)(128)(2,1)S(1)}, bf16[128]{0:T(256)(128)(2,1)}, u32[]{:S(2)}) copy-start(bf16[128]{0:T(256)(128)(2,1)} %param.12) | copy-start | bytes 772
  94.3 44.2 %all-to-all-start = ((f32[512,1,128]{2,1,0:T(1,128)}), f32[512,1,128]{2,1,0:T(1,128)S(1)}, u32[]{:S(2)}, u32[]{:S(2)}) async-start(f32[512,1,128]{2,1,0:T(1,128)} %bitcast.17), calls=%async_computation | async-start | bytes 524288 | tf_op jit(solution)/shard_map/all_to_all | solution.py:139
  140.1 26.6 %all-to-all-start.1 = ((f32[16,2,2377]{2,1,0:T(2,128)}), f32[16,2,2377]{2,1,0:T(2,128)S(1)}, u32[]{:S(2)}, u32[]{:S(2)}) async-start(f32[16,2,2377]{2,1,0:T(2,128)} %all_to_all.17), calls=%async_computation.2 | async-start | bytes 622592 | tf_op jit(solution)/shard_map/all_to_all | solution.py:148
  149.7 44.4 %reduce-scatter.7.cloned.1.call-start = ((), (), s32[]{:S(2)}) async-start(), calls=%async_computation.7 | async-start | bytes 393216
  167.8 27.3 %all-to-all-start.2 = ((f32[32,2,2]{2,1,0:T(2,128)}), f32[32,2,2]{2,1,0:T(2,128)S(1)}, u32[]{:S(2)}, u32[]{:S(2)}) async-start(f32[32,2,2]{2,1,0:T(2,128)} %broadcast_in_dim.50), calls=%async_computation.3 | async-start | bytes 65536 | tf_op jit(solution)/shard_map/all_to_all | solution.py:155
Sparse Core Ops, SparseCore 0:
  27.8 42.7 all-gather.1
  92.8 41.2 reduce-scatter.4
  153.3 40.7 reduce-scatter.6

commit v9 on v6

--- a/solution.py
+++ b/solution.py
@@ -19,8 +19,9 @@
 GY = ("zl", "x")
 
 
-def attention_kernel(cache_slots, key_rows, len_ref, q_ref, k_ref, v_ref, o_ref, m_sc, l_sc, acc_sc):
+def attention_kernel(cache_blocks, key_rows, len_ref, q_ref, kc_ref, vc_ref, kn_ref, vn_ref, o_ref, m_sc, l_sc, acc_sc):
     step = pl.program_id(0)
+    cache_slots = cache_blocks * key_rows
 
     @pl.when(step == 0)
     def _():
@@ -28,44 +29,51 @@
         l_sc[...] = jnp.zeros(l_sc.shape, jnp.float32)
         acc_sc[...] = jnp.zeros(acc_sc.shape, jnp.float32)
 
-    q = q_ref[...]
-    k = k_ref[...]
-    s = lax.dot_general(q, k, (((1,), (1,)), ((), ())), preferred_element_type=jnp.float32) * HEAD_DIM ** (-0.5)
-    rows = q.shape[0]
-    slot = step * key_rows + lax.broadcasted_iota(jnp.int32, (rows, key_rows), 1)
-    place = lax.broadcasted_iota(jnp.int32, (rows, key_rows), 0)
-    limit = jnp.where(slot < cache_slots, len_ref[0], cache_slots + place + 1)
-    allowed = slot < limit
-    s = jnp.where(allowed, s, NEG_FILL)
-    m_old = m_sc[...]
-    m_new = jnp.maximum(m_old, jnp.max(s, axis=1, keepdims=True))
-    p = jnp.where(allowed, jnp.exp(s - m_new), 0.0)
-    factor = jnp.exp(m_old - m_new)
-    l_sc[...] = l_sc[...] * factor + jnp.sum(p, axis=1, keepdims=True)
-    v = v_ref[...]
-    high = p.astype(jnp.bfloat16)
-    low = (p - high.astype(jnp.float32)).astype(jnp.bfloat16)
-    pv = jnp.dot(high, v, preferred_element_type=jnp.float32) + jnp.dot(low, v, preferred_element_type=jnp.float32)
-    acc_sc[...] = acc_sc[...] * factor + pv
-    m_sc[...] = m_new
+    def fold(k, v):
+        q = q_ref[...]
+        s = lax.dot_general(q, k, (((1,), (1,)), ((), ())), preferred_element_type=jnp.float32) * HEAD_DIM ** (-0.5)
+        rows = q.shape[0]
+        slot = step * key_rows + lax.broadcasted_iota(jnp.int32, (rows, key_rows), 1)
+        place = lax.broadcasted_iota(jnp.int32, (rows, key_rows), 0)
+        limit = jnp.where(slot < cache_slots, len_ref[0], cache_slots + place + 1)
+        allowed = slot < limit
+        s = jnp.where(allowed, s, NEG_FILL)
+        m_old = m_sc[...]
+        m_new = jnp.maximum(m_old, jnp.max(s, axis=1, keepdims=True))
+        p = jnp.where(allowed, jnp.exp(s - m_new), 0.0)
+        factor = jnp.exp(m_old - m_new)
+        l_sc[...] = l_sc[...] * factor + jnp.sum(p, axis=1, keepdims=True)
+        high = p.astype(jnp.bfloat16)
+        low = (p - high.astype(jnp.float32)).astype(jnp.bfloat16)
+        pv = jnp.dot(high, v, preferred_element_type=jnp.float32) + jnp.dot(low, v, preferred_element_type=jnp.float32)
+        acc_sc[...] = acc_sc[...] * factor + pv
+        m_sc[...] = m_new
 
-    @pl.when(step == pl.num_programs(0) - 1)
+    @pl.when(step < cache_blocks)
     def _():
+        fold(kc_ref[...], vc_ref[...])
+
+    @pl.when(step == cache_blocks)
+    def _():
+        fold(kn_ref[...], vn_ref[...])
         o_ref[...] = (acc_sc[...] / l_sc[...]).astype(o_ref.dtype)
 
 
-def attend(queries, keys, values, live_slots, cache_slots, key_rows=512):
+def attend(queries, cache_keys, cache_values, new_keys, new_values, live_slots):
     rows, width = queries.shape
-    steps = keys.shape[0] // key_rows
+    cache_blocks = cache_keys.shape[0] // rows
+    last = cache_blocks - 1
     return pl.pallas_call(
-        functools.partial(attention_kernel, cache_slots, key_rows),
+        functools.partial(attention_kernel, cache_blocks, rows),
         grid_spec=pltpu.PrefetchScalarGridSpec(
             num_scalar_prefetch=1,
-            grid=(steps,),
+            grid=(cache_blocks + 1,),
             in_specs=[
                 pl.BlockSpec((rows, width), lambda i, n: (0, 0)),
-                pl.BlockSpec((key_rows, width), lambda i, n: (i, 0)),
-                pl.BlockSpec((key_rows, width), lambda i, n: (i, 0)),
+                pl.BlockSpec((rows, width), lambda i, n: (jnp.minimum(i, last), 0)),
+                pl.BlockSpec((rows, width), lambda i, n: (jnp.minimum(i, last), 0)),
+                pl.BlockSpec((rows, width), lambda i, n: (0, 0)),
+                pl.BlockSpec((rows, width), lambda i, n: (0, 0)),
             ],
             out_specs=pl.BlockSpec((rows, width), lambda i, n: (0, 0)),
             scratch_shapes=[
@@ -76,7 +84,7 @@
         ),
         out_shape=jax.ShapeDtypeStruct((rows, width), jnp.bfloat16),
         compiler_params=pltpu.CompilerParams(dimension_semantics=("arbitrary",)),
-    )(live_slots, queries, keys, values)
+    )(live_slots, queries, cache_keys, cache_values, new_keys, new_values)
 
 
 def per_device(
@@ -123,9 +131,9 @@
     heads = []
     for h in range(head_count):
         cols = slice(h * HEAD_DIM, (h + 1) * HEAD_DIM)
-        keys_all = jnp.concatenate([cache_local[:, 0, cols], new_keys[:, h]], axis=0)
-        values_all = jnp.concatenate([cache_local[:, 1, cols], new_values[:, h]], axis=0)
-        heads.append(attend(queries[:, h], keys_all, values_all, live, cache_slots))
+        heads.append(attend(
+            queries[:, h], cache_local[:, 0, cols], cache_local[:, 1, cols], new_keys[:, h], new_values[:, h], live
+        ))
     attended = jnp.concatenate(heads, axis=1)
     partial_out = jnp.dot(attended, out_cols, preferred_element_type=jnp.float32).astype(jnp.bfloat16)
     branch = lax.psum_scatter(partial_out, ("y", "c"), scatter_dimension=1, tiled=True)

time: 203 us -> 202 us (level)
    unnamed x22 -> x18, local copies, waits for them, and re-layouts: 4.11 us -> 4.11 us
where the time goes in v9:
time: 202 us
  waiting for transfers between devices  74.4 us (37%)
  blocking collectives  49 us (24%)
  starting transfers between devices  27.2 us (13%)
  between operations  13.9 us (7%)
  local copies, waits for them, and re-layouts  13.8 us (7%)
  Pallas kernels  12.5 us (6%)
  matrix products  6.01 us (3%)
  other arithmetic  4.78 us (2%)
    all_gather x1, waiting for transfers between devices, per_device(): features = lax.all_gather(pair, ('y', 'c'), axis=1, tiled=True)  36.6 us
    all_to_all x1, blocking collectives, per_device(): last_terms = lax.all_to_all(last_term, GX, 0, 0, tiled=True)  28.6 us
    all_gather x1, blocking collectives, per_device(): pair = lax.all_gather(layer_input, 'zh', axis=1, tiled=True)  20.4 us
    all_to_all x1, waiting for transfers between devices, per_device(): packed = lax.all_to_all(packed, GX, 0, 0, tiled=True)  15.1 us
    all_to_all x1, starting transfers between devices, per_device(): stats = lax.all_to_all(spread, GY, 0, 0, tiled=True)  14 us
    pallas_call x1, Pallas kernels, attend(): pl.pallas_call(functools.partial(attention_kernel, cache_blocks, rows), g...  12.5 us
    unnamed x4, waiting for transfers between devices  11.3 us
    all_to_all x1, waiting for transfers between devices, per_device(): lax.all_to_all(jnp.broadcast_to(last_row[None], (n_gy, block_cols)), GY,...  11.3 us
  transfers between devices with their start and end apart: 6, of which 4 were waited for; matrix products, arithmetic and copies ran while one was open for 6% of the time, Pallas kernels for 0%

profile of v9, /device:TPU:1, one launch (start us, length us, event | category | flops | bytes accessed | tf_op | source)
XLA Modules:
  0.0 201.7 jit_solution(13016627407714885463)
XLA Ops:
  7.2 20.4 %all_gather.6 = bf16[512,256]{1,0:T(8,128)(2,1)} all-gather(bf16[512,128]{1,0:T(8,128)(2,1)} %param.7), channel_id=1, replica_groups=mesh['y'=4,'zh'=2,'c'=2,'zl'=8,'x'=4] {'zh'}, dimensions={1}, use_global_device_ids=true | all-gather | bytes 393216 | tf_op jit(solution)/shard_map/all_gather | solution.py:107
  27.7 2.9 %copy.51 = bf16[4,2,2,128,3,128]{5,3,2,1,0,4:T(8,128)(2,1)} copy(bf16[4,2,2,128,3,128]{5,3,1,2,0,4:T(8,128)(2,1)} %bitcast.51) | data formatting | bytes 3145728 | tf_op jit(solution)/shard_map/transpose | solution.py:110
  30.8 0.8 copy-done.4
  32.6 1.4 slice_bitcast_fusion
  33.9 36.6 %all-gather.2.cloned.1.call-done = bf16[512,2048]{1,0:T(8,128)(2,1)} async-done(((bf16[512,256]{1,0:T(8,128)(2,1)}), bf16[512,2048]{1,0:T(8,128)(2,1)}) %all-gather.2.cloned.1.call-update) | async-done | bytes 2097168 | tf_op jit(solution)/shard_map/all_gather | solution.py:108
  70.6 2.2 %fusion = f32[512]{0:T(512)S(1)} fusion(bf16[512,2048]{1,0:T(8,128)(2,1)} %all-gather.2.cloned.1.call-done), kind=kLoop, calls=%fused_computation.2 | loop fusion | flops 3145216 | bytes 2099200 | tf_op jit(solution)/shard_map/reduce_sum | solution.py:114
  72.8 2.7 %fusion.6 = bf16[512,3,128]{2,0,1:T(8,128)(2,1)S(1)} fusion(bf16[2048,3,128]{2,0,1:T(8,128)(2,1)} %bitcast.52, bf16[512,2048]{1,0:T(8,128)(2,1)S(1)} %copy-done.1, f32[512]{0:T(512)S(1)} %add_rsqrt_fusion), kind=kOutput, calls=%fused_computation.9 | convolution fusion | flops 808648704 | bytes 4065280 | tf_op jit(solution)/shard_map/td,dcf->tcf/dot_general | solution.py:116
  75.5 0.7 slice_bitcast_fusion.2
  76.3 12.5 %shard_map.102 = bf16[512,128]{1,0:T(8,128)(2,1)} custom-call(s32[1]{0:T(128)} %dynamic_slice.4.len_ref, bf16[512,128]{1,0:T(8,128)(2,1)} %get-tuple-element.50.q_ref, bf16[3584,128]{1,0:T(8,128)(2,1)} %get-tuple-element.47.kc_ref, bf16[3584,128]{1,0:T(8,128)(2,1)} %get-tuple-element.46.vc_ref, bf16[512,128]{1,0:T(8,128)(2,1)} %get-tuple-element.49.kn_ref, ...), custom_call_target="tpu_custom_call" | custom-call | tf_op jit(solution)/shard_map/pallas_call | solution.py:66
  88.8 3.0 %convolution_convert_fusion = bf16[512,2048]{1,0:T(8,128)(2,1)} fusion(bf16[512,128]{1,0:T(8,128)(2,1)} %shard_map.102, bf16[128,2048]{0,1:T(8,128)(2,1)S(1)} %bitcast.50), kind=kOutput, calls=%fused_computation.4 | convolution fusion | flops 269484032 | bytes 2752512 | tf_op jit(solution)/shard_map/dot_general | solution.py:138
  91.8 0.8 slice_reduce_fusion.2
  92.6 28.6 %all_to_all.29 = bf16[16,1,128]{2,1,0:T(2,128)(2,1)S(1)} all-to-all(bf16[16,1,128]{2,1,0:T(2,128)(2,1)S(1)} %copy.56), channel_id=1, replica_groups=mesh['y'=4,'zh'=2,'c'=2,'zl'=8,'x'=4] {'y','zh','c'}, dimensions={0} | all-to-all | bytes 8192 | tf_op jit(solution)/shard_map/all_to_all | solution.py:142
  121.9 5.0 %all-to-all-start.1 = ((bf16[32,1,128]{2,1,0:T(2,128)(2,1)}), bf16[32,1,128]{2,1,0:T(2,128)(2,1)S(1)}, u32[]{:S(2)}, u32[]{:S(2)}) async-start(bf16[32,1,128]{2,1,0:T(2,128)(2,1)} %broadcast_in_dim.6), calls=%async_computation.1 | async-start | bytes 32768 | tf_op jit(solution)/shard_map/all_to_all | solution.py:146
  126.9 11.3 %all-to-all-done.1 = bf16[32,1,128]{2,1,0:T(2,128)(2,1)S(1)} async-done(((bf16[32,1,128]{2,1,0:T(2,128)(2,1)}), bf16[32,1,128]{2,1,0:T(2,128)(2,1)S(1)}, u32[]{:S(2)}, u32[]{:S(2)}) %all-to-all-start.1) | async-done | bytes 8224 | tf_op jit(solution)/shard_map/all_to_all | solution.py:146
  138.9 0.9 all_to_all.22
  139.8 8.1 %all-to-all-start.2 = ((f32[16,2,2377]{2,1,0:T(2,128)}), f32[16,2,2377]{2,1,0:T(2,128)S(1)}, u32[]{:S(2)}, u32[]{:S(2)}) async-start(f32[16,2,2377]{2,1,0:T(2,128)} %all_to_all.22), calls=%async_computation.3 | async-start | bytes 622592 | tf_op jit(solution)/shard_map/all_to_all | solution.py:156
  147.9 1.8 copy.61
  149.7 15.1 %all-to-all-done.2 = f32[16,2,2377]{2,1,0:T(2,128)S(1)} async-done(((f32[16,2,2377]{2,1,0:T(2,128)}), f32[16,2,2377]{2,1,0:T(2,128)S(1)}, u32[]{:S(2)}, u32[]{:S(2)}) %all-to-all-start.2) | async-done | bytes 304288 | tf_op jit(solution)/shard_map/all_to_all | solution.py:156
  165.3 0.6 broadcast_in_dim.8
  166.0 14.0 %all-to-all-start.3 = ((f32[32,2,2]{2,1,0:T(2,128)}), f32[32,2,2]{2,1,0:T(2,128)S(1)}, u32[]{:S(2)}, u32[]{:S(2)}) async-start(f32[32,2,2]{2,1,0:T(2,128)} %broadcast_in_dim.8), calls=%async_computation.4 | async-start | bytes 65536 | tf_op jit(solution)/shard_map/all_to_all | solution.py:163
  180.0 1.0 copy.60
  181.0 11.3 %reduce-scatter.7.cloned.1.call-done = bf16[128,512]{1,0:T(8,128)(2,1)} async-done(((bf16[256,512]{1,0:T(8,128)(2,1)}), bf16[128,512]{1,0:T(8,128)(2,1)}) %reduce-scatter.7.cloned.1.call-update) | async-done | bytes 131088
  192.3 1.0 copy.62
  194.4 0.7 add_convert_fusion
  (44 shorter events, 4.3 us)
Async XLA Ops:
  7.2 131.3 %copy-start = (bf16[2376,128]{1,0:T(8,128)(2,1)S(1)}, bf16[2376,128]{1,0:T(8,128)(2,1)}, u32[]{:S(2)}) copy-start(bf16[2376,128]{1,0:T(8,128)(2,1)} %param.13) | copy-start | bytes 1824772
  7.2 63.4 %all-gather.2.cloned.1.call-start = ((), (), s32[]{:S(2)}) async-start(), calls=%async_computation.6 | async-start | bytes 2359296 | tf_op jit(solution)/shard_map/all_gather | solution.py:108
  27.6 111.3 %reduce-scatter.5.cloned.1.call-start = ((), (), s32[]{:S(2)}) async-start(), calls=%async_computation.7 | async-start | bytes 2359296 | tf_op jit(solution)/shard_map/reduce_scatter | solution.py:139
  27.7 2.9 %copy-start.2 = (bf16[1,3584,2,128]{3,2,1,0:T(2,128)(2,1)S(1)}, bf16[1,3584,2,128]{3,2,1,0:T(2,128)(2,1)}, u32[]{:S(2)}) copy-start(bf16[1,3584,2,128]{3,2,1,0:T(2,128)(2,1)} %param.10) | copy-start | bytes 5505028
  30.6 1.0 copy-start.4
  30.6 1.4 copy-start.5
  70.6 2.2 %copy-start.1 = (bf16[512,2048]{1,0:T(8,128)(2,1)S(1)}, bf16[512,2048]{1,0:T(8,128)(2,1)}, u32[]{:S(2)}) copy-start(bf16[512,2048]{1,0:T(8,128)(2,1)} %all-gather.2.cloned.1.call-done) | copy-start | bytes 6291460
  88.8 32.5 %copy-start.3 = (bf16[512,128]{1,0:T(8,128)(2,1)S(1)}, bf16[512,128]{1,0:T(8,128)(2,1)}, u32[]{:S(2)}) copy-start(bf16[512,128]{1,0:T(8,128)(2,1)} %param.7) | copy-start | bytes 393220
  88.8 38.1 %copy-start.6 = (bf16[128]{0:T(256)(128)(2,1)S(1)}, bf16[128]{0:T(256)(128)(2,1)}, u32[]{:S(2)}) copy-start(bf16[128]{0:T(256)(128)(2,1)} %param.12) | copy-start | bytes 772
  121.9 16.4 %all-to-all-start.1 = ((bf16[32,1,128]{2,1,0:T(2,128)(2,1)}), bf16[32,1,128]{2,1,0:T(2,128)(2,1)S(1)}, u32[]{:S(2)}, u32[]{:S(2)}) async-start(bf16[32,1,128]{2,1,0:T(2,128)(2,1)} %broadcast_in_dim.6), calls=%async_computation.1 | async-start | bytes 32768 | tf_op jit(solution)/shard_map/all_to_all | solution.py:146
  139.8 25.0 %all-to-all-start.2 = ((f32[16,2,2377]{2,1,0:T(2,128)}), f32[16,2,2377]{2,1,0:T(2,128)S(1)}, u32[]{:S(2)}, u32[]{:S(2)}) async-start(f32[16,2,2377]{2,1,0:T(2,128)} %all_to_all.22), calls=%async_computation.3 | async-start | bytes 622592 | tf_op jit(solution)/shard_map/all_to_all | solution.py:156
  147.8 44.5 %reduce-scatter.7.cloned.1.call-start = ((), (), s32[]{:S(2)}) async-start(), calls=%async_computation.8 | async-start | bytes 393216
  166.0 27.4 %all-to-all-start.3 = ((f32[32,2,2]{2,1,0:T(2,128)}), f32[32,2,2]{2,1,0:T(2,128)S(1)}, u32[]{:S(2)}, u32[]{:S(2)}) async-start(f32[32,2,2]{2,1,0:T(2,128)} %broadcast_in_dim.8), calls=%async_computation.4 | async-start | bytes 65536 | tf_op jit(solution)/shard_map/all_to_all | solution.py:163
Sparse Core Ops, SparseCore 0:
  27.8 42.7 all-gather.1
  91.9 40.2 reduce-scatter.4
  151.4 40.8 reduce-scatter.6

commit v10 on v9

--- a/solution.py
+++ b/solution.py
@@ -29,18 +29,19 @@
         l_sc[...] = jnp.zeros(l_sc.shape, jnp.float32)
         acc_sc[...] = jnp.zeros(acc_sc.shape, jnp.float32)
 
-    def fold(k, v):
+    def fold(k, v, limit):
         q = q_ref[...]
         s = lax.dot_general(q, k, (((1,), (1,)), ((), ())), preferred_element_type=jnp.float32) * HEAD_DIM ** (-0.5)
-        rows = q.shape[0]
-        slot = step * key_rows + lax.broadcasted_iota(jnp.int32, (rows, key_rows), 1)
-        place = lax.broadcasted_iota(jnp.int32, (rows, key_rows), 0)
-        limit = jnp.where(slot < cache_slots, len_ref[0], cache_slots + place + 1)
-        allowed = slot < limit
-        s = jnp.where(allowed, s, NEG_FILL)
+        if limit is not None:
+            rows = q.shape[0]
+            slot = step * key_rows + lax.broadcasted_iota(jnp.int32, (rows, key_rows), 1)
+            allowed = slot < limit(rows)
+            s = jnp.where(allowed, s, NEG_FILL)
         m_old = m_sc[...]
         m_new = jnp.maximum(m_old, jnp.max(s, axis=1, keepdims=True))
-        p = jnp.where(allowed, jnp.exp(s - m_new), 0.0)
+        p = jnp.exp(s - m_new)
+        if limit is not None:
+            p = jnp.where(allowed, p, 0.0)
         factor = jnp.exp(m_old - m_new)
         l_sc[...] = l_sc[...] * factor + jnp.sum(p, axis=1, keepdims=True)
         high = p.astype(jnp.bfloat16)
@@ -49,13 +50,25 @@
         acc_sc[...] = acc_sc[...] * factor + pv
         m_sc[...] = m_new
 
-    @pl.when(step < cache_blocks)
-    def _():
-        fold(kc_ref[...], vc_ref[...])
+    live = len_ref[0]
+    first_slot = step * key_rows
+    in_cache = step < cache_blocks
+
+    @pl.when(in_cache & (first_slot + key_rows <= live))
+    def _():
+        fold(kc_ref[...], vc_ref[...], None)
+
+    @pl.when(in_cache & (first_slot < live) & (first_slot + key_rows > live))
+    def _():
+        fold(kc_ref[...], vc_ref[...], lambda rows: live)
 
     @pl.when(step == cache_blocks)
     def _():
-        fold(kn_ref[...], vn_ref[...])
+        fold(
+            kn_ref[...],
+            vn_ref[...],
+            lambda rows: cache_slots + lax.broadcasted_iota(jnp.int32, (rows, key_rows), 0) + 1,
+        )
         o_ref[...] = (acc_sc[...] / l_sc[...]).astype(o_ref.dtype)
 
 

time: 202 us -> 201 us (level)
  no operation moved by 1% of the time
where the time goes in v10:
time: 201 us; the launch traced here: 200 us
  waiting for transfers between devices  74.5 us (37%)
  blocking collectives  49 us (24%)
  starting transfers between devices  27.1 us (13%)
  between operations  13.9 us (7%)
  local copies, waits for them, and re-layouts  13.8 us (7%)
  Pallas kernels  11 us (5%)
  matrix products  6.01 us (3%)
  other arithmetic  4.78 us (2%)
    all_gather x1, waiting for transfers between devices, per_device(): features = lax.all_gather(pair, ('y', 'c'), axis=1, tiled=True)  36.6 us
    all_to_all x1, blocking collectives, per_device(): last_terms = lax.all_to_all(last_term, GX, 0, 0, tiled=True)  28.6 us
    all_gather x1, blocking collectives, per_device(): pair = lax.all_gather(layer_input, 'zh', axis=1, tiled=True)  20.4 us
    all_to_all x1, waiting for transfers between devices, per_device(): packed = lax.all_to_all(packed, GX, 0, 0, tiled=True)  15.1 us
    all_to_all x1, starting transfers between devices, per_device(): stats = lax.all_to_all(spread, GY, 0, 0, tiled=True)  13.8 us
    unnamed x4, waiting for transfers between devices  11.4 us
    all_to_all x1, waiting for transfers between devices, per_device(): lax.all_to_all(jnp.broadcast_to(last_row[None], (n_gy, block_cols)), GY,...  11.3 us
    pallas_call x1, Pallas kernels, attend(): pl.pallas_call(functools.partial(attention_kernel, cache_blocks, rows), g...  11 us
  transfers between devices with their start and end apart: 6, of which 4 were waited for; matrix products, arithmetic and copies ran while one was open for 6% of the time, Pallas kernels for 0%

profile of v10, /device:TPU:1, one launch (start us, length us, event | category | flops | bytes accessed | tf_op | source)
XLA Modules:
  0.0 200.2 jit_solution(3783943233977010964)
XLA Ops:
  7.2 20.4 %all_gather.6 = bf16[512,256]{1,0:T(8,128)(2,1)} all-gather(bf16[512,128]{1,0:T(8,128)(2,1)} %param.7), channel_id=1, replica_groups=mesh['y'=4,'zh'=2,'c'=2,'zl'=8,'x'=4] {'zh'}, dimensions={1}, use_global_device_ids=true | all-gather | bytes 393216 | tf_op jit(solution)/shard_map/all_gather | solution.py:120
  27.7 2.9 %copy.51 = bf16[4,2,2,128,3,128]{5,3,2,1,0,4:T(8,128)(2,1)} copy(bf16[4,2,2,128,3,128]{5,3,1,2,0,4:T(8,128)(2,1)} %bitcast.51) | data formatting | bytes 3145728 | tf_op jit(solution)/shard_map/transpose | solution.py:123
  30.8 0.8 copy-done.4
  32.6 1.4 slice_bitcast_fusion
  33.9 36.6 %all-gather.2.cloned.1.call-done = bf16[512,2048]{1,0:T(8,128)(2,1)} async-done(((bf16[512,256]{1,0:T(8,128)(2,1)}), bf16[512,2048]{1,0:T(8,128)(2,1)}) %all-gather.2.cloned.1.call-update) | async-done | bytes 2097168 | tf_op jit(solution)/shard_map/all_gather | solution.py:121
  70.6 2.2 %fusion = f32[512]{0:T(512)S(1)} fusion(bf16[512,2048]{1,0:T(8,128)(2,1)} %all-gather.2.cloned.1.call-done), kind=kLoop, calls=%fused_computation.2 | loop fusion | flops 3145216 | bytes 2099200 | tf_op jit(solution)/shard_map/reduce_sum | solution.py:127
  72.8 2.7 %fusion.6 = bf16[512,3,128]{2,0,1:T(8,128)(2,1)S(1)} fusion(bf16[2048,3,128]{2,0,1:T(8,128)(2,1)} %bitcast.52, bf16[512,2048]{1,0:T(8,128)(2,1)S(1)} %copy-done.1, f32[512]{0:T(512)S(1)} %add_rsqrt_fusion), kind=kOutput, calls=%fused_computation.9 | convolution fusion | flops 808648704 | bytes 4065280 | tf_op jit(solution)/shard_map/td,dcf->tcf/dot_general | solution.py:129
  75.5 0.7 slice_bitcast_fusion.2
  76.3 11.0 %shard_map.102 = bf16[512,128]{1,0:T(8,128)(2,1)} custom-call(s32[1]{0:T(128)} %dynamic_slice.4.len_ref, bf16[512,128]{1,0:T(8,128)(2,1)} %get-tuple-element.50.q_ref, bf16[3584,128]{1,0:T(8,128)(2,1)} %get-tuple-element.47.kc_ref, bf16[3584,128]{1,0:T(8,128)(2,1)} %get-tuple-element.46.vc_ref, bf16[512,128]{1,0:T(8,128)(2,1)} %get-tuple-element.49.kn_ref, ...), custom_call_target="tpu_custom_call" | custom-call | tf_op jit(solution)/shard_map/pallas_call | solution.py:79
  87.3 3.0 %convolution_convert_fusion = bf16[512,2048]{1,0:T(8,128)(2,1)} fusion(bf16[512,128]{1,0:T(8,128)(2,1)} %shard_map.102, bf16[128,2048]{0,1:T(8,128)(2,1)S(1)} %bitcast.50), kind=kOutput, calls=%fused_computation.4 | convolution fusion | flops 269484032 | bytes 2752512 | tf_op jit(solution)/shard_map/dot_general | solution.py:151
  90.3 0.8 slice_reduce_fusion.2
  91.1 28.6 %all_to_all.29 = bf16[16,1,128]{2,1,0:T(2,128)(2,1)S(1)} all-to-all(bf16[16,1,128]{2,1,0:T(2,128)(2,1)S(1)} %copy.56), channel_id=1, replica_groups=mesh['y'=4,'zh'=2,'c'=2,'zl'=8,'x'=4] {'y','zh','c'}, dimensions={0} | all-to-all | bytes 8192 | tf_op jit(solution)/shard_map/all_to_all | solution.py:155
  120.4 6.3 %all-to-all-start.1 = ((bf16[32,1,128]{2,1,0:T(2,128)(2,1)}), bf16[32,1,128]{2,1,0:T(2,128)(2,1)S(1)}, u32[]{:S(2)}, u32[]{:S(2)}) async-start(bf16[32,1,128]{2,1,0:T(2,128)(2,1)} %broadcast_in_dim.6), calls=%async_computation.1 | async-start | bytes 32768 | tf_op jit(solution)/shard_map/all_to_all | solution.py:159
  126.7 11.3 %all-to-all-done.1 = bf16[32,1,128]{2,1,0:T(2,128)(2,1)S(1)} async-done(((bf16[32,1,128]{2,1,0:T(2,128)(2,1)}), bf16[32,1,128]{2,1,0:T(2,128)(2,1)S(1)}, u32[]{:S(2)}, u32[]{:S(2)}) %all-to-all-start.1) | async-done | bytes 8224 | tf_op jit(solution)/shard_map/all_to_all | solution.py:159
  138.7 0.9 all_to_all.22
  139.6 7.0 %all-to-all-start.2 = ((f32[16,2,2377]{2,1,0:T(2,128)}), f32[16,2,2377]{2,1,0:T(2,128)S(1)}, u32[]{:S(2)}, u32[]{:S(2)}) async-start(f32[16,2,2377]{2,1,0:T(2,128)} %all_to_all.22), calls=%async_computation.3 | async-start | bytes 622592 | tf_op jit(solution)/shard_map/all_to_all | solution.py:169
  146.6 1.8 copy.61
  148.4 15.1 %all-to-all-done.2 = f32[16,2,2377]{2,1,0:T(2,128)S(1)} async-done(((f32[16,2,2377]{2,1,0:T(2,128)}), f32[16,2,2377]{2,1,0:T(2,128)S(1)}, u32[]{:S(2)}, u32[]{:S(2)}) %all-to-all-start.2) | async-done | bytes 304288 | tf_op jit(solution)/shard_map/all_to_all | solution.py:169
  164.0 0.6 broadcast_in_dim.8
  164.7 13.8 %all-to-all-start.3 = ((f32[32,2,2]{2,1,0:T(2,128)}), f32[32,2,2]{2,1,0:T(2,128)S(1)}, u32[]{:S(2)}, u32[]{:S(2)}) async-start(f32[32,2,2]{2,1,0:T(2,128)} %broadcast_in_dim.8), calls=%async_computation.4 | async-start | bytes 65536 | tf_op jit(solution)/shard_map/all_to_all | solution.py:176
  178.5 1.0 copy.60
  179.4 11.4 %reduce-scatter.7.cloned.1.call-done = bf16[128,512]{1,0:T(8,128)(2,1)} async-done(((bf16[256,512]{1,0:T(8,128)(2,1)}), bf16[128,512]{1,0:T(8,128)(2,1)}) %reduce-scatter.7.cloned.1.call-update) | async-done | bytes 131088
  190.8 1.0 copy.62
  192.9 0.7 add_convert_fusion
  (44 shorter events, 4.3 us)
Async XLA Ops:
  7.2 131.1 %copy-start = (bf16[2376,128]{1,0:T(8,128)(2,1)S(1)}, bf16[2376,128]{1,0:T(8,128)(2,1)}, u32[]{:S(2)}) copy-start(bf16[2376,128]{1,0:T(8,128)(2,1)} %param.13) | copy-start | bytes 1824772
  7.2 63.4 %all-gather.2.cloned.1.call-start = ((), (), s32[]{:S(2)}) async-start(), calls=%async_computation.6 | async-start | bytes 2359296 | tf_op jit(solution)/shard_map/all_gather | solution.py:121
  27.6 111.0 %reduce-scatter.5.cloned.1.call-start = ((), (), s32[]{:S(2)}) async-start(), calls=%async_computation.7 | async-start | bytes 2359296 | tf_op jit(solution)/shard_map/reduce_scatter | solution.py:152
  27.7 2.9 %copy-start.2 = (bf16[1,3584,2,128]{3,2,1,0:T(2,128)(2,1)S(1)}, bf16[1,3584,2,128]{3,2,1,0:T(2,128)(2,1)}, u32[]{:S(2)}) copy-start(bf16[1,3584,2,128]{3,2,1,0:T(2,128)(2,1)} %param.10) | copy-start | bytes 5505028
  30.6 1.0 copy-start.4
  30.6 1.4 copy-start.5
  70.6 2.2 %copy-start.1 = (bf16[512,2048]{1,0:T(8,128)(2,1)S(1)}, bf16[512,2048]{1,0:T(8,128)(2,1)}, u32[]{:S(2)}) copy-start(bf16[512,2048]{1,0:T(8,128)(2,1)} %all-gather.2.cloned.1.call-done) | copy-start | bytes 6291460
  87.3 32.5 %copy-start.3 = (bf16[512,128]{1,0:T(8,128)(2,1)S(1)}, bf16[512,128]{1,0:T(8,128)(2,1)}, u32[]{:S(2)}) copy-start(bf16[512,128]{1,0:T(8,128)(2,1)} %param.7) | copy-start | bytes 393220
  87.3 39.4 %copy-start.6 = (bf16[128]{0:T(256)(128)(2,1)S(1)}, bf16[128]{0:T(256)(128)(2,1)}, u32[]{:S(2)}) copy-start(bf16[128]{0:T(256)(128)(2,1)} %param.12) | copy-start | bytes 772
  120.4 17.6 %all-to-all-start.1 = ((bf16[32,1,128]{2,1,0:T(2,128)(2,1)}), bf16[32,1,128]{2,1,0:T(2,128)(2,1)S(1)}, u32[]{:S(2)}, u32[]{:S(2)}) async-start(bf16[32,1,128]{2,1,0:T(2,128)(2,1)} %broadcast_in_dim.6), calls=%async_computation.1 | async-start | bytes 32768 | tf_op jit(solution)/shard_map/all_to_all | solution.py:159
  139.6 23.9 %all-to-all-start.2 = ((f32[16,2,2377]{2,1,0:T(2,128)}), f32[16,2,2377]{2,1,0:T(2,128)S(1)}, u32[]{:S(2)}, u32[]{:S(2)}) async-start(f32[16,2,2377]{2,1,0:T(2,128)} %all_to_all.22), calls=%async_computation.3 | async-start | bytes 622592 | tf_op jit(solution)/shard_map/all_to_all | solution.py:169
  146.5 44.3 %reduce-scatter.7.cloned.1.call-start = ((), (), s32[]{:S(2)}) async-start(), calls=%async_computation.8 | async-start | bytes 393216
  164.7 27.2 %all-to-all-start.3 = ((f32[32,2,2]{2,1,0:T(2,128)}), f32[32,2,2]{2,1,0:T(2,128)S(1)}, u32[]{:S(2)}, u32[]{:S(2)}) async-start(f32[32,2,2]{2,1,0:T(2,128)} %broadcast_in_dim.8), calls=%async_computation.4 | async-start | bytes 65536 | tf_op jit(solution)/shard_map/all_to_all | solution.py:176
Sparse Core Ops, SparseCore 0:
  27.8 42.7 all-gather.1
  90.4 40.2 reduce-scatter.4
  150.1 40.6 reduce-scatter.6

commit v11 on v10

--- a/solution.py
+++ b/solution.py
@@ -152,13 +152,13 @@
     branch = lax.psum_scatter(partial_out, ("y", "c"), scatter_dimension=1, tiled=True)
     last_term = partial_out[new_rows - 1].reshape(n_y, n_c, n_zh, block_cols)
     last_term = jnp.transpose(last_term, (0, 2, 1, 3)).reshape(n_gx, block_cols)
-    last_terms = lax.all_to_all(last_term, GX, 0, 0, tiled=True)
-    last_row = (
-        layer_input[new_rows - 1].astype(jnp.float32) + jnp.sum(last_terms.astype(jnp.float32), axis=0)
-    ).astype(jnp.bfloat16)
-    every_last = lax.all_to_all(
-        jnp.broadcast_to(last_row[None], (n_gy, block_cols)), GY, 0, 0, tiled=True
+    own_block = (lax.axis_index(GX) == jnp.arange(n_gx))[:, None]
+    terms = last_term.astype(jnp.float32) + jnp.where(
+        own_block, layer_input[new_rows - 1].astype(jnp.float32)[None], 0.0
     )
+    spread = jnp.broadcast_to(terms[:, None], (n_gx, n_gy, block_cols)).reshape(n_gx * n_gy, block_cols)
+    rows_in = lax.all_to_all(spread, GX + GY, 0, 0, tiled=True)
+    every_last = jnp.sum(rows_in.reshape(n_gx, n_gy, block_cols), axis=0).astype(jnp.bfloat16)
     last_wide = every_last.astype(jnp.float32)
     square_part = jnp.sum(last_wide * last_wide, axis=1, keepdims=True)
     gained = (last_wide * final_gain.astype(jnp.float32)).astype(jnp.bfloat16)

time: 201 us -> 202 us (level)
  blocking collectives: 49 us -> 20.4 us
  starting transfers between devices: 27.1 us -> 46.4 us
  waiting for transfers between devices: 74.5 us -> 87.8 us
  Pallas kernels: 11 us -> 8.42 us
    all_to_all x1 -> x0, blocking collectives: 28.6 us -> none  [per_device(): last_terms = lax.all_to_all(last_term, GX, 0, 0, tiled=True)]
    all_to_all x1, starting transfers between devices: 6.27 us -> 22.8 us  [per_device(): rows_in = lax.all_to_all(spread, GX + GY, 0, 0, tiled=True)]
    all_to_all x1, waiting for transfers between devices: 11.3 us -> 24.5 us  [per_device(): rows_in = lax.all_to_all(spread, GX + GY, 0, 0, tiled=True)]
    all_to_all x1, starting transfers between devices: 6.97 us -> 9.64 us  [per_device(): packed = lax.all_to_all(packed, GX, 0, 0, tiled=True)]
    pallas_call x1, Pallas kernels: 11 us -> 8.42 us  [attend(): pl.pallas_call(functools.partial(attention_kernel, cache_blocks, rows), g...]
where the time goes in v11:
time: 202 us
  waiting for transfers between devices  87.8 us (43%)
  starting transfers between devices  46.4 us (23%)
  blocking collectives  20.4 us (10%)
  between operations  13.9 us (7%)
  local copies, waits for them, and re-layouts  13.1 us (6%)
  Pallas kernels  8.42 us (4%)
  matrix products  6.01 us (3%)
  other arithmetic  5.6 us (3%)
    all_gather x1, waiting for transfers between devices, per_device(): features = lax.all_gather(pair, ('y', 'c'), axis=1, tiled=True)  36.6 us
    all_to_all x1, waiting for transfers between devices, per_device(): rows_in = lax.all_to_all(spread, GX + GY, 0, 0, tiled=True)  24.5 us
    all_to_all x1, starting transfers between devices, per_device(): rows_in = lax.all_to_all(spread, GX + GY, 0, 0, tiled=True)  22.8 us
    all_gather x1, blocking collectives, per_device(): pair = lax.all_gather(layer_input, 'zh', axis=1, tiled=True)  20.4 us
    all_to_all x1, waiting for transfers between devices, per_device(): packed = lax.all_to_all(packed, GX, 0, 0, tiled=True)  15.1 us
    all_to_all x1, starting transfers between devices, per_device(): stats = lax.all_to_all(spread, GY, 0, 0, tiled=True)  13.8 us
    unnamed x4, waiting for transfers between devices  11.5 us
    all_to_all x1, starting transfers between devices, per_device(): packed = lax.all_to_all(packed, GX, 0, 0, tiled=True)  9.64 us
  transfers between devices with their start and end apart: 6, of which 4 were waited for; matrix products, arithmetic and copies ran while one was open for 6% of the time, Pallas kernels for 0%

profile of v11, /device:TPU:1, one launch (start us, length us, event | category | flops | bytes accessed | tf_op | source)
XLA Modules:
  0.0 201.6 jit_solution(15137894848057835235)
XLA Ops:
  7.2 20.4 %all_gather.6 = bf16[512,256]{1,0:T(8,128)(2,1)} all-gather(bf16[512,128]{1,0:T(8,128)(2,1)} %param.7), channel_id=1, replica_groups=mesh['y'=4,'zh'=2,'c'=2,'zl'=8,'x'=4] {'zh'}, dimensions={1}, use_global_device_ids=true | all-gather | bytes 393216 | tf_op jit(solution)/shard_map/all_gather | solution.py:120
  27.7 2.9 %copy.48 = bf16[4,2,2,128,3,128]{5,3,2,1,0,4:T(8,128)(2,1)} copy(bf16[4,2,2,128,3,128]{5,3,1,2,0,4:T(8,128)(2,1)} %bitcast.49) | data formatting | bytes 3145728 | tf_op jit(solution)/shard_map/transpose | solution.py:123
  30.8 0.8 copy-done.4
  32.6 1.4 slice_bitcast_fusion
  33.9 36.6 %all-gather.2.cloned.1.call-done = bf16[512,2048]{1,0:T(8,128)(2,1)} async-done(((bf16[512,256]{1,0:T(8,128)(2,1)}), bf16[512,2048]{1,0:T(8,128)(2,1)}) %all-gather.2.cloned.1.call-update) | async-done | bytes 2097168 | tf_op jit(solution)/shard_map/all_gather | solution.py:121
  70.6 2.2 %fusion = f32[512]{0:T(512)S(1)} fusion(bf16[512,2048]{1,0:T(8,128)(2,1)} %all-gather.2.cloned.1.call-done), kind=kLoop, calls=%fused_computation.2 | loop fusion | flops 3145216 | bytes 2099200 | tf_op jit(solution)/shard_map/reduce_sum | solution.py:127
  72.8 2.7 %fusion.6 = bf16[512,3,128]{2,0,1:T(8,128)(2,1)S(1)} fusion(bf16[2048,3,128]{2,0,1:T(8,128)(2,1)} %bitcast.50, bf16[512,2048]{1,0:T(8,128)(2,1)S(1)} %copy-done.1, f32[512]{0:T(512)S(1)} %add_rsqrt_fusion), kind=kOutput, calls=%fused_computation.9 | convolution fusion | flops 808648704 | bytes 4065280 | tf_op jit(solution)/shard_map/td,dcf->tcf/dot_general | solution.py:129
  75.5 0.7 slice_bitcast_fusion.2
  76.3 8.4 %shard_map.102 = bf16[512,128]{1,0:T(8,128)(2,1)} custom-call(s32[1]{0:T(128)} %dynamic_slice.4.len_ref, bf16[512,128]{1,0:T(8,128)(2,1)} %get-tuple-element.50.q_ref, bf16[3584,128]{1,0:T(8,128)(2,1)} %get-tuple-element.47.kc_ref, bf16[3584,128]{1,0:T(8,128)(2,1)} %get-tuple-element.46.vc_ref, bf16[512,128]{1,0:T(8,128)(2,1)} %get-tuple-element.49.kn_ref, ...), custom_call_target="tpu_custom_call" | custom-call | tf_op jit(solution)/shard_map/pallas_call | solution.py:79
  84.7 3.0 %convolution_convert_fusion = bf16[512,2048]{1,0:T(8,128)(2,1)} fusion(bf16[512,128]{1,0:T(8,128)(2,1)} %shard_map.102, bf16[128,2048]{0,1:T(8,128)(2,1)S(1)} %bitcast.48), kind=kOutput, calls=%fused_computation.4 | convolution fusion | flops 269484032 | bytes 2752512 | tf_op jit(solution)/shard_map/dot_general | solution.py:151
  87.8 0.8 slice_convert_fusion
  88.6 0.7 broadcast_in_dim.48
  89.3 22.8 %all-to-all-start = ((f32[512,1,128]{2,1,0:T(1,128)}), f32[512,1,128]{2,1,0:T(1,128)S(1)}, u32[]{:S(2)}, u32[]{:S(2)}) async-start(f32[512,1,128]{2,1,0:T(1,128)} %bitcast.17), calls=%async_computation | async-start | bytes 524288 | tf_op jit(solution)/shard_map/all_to_all | solution.py:160
  112.2 24.5 %all-to-all-done = f32[512,1,128]{2,1,0:T(1,128)S(1)} async-done(((f32[512,1,128]{2,1,0:T(1,128)}), f32[512,1,128]{2,1,0:T(1,128)S(1)}, u32[]{:S(2)}, u32[]{:S(2)}) %all-to-all-start) | async-done | bytes 262176 | tf_op jit(solution)/shard_map/all_to_all | solution.py:160
  137.3 0.9 all_to_all.17
  138.2 9.6 %all-to-all-start.1 = ((f32[16,2,2377]{2,1,0:T(2,128)}), f32[16,2,2377]{2,1,0:T(2,128)S(1)}, u32[]{:S(2)}, u32[]{:S(2)}) async-start(f32[16,2,2377]{2,1,0:T(2,128)} %all_to_all.17), calls=%async_computation.2 | async-start | bytes 622592 | tf_op jit(solution)/shard_map/all_to_all | solution.py:169
  147.9 1.8 copy.57
  149.7 15.1 %all-to-all-done.1 = f32[16,2,2377]{2,1,0:T(2,128)S(1)} async-done(((f32[16,2,2377]{2,1,0:T(2,128)}), f32[16,2,2377]{2,1,0:T(2,128)S(1)}, u32[]{:S(2)}, u32[]{:S(2)}) %all-to-all-start.1) | async-done | bytes 304288 | tf_op jit(solution)/shard_map/all_to_all | solution.py:169
  165.3 0.6 broadcast_in_dim.50
  166.0 13.8 %all-to-all-start.2 = ((f32[32,2,2]{2,1,0:T(2,128)}), f32[32,2,2]{2,1,0:T(2,128)S(1)}, u32[]{:S(2)}, u32[]{:S(2)}) async-start(f32[32,2,2]{2,1,0:T(2,128)} %broadcast_in_dim.50), calls=%async_computation.3 | async-start | bytes 65536 | tf_op jit(solution)/shard_map/all_to_all | solution.py:176
  179.8 1.0 copy.56
  180.8 11.5 %reduce-scatter.7.cloned.1.call-done = bf16[128,512]{1,0:T(8,128)(2,1)} async-done(((bf16[256,512]{1,0:T(8,128)(2,1)}), bf16[128,512]{1,0:T(8,128)(2,1)}) %reduce-scatter.7.cloned.1.call-update) | async-done | bytes 131088
  192.2 1.0 copy.58
  194.4 0.7 add_convert_fusion
  (43 shorter events, 3.7 us)
Async XLA Ops:
  7.2 129.8 %copy-start = (bf16[2376,128]{1,0:T(8,128)(2,1)S(1)}, bf16[2376,128]{1,0:T(8,128)(2,1)}, u32[]{:S(2)}) copy-start(bf16[2376,128]{1,0:T(8,128)(2,1)} %param.13) | copy-start | bytes 1824772
  7.2 63.4 %all-gather.2.cloned.1.call-start = ((), (), s32[]{:S(2)}) async-start(), calls=%async_computation.5 | async-start | bytes 2359296 | tf_op jit(solution)/shard_map/all_gather | solution.py:121
  27.6 109.7 %reduce-scatter.5.cloned.1.call-start = ((), (), s32[]{:S(2)}) async-start(), calls=%async_computation.6 | async-start | bytes 2359296 | tf_op jit(solution)/shard_map/reduce_scatter | solution.py:152
  27.7 2.9 %copy-start.2 = (bf16[1,3584,2,128]{3,2,1,0:T(2,128)(2,1)S(1)}, bf16[1,3584,2,128]{3,2,1,0:T(2,128)(2,1)}, u32[]{:S(2)}) copy-start(bf16[1,3584,2,128]{3,2,1,0:T(2,128)(2,1)} %param.10) | copy-start | bytes 5505028
  30.6 1.0 copy-start.4
  30.6 1.4 copy-start.5
  70.6 2.2 %copy-start.1 = (bf16[512,2048]{1,0:T(8,128)(2,1)S(1)}, bf16[512,2048]{1,0:T(8,128)(2,1)}, u32[]{:S(2)}) copy-start(bf16[512,2048]{1,0:T(8,128)(2,1)} %all-gather.2.cloned.1.call-done) | copy-start | bytes 6291460
  84.7 3.1 %copy-start.3 = (bf16[512,128]{1,0:T(8,128)(2,1)S(1)}, bf16[512,128]{1,0:T(8,128)(2,1)}, u32[]{:S(2)}) copy-start(bf16[512,128]{1,0:T(8,128)(2,1)} %param.7) | copy-start | bytes 393220
  87.7 24.5 %copy-start.6 = (bf16[128]{0:T(256)(128)(2,1)S(1)}, bf16[128]{0:T(256)(128)(2,1)}, u32[]{:S(2)}) copy-start(bf16[128]{0:T(256)(128)(2,1)} %param.12) | copy-start | bytes 772
  89.3 47.4 %all-to-all-start = ((f32[512,1,128]{2,1,0:T(1,128)}), f32[512,1,128]{2,1,0:T(1,128)S(1)}, u32[]{:S(2)}, u32[]{:S(2)}) async-start(f32[512,1,128]{2,1,0:T(1,128)} %bitcast.17), calls=%async_computation | async-start | bytes 524288 | tf_op jit(solution)/shard_map/all_to_all | solution.py:160
  138.2 26.6 %all-to-all-start.1 = ((f32[16,2,2377]{2,1,0:T(2,128)}), f32[16,2,2377]{2,1,0:T(2,128)S(1)}, u32[]{:S(2)}, u32[]{:S(2)}) async-start(f32[16,2,2377]{2,1,0:T(2,128)} %all_to_all.17), calls=%async_computation.2 | async-start | bytes 622592 | tf_op jit(solution)/shard_map/all_to_all | solution.py:169
  147.9 44.4 %reduce-scatter.7.cloned.1.call-start = ((), (), s32[]{:S(2)}) async-start(), calls=%async_computation.7 | async-start | bytes 393216
  166.0 27.3 %all-to-all-start.2 = ((f32[32,2,2]{2,1,0:T(2,128)}), f32[32,2,2]{2,1,0:T(2,128)S(1)}, u32[]{:S(2)}, u32[]{:S(2)}) async-start(f32[32,2,2]{2,1,0:T(2,128)} %broadcast_in_dim.50), calls=%async_computation.3 | async-start | bytes 65536 | tf_op jit(solution)/shard_map/all_to_all | solution.py:176
Sparse Core Ops, SparseCore 0:
  27.8 42.7 all-gather.1
  87.8 44.4 reduce-scatter.4
  151.5 40.7 reduce-scatter.6

commit v12 on v10

--- a/solution.py
+++ b/solution.py
@@ -117,10 +117,10 @@
     request = lax.axis_index("zl") * lax.axis_size("x") + lax.axis_index("x")
     own_len = lax.dynamic_index_in_dim(cached_lengths, request, 0, keepdims=False)
 
-    pair = lax.all_gather(layer_input, "zh", axis=1, tiled=True)
-    features = lax.all_gather(pair, ("y", "c"), axis=1, tiled=True)
+    half = lax.all_gather(layer_input, ("y", "c"), axis=1, tiled=True)
+    features = lax.all_gather(half, "zh", axis=1, tiled=True)
     weight_rows = project_weight.reshape(n_y, n_zh, n_c, block_cols, 3, project_weight.shape[-1])
-    weight_rows = jnp.transpose(weight_rows, (0, 2, 1, 3, 4, 5)).reshape(project_weight.shape)
+    weight_rows = jnp.transpose(weight_rows, (1, 0, 2, 3, 4, 5)).reshape(project_weight.shape)
 
     widened = features.astype(jnp.float32)
     normed = (

time: 201 us -> 293 us (1.46)
  waiting for transfers between devices: 74.5 us -> 184 us
  blocking collectives: 49 us -> 28.7 us
    all_gather x1 -> x2, waiting for transfers between devices: 36.6 us -> 146 us  [the longest x1 107 us: per_device(): features = lax.all_gather(half, 'zh', axis=1, tiled=True)]
    all_gather x1 -> x0, blocking collectives: 20.4 us -> none  [per_device(): pair = lax.all_gather(layer_input, 'zh', axis=1, tiled=True)]
    all_to_all x1, starting transfers between devices: 6.27 us -> 10.3 us  [per_device(): lax.all_to_all(jnp.broadcast_to(last_row[None], (n_gy, block_cols)), GY,...]
    unnamed x4 -> x5, waiting for transfers between devices: 11.4 us -> 11.5 us
  transfers between devices with their start and end apart: 6 -> 7, of which waited for: 4 -> 5; matrix products, arithmetic and copies ran while one was open for 6% -> 5% of each run, Pallas kernels for 0% -> 0%
where the time goes in v12:
time: 293 us; the launch traced here: 292 us
  waiting for transfers between devices  184 us (63%)
  blocking collectives  28.7 us (10%)
  starting transfers between devices  28.2 us (10%)
  local copies, waits for them, and re-layouts  14.4 us (5%)
  between operations  13.9 us (5%)
  Pallas kernels  12.4 us (4%)
  matrix products  6.02 us (2%)
  other arithmetic  4.78 us (2%)
    all_gather x1, waiting for transfers between devices, per_device(): features = lax.all_gather(half, 'zh', axis=1, tiled=True)  107 us
    all_gather x1, waiting for transfers between devices, per_device(): half = lax.all_gather(layer_input, ('y', 'c'), axis=1, tiled=True)  39 us
    all_to_all x1, blocking collectives, per_device(): last_terms = lax.all_to_all(last_term, GX, 0, 0, tiled=True)  28.7 us
    all_to_all x1, waiting for transfers between devices, per_device(): packed = lax.all_to_all(packed, GX, 0, 0, tiled=True)  15.3 us
    pallas_call x1, Pallas kernels, attend(): pl.pallas_call(functools.partial(attention_kernel, cache_blocks, rows), g...  12.4 us
    all_to_all x1, starting transfers between devices, per_device(): stats = lax.all_to_all(spread, GY, 0, 0, tiled=True)  12.4 us
    unnamed x5, waiting for transfers between devices  11.5 us
    all_to_all x1, waiting for transfers between devices, per_device(): lax.all_to_all(jnp.broadcast_to(last_row[None], (n_gy, block_cols)), GY,...  11.3 us
  transfers between devices with their start and end apart: 7, of which 5 were waited for; matrix products, arithmetic and copies ran while one was open for 5% of the time, Pallas kernels for 0%

profile of v12, /device:TPU:1, one launch (start us, length us, event | category | flops | bytes accessed | tf_op | source)
XLA Modules:
  0.0 292.2 jit_solution(7972490822556565627)
XLA Ops:
  7.2 0.7 all-gather.3.cloned.1.call-update
  8.0 39.0 %all-gather.3.cloned.1.call-done = bf16[512,1024]{1,0:T(8,128)(2,1)} async-done(((bf16[512,128]{1,0:T(8,128)(2,1)}), bf16[512,1024]{1,0:T(8,128)(2,1)}) %all-gather.3.cloned.1.call-update) | async-done | bytes 1048592 | tf_op jit(solution)/shard_map/all_gather | solution.py:120
  47.0 2.7 copy.51
  49.7 1.8 copy.66
  52.5 1.4 slice_bitcast_fusion
  53.9 106.7 %all-gather.5.cloned.1.call-done = bf16[512,2048]{1,0:T(8,128)(2,1)} async-done(((bf16[512,1024]{1,0:T(8,128)(2,1)}), bf16[512,2048]{1,0:T(8,128)(2,1)}) %all-gather.5.cloned.1.call-update) | async-done | bytes 2097168 | tf_op jit(solution)/shard_map/all_gather | solution.py:121
  160.5 2.2 fusion
  162.8 2.7 fusion.6
  165.5 0.7 slice_bitcast_fusion.2
  166.2 12.4 %shard_map.102 = bf16[512,128]{1,0:T(8,128)(2,1)} custom-call(s32[1]{0:T(128)} %dynamic_slice.4.len_ref, bf16[512,128]{1,0:T(8,128)(2,1)} %get-tuple-element.50.q_ref, bf16[3584,128]{1,0:T(8,128)(2,1)} %get-tuple-element.47.kc_ref, bf16[3584,128]{1,0:T(8,128)(2,1)} %get-tuple-element.46.vc_ref, bf16[512,128]{1,0:T(8,128)(2,1)} %get-tuple-element.49.kn_ref, ...), custom_call_target="tpu_custom_call" | custom-call | tf_op jit(solution)/shard_map/pallas_call | solution.py:79
  178.6 3.0 %convolution_convert_fusion = bf16[512,2048]{1,0:T(8,128)(2,1)} fusion(bf16[512,128]{1,0:T(8,128)(2,1)} %shard_map.102, bf16[128,2048]{0,1:T(8,128)(2,1)S(1)} %bitcast.50), kind=kOutput, calls=%fused_computation.4 | convolution fusion | flops 269484032 | bytes 2752512 | tf_op jit(solution)/shard_map/dot_general | solution.py:151
  181.6 0.8 slice_reduce_fusion.2
  182.5 28.7 %all_to_all.29 = bf16[16,1,128]{2,1,0:T(2,128)(2,1)S(1)} all-to-all(bf16[16,1,128]{2,1,0:T(2,128)(2,1)S(1)} %copy.56), channel_id=1, replica_groups=mesh['y'=4,'zh'=2,'c'=2,'zl'=8,'x'=4] {'y','zh','c'}, dimensions={0} | all-to-all | bytes 8192 | tf_op jit(solution)/shard_map/all_to_all | solution.py:155
  211.8 10.3 %all-to-all-start.1 = ((bf16[32,1,128]{2,1,0:T(2,128)(2,1)}), bf16[32,1,128]{2,1,0:T(2,128)(2,1)S(1)}, u32[]{:S(2)}, u32[]{:S(2)}) async-start(bf16[32,1,128]{2,1,0:T(2,128)(2,1)} %broadcast_in_dim.6), calls=%async_computation.1 | async-start | bytes 32768 | tf_op jit(solution)/shard_map/all_to_all | solution.py:159
  222.1 11.3 %all-to-all-done.1 = bf16[32,1,128]{2,1,0:T(2,128)(2,1)S(1)} async-done(((bf16[32,1,128]{2,1,0:T(2,128)(2,1)}), bf16[32,1,128]{2,1,0:T(2,128)(2,1)S(1)}, u32[]{:S(2)}, u32[]{:S(2)}) %all-to-all-start.1) | async-done | bytes 8224 | tf_op jit(solution)/shard_map/all_to_all | solution.py:159
  234.1 0.9 all_to_all.22
  235.0 5.4 %all-to-all-start.2 = ((f32[16,2,2377]{2,1,0:T(2,128)}), f32[16,2,2377]{2,1,0:T(2,128)S(1)}, u32[]{:S(2)}, u32[]{:S(2)}) async-start(f32[16,2,2377]{2,1,0:T(2,128)} %all_to_all.22), calls=%async_computation.3 | async-start | bytes 622592 | tf_op jit(solution)/shard_map/all_to_all | solution.py:169
  240.5 1.8 copy.61
  242.3 15.3 %all-to-all-done.2 = f32[16,2,2377]{2,1,0:T(2,128)S(1)} async-done(((f32[16,2,2377]{2,1,0:T(2,128)}), f32[16,2,2377]{2,1,0:T(2,128)S(1)}, u32[]{:S(2)}, u32[]{:S(2)}) %all-to-all-start.2) | async-done | bytes 304288 | tf_op jit(solution)/shard_map/all_to_all | solution.py:169
  258.7 12.4 %all-to-all-start.3 = ((f32[32,2,2]{2,1,0:T(2,128)}), f32[32,2,2]{2,1,0:T(2,128)S(1)}, u32[]{:S(2)}, u32[]{:S(2)}) async-start(f32[32,2,2]{2,1,0:T(2,128)} %broadcast_in_dim.8), calls=%async_computation.4 | async-start | bytes 65536 | tf_op jit(solution)/shard_map/all_to_all | solution.py:176
  271.1 1.0 copy.60
  272.1 10.8 %reduce-scatter.7.cloned.1.call-done = bf16[128,512]{1,0:T(8,128)(2,1)} async-done(((bf16[256,512]{1,0:T(8,128)(2,1)}), bf16[128,512]{1,0:T(8,128)(2,1)}) %reduce-scatter.7.cloned.1.call-update) | async-done | bytes 131088
  282.9 1.0 copy.62
  285.0 0.7 add_convert_fusion
  (44 shorter events, 4.7 us)
Async XLA Ops:
  7.2 226.5 %copy-start = (bf16[2376,128]{1,0:T(8,128)(2,1)S(1)}, bf16[2376,128]{1,0:T(8,128)(2,1)}, u32[]{:S(2)}) copy-start(bf16[2376,128]{1,0:T(8,128)(2,1)} %param.13) | copy-start | bytes 1824772
  7.2 39.7 %all-gather.3.cloned.1.call-start = ((), (), s32[]{:S(2)}) async-start(), calls=%async_computation.6 | async-start | bytes 1179648 | tf_op jit(solution)/shard_map/all_gather | solution.py:120
  7.9 152.6 %all-gather.5.cloned.1.call-start = ((), (), s32[]{:S(2)}) async-start(), calls=%async_computation.7 | async-start | bytes 3145728 | tf_op jit(solution)/shard_map/all_gather | solution.py:121
  47.0 187.1 %reduce-scatter.5.cloned.1.call-start = ((), (), s32[]{:S(2)}) async-start(), calls=%async_computation.8 | async-start | bytes 2359296 | tf_op jit(solution)/shard_map/reduce_scatter | solution.py:152
  49.7 1.8 copy-start.3
  49.7 2.1 copy-start.4
  160.5 2.2 copy-start.1
  178.6 32.6 %copy-start.2 = (bf16[512,128]{1,0:T(8,128)(2,1)S(1)}, bf16[512,128]{1,0:T(8,128)(2,1)}, u32[]{:S(2)}) copy-start(bf16[512,128]{1,0:T(8,128)(2,1)} %param.7) | copy-start | bytes 393220
  178.6 43.5 %copy-start.5 = (bf16[128]{0:T(256)(128)(2,1)S(1)}, bf16[128]{0:T(256)(128)(2,1)}, u32[]{:S(2)}) copy-start(bf16[128]{0:T(256)(128)(2,1)} %param.12) | copy-start | bytes 772
  211.8 21.6 %all-to-all-start.1 = ((bf16[32,1,128]{2,1,0:T(2,128)(2,1)}), bf16[32,1,128]{2,1,0:T(2,128)(2,1)S(1)}, u32[]{:S(2)}, u32[]{:S(2)}) async-start(bf16[32,1,128]{2,1,0:T(2,128)(2,1)} %broadcast_in_dim.6), calls=%async_computation.1 | async-start | bytes 32768 | tf_op jit(solution)/shard_map/all_to_all | solution.py:159
  235.0 22.6 %all-to-all-start.2 = ((f32[16,2,2377]{2,1,0:T(2,128)}), f32[16,2,2377]{2,1,0:T(2,128)S(1)}, u32[]{:S(2)}, u32[]{:S(2)}) async-start(f32[16,2,2377]{2,1,0:T(2,128)} %all_to_all.22), calls=%async_computation.3 | async-start | bytes 622592 | tf_op jit(solution)/shard_map/all_to_all | solution.py:169
  240.4 42.5 %reduce-scatter.7.cloned.1.call-start = ((), (), s32[]{:S(2)}) async-start(), calls=%async_computation.9 | async-start | bytes 393216
  258.7 25.2 %all-to-all-start.3 = ((f32[32,2,2]{2,1,0:T(2,128)}), f32[32,2,2]{2,1,0:T(2,128)S(1)}, u32[]{:S(2)}, u32[]{:S(2)}) async-start(f32[32,2,2]{2,1,0:T(2,128)} %broadcast_in_dim.8), calls=%async_computation.4 | async-start | bytes 65536 | tf_op jit(solution)/shard_map/all_to_all | solution.py:176
Sparse Core Ops, SparseCore 0:
  10.1 36.7 all-gather.2
  49.0 111.4 all-gather.4
  181.8 40.7 reduce-scatter.4
  243.7 39.1 reduce-scatter.6

commit v13 on v10

--- a/solution.py
+++ b/solution.py
@@ -19,7 +19,7 @@
 GY = ("zl", "x")
 
 
-def attention_kernel(cache_blocks, key_rows, len_ref, q_ref, kc_ref, vc_ref, kn_ref, vn_ref, o_ref, m_sc, l_sc, acc_sc):
+def attention_kernel(cache_blocks, key_rows, new_rows, len_ref, q_ref, kc_ref, vc_ref, kn_ref, vn_ref, o_ref, m_sc, l_sc, acc_sc):
     step = pl.program_id(0)
     cache_slots = cache_blocks * key_rows
 
@@ -33,9 +33,9 @@
         q = q_ref[...]
         s = lax.dot_general(q, k, (((1,), (1,)), ((), ())), preferred_element_type=jnp.float32) * HEAD_DIM ** (-0.5)
         if limit is not None:
-            rows = q.shape[0]
-            slot = step * key_rows + lax.broadcasted_iota(jnp.int32, (rows, key_rows), 1)
-            allowed = slot < limit(rows)
+            rows, width = s.shape
+            slot = step * key_rows + lax.broadcasted_iota(jnp.int32, (rows, width), 1)
+            allowed = slot < limit(rows, width)
             s = jnp.where(allowed, s, NEG_FILL)
         m_old = m_sc[...]
         m_new = jnp.maximum(m_old, jnp.max(s, axis=1, keepdims=True))
@@ -60,31 +60,32 @@
 
     @pl.when(in_cache & (first_slot < live) & (first_slot + key_rows > live))
     def _():
-        fold(kc_ref[...], vc_ref[...], lambda rows: live)
+        fold(kc_ref[...], vc_ref[...], lambda rows, width: live)
 
     @pl.when(step == cache_blocks)
     def _():
         fold(
             kn_ref[...],
             vn_ref[...],
-            lambda rows: cache_slots + lax.broadcasted_iota(jnp.int32, (rows, key_rows), 0) + 1,
+            lambda rows, width: cache_slots + lax.broadcasted_iota(jnp.int32, (rows, width), 0) + 1,
         )
         o_ref[...] = (acc_sc[...] / l_sc[...]).astype(o_ref.dtype)
 
 
 def attend(queries, cache_keys, cache_values, new_keys, new_values, live_slots):
     rows, width = queries.shape
-    cache_blocks = cache_keys.shape[0] // rows
+    key_rows = cache_keys.shape[0] // 4 if cache_keys.shape[0] % (4 * 128) == 0 else rows
+    cache_blocks = cache_keys.shape[0] // key_rows
     last = cache_blocks - 1
     return pl.pallas_call(
-        functools.partial(attention_kernel, cache_blocks, rows),
+        functools.partial(attention_kernel, cache_blocks, key_rows, rows),
         grid_spec=pltpu.PrefetchScalarGridSpec(
             num_scalar_prefetch=1,
             grid=(cache_blocks + 1,),
             in_specs=[
                 pl.BlockSpec((rows, width), lambda i, n: (0, 0)),
-                pl.BlockSpec((rows, width), lambda i, n: (jnp.minimum(i, last), 0)),
-                pl.BlockSpec((rows, width), lambda i, n: (jnp.minimum(i, last), 0)),
+                pl.BlockSpec((key_rows, width), lambda i, n: (jnp.minimum(i, last), 0)),
+                pl.BlockSpec((key_rows, width), lambda i, n: (jnp.minimum(i, last), 0)),
                 pl.BlockSpec((rows, width), lambda i, n: (0, 0)),
                 pl.BlockSpec((rows, width), lambda i, n: (0, 0)),
             ],

time: 201 us -> 199 us (0.990)
  Pallas kernels: 11 us -> 8.4 us
    pallas_call x1, Pallas kernels: 11 us -> 8.4 us  [attend(): pl.pallas_call(functools.partial(attention_kernel, cache_blocks, key_rows...]
where the time goes in v13:
time: 199 us; the launch traced here: 198 us
  waiting for transfers between devices  74.5 us (37%)
  blocking collectives  49 us (25%)
  starting transfers between devices  27.1 us (14%)
  between operations  13.9 us (7%)
  local copies, waits for them, and re-layouts  13.8 us (7%)
  Pallas kernels  8.4 us (4%)
  matrix products  6.01 us (3%)
  other arithmetic  4.78 us (2%)
    all_gather x1, waiting for transfers between devices, per_device(): features = lax.all_gather(pair, ('y', 'c'), axis=1, tiled=True)  36.6 us
    all_to_all x1, blocking collectives, per_device(): last_terms = lax.all_to_all(last_term, GX, 0, 0, tiled=True)  28.6 us
    all_gather x1, blocking collectives, per_device(): pair = lax.all_gather(layer_input, 'zh', axis=1, tiled=True)  20.4 us
    all_to_all x1, waiting for transfers between devices, per_device(): packed = lax.all_to_all(packed, GX, 0, 0, tiled=True)  15.1 us
    all_to_all x1, starting transfers between devices, per_device(): stats = lax.all_to_all(spread, GY, 0, 0, tiled=True)  13.8 us
    unnamed x4, waiting for transfers between devices  11.5 us
    all_to_all x1, waiting for transfers between devices, per_device(): lax.all_to_all(jnp.broadcast_to(last_row[None], (n_gy, block_cols)), GY,...  11.3 us
    pallas_call x1, Pallas kernels, attend(): pl.pallas_call(functools.partial(attention_kernel, cache_blocks, key_rows...  8.4 us
  transfers between devices with their start and end apart: 6, of which 4 were waited for; matrix products, arithmetic and copies ran while one was open for 6% of the time, Pallas kernels for 0%

profile of v13, /device:TPU:1, one launch (start us, length us, event | category | flops | bytes accessed | tf_op | source)
XLA Modules:
  0.0 197.5 jit_solution(17322475796381856076)
XLA Ops:
  7.2 20.4 %all_gather.6 = bf16[512,256]{1,0:T(8,128)(2,1)} all-gather(bf16[512,128]{1,0:T(8,128)(2,1)} %param.7), channel_id=1, replica_groups=mesh['y'=4,'zh'=2,'c'=2,'zl'=8,'x'=4] {'zh'}, dimensions={1}, use_global_device_ids=true | all-gather | bytes 393216 | tf_op jit(solution)/shard_map/all_gather | solution.py:121
  27.7 2.9 %copy.51 = bf16[4,2,2,128,3,128]{5,3,2,1,0,4:T(8,128)(2,1)} copy(bf16[4,2,2,128,3,128]{5,3,1,2,0,4:T(8,128)(2,1)} %bitcast.51) | data formatting | bytes 3145728 | tf_op jit(solution)/shard_map/transpose | solution.py:124
  30.8 0.8 copy-done.4
  32.6 1.4 slice_bitcast_fusion
  33.9 36.6 %all-gather.2.cloned.1.call-done = bf16[512,2048]{1,0:T(8,128)(2,1)} async-done(((bf16[512,256]{1,0:T(8,128)(2,1)}), bf16[512,2048]{1,0:T(8,128)(2,1)}) %all-gather.2.cloned.1.call-update) | async-done | bytes 2097168 | tf_op jit(solution)/shard_map/all_gather | solution.py:122
  70.6 2.2 %fusion = f32[512]{0:T(512)S(1)} fusion(bf16[512,2048]{1,0:T(8,128)(2,1)} %all-gather.2.cloned.1.call-done), kind=kLoop, calls=%fused_computation.2 | loop fusion | flops 3145216 | bytes 2099200 | tf_op jit(solution)/shard_map/reduce_sum | solution.py:128
  72.8 2.7 %fusion.6 = bf16[512,3,128]{2,0,1:T(8,128)(2,1)S(1)} fusion(bf16[2048,3,128]{2,0,1:T(8,128)(2,1)} %bitcast.52, bf16[512,2048]{1,0:T(8,128)(2,1)S(1)} %copy-done.1, f32[512]{0:T(512)S(1)} %add_rsqrt_fusion), kind=kOutput, calls=%fused_computation.9 | convolution fusion | flops 808648704 | bytes 4065280 | tf_op jit(solution)/shard_map/td,dcf->tcf/dot_general | solution.py:130
  75.5 0.7 slice_bitcast_fusion.2
  76.3 8.4 %shard_map.102 = bf16[512,128]{1,0:T(8,128)(2,1)} custom-call(s32[1]{0:T(128)} %dynamic_slice.4.len_ref, bf16[512,128]{1,0:T(8,128)(2,1)} %get-tuple-element.50.q_ref, bf16[3584,128]{1,0:T(8,128)(2,1)} %get-tuple-element.47.kc_ref, bf16[3584,128]{1,0:T(8,128)(2,1)} %get-tuple-element.46.vc_ref, bf16[512,128]{1,0:T(8,128)(2,1)} %get-tuple-element.49.kn_ref, ...), custom_call_target="tpu_custom_call" | custom-call | tf_op jit(solution)/shard_map/pallas_call | solution.py:80
  84.7 3.0 %convolution_convert_fusion = bf16[512,2048]{1,0:T(8,128)(2,1)} fusion(bf16[512,128]{1,0:T(8,128)(2,1)} %shard_map.102, bf16[128,2048]{0,1:T(8,128)(2,1)S(1)} %bitcast.50), kind=kOutput, calls=%fused_computation.4 | convolution fusion | flops 269484032 | bytes 2752512 | tf_op jit(solution)/shard_map/dot_general | solution.py:152
  87.7 0.8 slice_reduce_fusion.2
  88.5 28.6 %all_to_all.29 = bf16[16,1,128]{2,1,0:T(2,128)(2,1)S(1)} all-to-all(bf16[16,1,128]{2,1,0:T(2,128)(2,1)S(1)} %copy.56), channel_id=1, replica_groups=mesh['y'=4,'zh'=2,'c'=2,'zl'=8,'x'=4] {'y','zh','c'}, dimensions={0} | all-to-all | bytes 8192 | tf_op jit(solution)/shard_map/all_to_all | solution.py:156
  117.8 6.5 %all-to-all-start.1 = ((bf16[32,1,128]{2,1,0:T(2,128)(2,1)}), bf16[32,1,128]{2,1,0:T(2,128)(2,1)S(1)}, u32[]{:S(2)}, u32[]{:S(2)}) async-start(bf16[32,1,128]{2,1,0:T(2,128)(2,1)} %broadcast_in_dim.6), calls=%async_computation.1 | async-start | bytes 32768 | tf_op jit(solution)/shard_map/all_to_all | solution.py:160
  124.3 11.3 %all-to-all-done.1 = bf16[32,1,128]{2,1,0:T(2,128)(2,1)S(1)} async-done(((bf16[32,1,128]{2,1,0:T(2,128)(2,1)}), bf16[32,1,128]{2,1,0:T(2,128)(2,1)S(1)}, u32[]{:S(2)}, u32[]{:S(2)}) %all-to-all-start.1) | async-done | bytes 8224 | tf_op jit(solution)/shard_map/all_to_all | solution.py:160
  136.2 0.9 all_to_all.22
  137.1 6.8 %all-to-all-start.2 = ((f32[16,2,2377]{2,1,0:T(2,128)}), f32[16,2,2377]{2,1,0:T(2,128)S(1)}, u32[]{:S(2)}, u32[]{:S(2)}) async-start(f32[16,2,2377]{2,1,0:T(2,128)} %all_to_all.22), calls=%async_computation.3 | async-start | bytes 622592 | tf_op jit(solution)/shard_map/all_to_all | solution.py:170
  143.9 1.8 copy.61
  145.8 15.1 %all-to-all-done.2 = f32[16,2,2377]{2,1,0:T(2,128)S(1)} async-done(((f32[16,2,2377]{2,1,0:T(2,128)}), f32[16,2,2377]{2,1,0:T(2,128)S(1)}, u32[]{:S(2)}, u32[]{:S(2)}) %all-to-all-start.2) | async-done | bytes 304288 | tf_op jit(solution)/shard_map/all_to_all | solution.py:170
  161.4 0.6 broadcast_in_dim.8
  162.0 13.8 %all-to-all-start.3 = ((f32[32,2,2]{2,1,0:T(2,128)}), f32[32,2,2]{2,1,0:T(2,128)S(1)}, u32[]{:S(2)}, u32[]{:S(2)}) async-start(f32[32,2,2]{2,1,0:T(2,128)} %broadcast_in_dim.8), calls=%async_computation.4 | async-start | bytes 65536 | tf_op jit(solution)/shard_map/all_to_all | solution.py:177
  175.8 1.0 copy.60
  176.8 11.4 %reduce-scatter.7.cloned.1.call-done = bf16[128,512]{1,0:T(8,128)(2,1)} async-done(((bf16[256,512]{1,0:T(8,128)(2,1)}), bf16[128,512]{1,0:T(8,128)(2,1)}) %reduce-scatter.7.cloned.1.call-update) | async-done | bytes 131088
  188.2 1.0 copy.62
  190.3 0.7 add_convert_fusion
  (44 shorter events, 4.3 us)
Async XLA Ops:
  7.2 128.7 %copy-start = (bf16[2376,128]{1,0:T(8,128)(2,1)S(1)}, bf16[2376,128]{1,0:T(8,128)(2,1)}, u32[]{:S(2)}) copy-start(bf16[2376,128]{1,0:T(8,128)(2,1)} %param.13) | copy-start | bytes 1824772
  7.2 63.4 %all-gather.2.cloned.1.call-start = ((), (), s32[]{:S(2)}) async-start(), calls=%async_computation.6 | async-start | bytes 2359296 | tf_op jit(solution)/shard_map/all_gather | solution.py:122
  27.6 108.6 %reduce-scatter.5.cloned.1.call-start = ((), (), s32[]{:S(2)}) async-start(), calls=%async_computation.7 | async-start | bytes 2359296 | tf_op jit(solution)/shard_map/reduce_scatter | solution.py:153
  27.7 2.9 %copy-start.2 = (bf16[1,3584,2,128]{3,2,1,0:T(2,128)(2,1)S(1)}, bf16[1,3584,2,128]{3,2,1,0:T(2,128)(2,1)}, u32[]{:S(2)}) copy-start(bf16[1,3584,2,128]{3,2,1,0:T(2,128)(2,1)} %param.10) | copy-start | bytes 5505028
  30.6 1.0 copy-start.4
  30.6 1.4 copy-start.5
  70.6 2.2 %copy-start.1 = (bf16[512,2048]{1,0:T(8,128)(2,1)S(1)}, bf16[512,2048]{1,0:T(8,128)(2,1)}, u32[]{:S(2)}) copy-start(bf16[512,2048]{1,0:T(8,128)(2,1)} %all-gather.2.cloned.1.call-done) | copy-start | bytes 6291460
  84.7 32.5 %copy-start.3 = (bf16[512,128]{1,0:T(8,128)(2,1)S(1)}, bf16[512,128]{1,0:T(8,128)(2,1)}, u32[]{:S(2)}) copy-start(bf16[512,128]{1,0:T(8,128)(2,1)} %param.7) | copy-start | bytes 393220
  84.7 39.6 %copy-start.6 = (bf16[128]{0:T(256)(128)(2,1)S(1)}, bf16[128]{0:T(256)(128)(2,1)}, u32[]{:S(2)}) copy-start(bf16[128]{0:T(256)(128)(2,1)} %param.12) | copy-start | bytes 772
  117.8 17.8 %all-to-all-start.1 = ((bf16[32,1,128]{2,1,0:T(2,128)(2,1)}), bf16[32,1,128]{2,1,0:T(2,128)(2,1)S(1)}, u32[]{:S(2)}, u32[]{:S(2)}) async-start(bf16[32,1,128]{2,1,0:T(2,128)(2,1)} %broadcast_in_dim.6), calls=%async_computation.1 | async-start | bytes 32768 | tf_op jit(solution)/shard_map/all_to_all | solution.py:160
  137.1 23.7 %all-to-all-start.2 = ((f32[16,2,2377]{2,1,0:T(2,128)}), f32[16,2,2377]{2,1,0:T(2,128)S(1)}, u32[]{:S(2)}, u32[]{:S(2)}) async-start(f32[16,2,2377]{2,1,0:T(2,128)} %all_to_all.22), calls=%async_computation.3 | async-start | bytes 622592 | tf_op jit(solution)/shard_map/all_to_all | solution.py:170
  143.9 44.3 %reduce-scatter.7.cloned.1.call-start = ((), (), s32[]{:S(2)}) async-start(), calls=%async_computation.8 | async-start | bytes 393216
  162.0 27.2 %all-to-all-start.3 = ((f32[32,2,2]{2,1,0:T(2,128)}), f32[32,2,2]{2,1,0:T(2,128)S(1)}, u32[]{:S(2)}, u32[]{:S(2)}) async-start(f32[32,2,2]{2,1,0:T(2,128)} %broadcast_in_dim.8), calls=%async_computation.4 | async-start | bytes 65536 | tf_op jit(solution)/shard_map/all_to_all | solution.py:177
Sparse Core Ops, SparseCore 0:
  27.8 42.7 all-gather.1
  87.8 40.1 reduce-scatter.4
  147.5 40.6 reduce-scatter.6

commit v14 on v13

--- a/solution.py
+++ b/solution.py
@@ -74,7 +74,7 @@
 
 def attend(queries, cache_keys, cache_values, new_keys, new_values, live_slots):
     rows, width = queries.shape
-    key_rows = cache_keys.shape[0] // 4 if cache_keys.shape[0] % (4 * 128) == 0 else rows
+    key_rows = cache_keys.shape[0] // 2 if cache_keys.shape[0] % (2 * 128) == 0 else rows
     cache_blocks = cache_keys.shape[0] // key_rows
     last = cache_blocks - 1
     return pl.pallas_call(

time: 199 us -> 199 us (level)
  no operation moved by 1% of the time
where the time goes in v14:
time: 199 us; the launch traced here: 198 us
  waiting for transfers between devices  74.4 us (37%)
  blocking collectives  49 us (25%)
  starting transfers between devices  26.3 us (13%)
  between operations  13.9 us (7%)
  local copies, waits for them, and re-layouts  13.8 us (7%)
  Pallas kernels  9.77 us (5%)
  matrix products  6.02 us (3%)
  other arithmetic  4.78 us (2%)
    all_gather x1, waiting for transfers between devices, per_device(): features = lax.all_gather(pair, ('y', 'c'), axis=1, tiled=True)  36.6 us
    all_to_all x1, blocking collectives, per_device(): last_terms = lax.all_to_all(last_term, GX, 0, 0, tiled=True)  28.6 us
    all_gather x1, blocking collectives, per_device(): pair = lax.all_gather(layer_input, 'zh', axis=1, tiled=True)  20.4 us
    all_to_all x1, waiting for transfers between devices, per_device(): packed = lax.all_to_all(packed, GX, 0, 0, tiled=True)  15.1 us
    all_to_all x1, starting transfers between devices, per_device(): stats = lax.all_to_all(spread, GY, 0, 0, tiled=True)  13.8 us
    unnamed x4, waiting for transfers between devices  11.4 us
    all_to_all x1, waiting for transfers between devices, per_device(): lax.all_to_all(jnp.broadcast_to(last_row[None], (n_gy, block_cols)), GY,...  11.3 us
    pallas_call x1, Pallas kernels, attend(): pl.pallas_call(functools.partial(attention_kernel, cache_blocks, key_rows...  9.77 us
  transfers between devices with their start and end apart: 6, of which 4 were waited for; matrix products, arithmetic and copies ran while one was open for 6% of the time, Pallas kernels for 0%

profile of v14, /device:TPU:1, one launch (start us, length us, event | category | flops | bytes accessed | tf_op | source)
XLA Modules:
  0.0 198.0 jit_solution(11875654319881393347)
XLA Ops:
  7.2 20.4 %all_gather.6 = bf16[512,256]{1,0:T(8,128)(2,1)} all-gather(bf16[512,128]{1,0:T(8,128)(2,1)} %param.7), channel_id=1, replica_groups=mesh['y'=4,'zh'=2,'c'=2,'zl'=8,'x'=4] {'zh'}, dimensions={1}, use_global_device_ids=true | all-gather | bytes 393216 | tf_op jit(solution)/shard_map/all_gather | solution.py:121
  27.7 2.9 %copy.51 = bf16[4,2,2,128,3,128]{5,3,2,1,0,4:T(8,128)(2,1)} copy(bf16[4,2,2,128,3,128]{5,3,1,2,0,4:T(8,128)(2,1)} %bitcast.51) | data formatting | bytes 3145728 | tf_op jit(solution)/shard_map/transpose | solution.py:124
  30.8 0.8 copy-done.4
  32.6 1.4 slice_bitcast_fusion
  33.9 36.6 %all-gather.2.cloned.1.call-done = bf16[512,2048]{1,0:T(8,128)(2,1)} async-done(((bf16[512,256]{1,0:T(8,128)(2,1)}), bf16[512,2048]{1,0:T(8,128)(2,1)}) %all-gather.2.cloned.1.call-update) | async-done | bytes 2097168 | tf_op jit(solution)/shard_map/all_gather | solution.py:122
  70.6 2.2 %fusion = f32[512]{0:T(512)S(1)} fusion(bf16[512,2048]{1,0:T(8,128)(2,1)} %all-gather.2.cloned.1.call-done), kind=kLoop, calls=%fused_computation.2 | loop fusion | flops 3145216 | bytes 2099200 | tf_op jit(solution)/shard_map/reduce_sum | solution.py:128
  72.8 2.7 %fusion.6 = bf16[512,3,128]{2,0,1:T(8,128)(2,1)S(1)} fusion(bf16[2048,3,128]{2,0,1:T(8,128)(2,1)} %bitcast.52, bf16[512,2048]{1,0:T(8,128)(2,1)S(1)} %copy-done.1, f32[512]{0:T(512)S(1)} %add_rsqrt_fusion), kind=kOutput, calls=%fused_computation.9 | convolution fusion | flops 808648704 | bytes 4065280 | tf_op jit(solution)/shard_map/td,dcf->tcf/dot_general | solution.py:130
  75.5 0.7 slice_bitcast_fusion.2
  76.3 9.8 %shard_map.102 = bf16[512,128]{1,0:T(8,128)(2,1)} custom-call(s32[1]{0:T(128)} %dynamic_slice.4.len_ref, bf16[512,128]{1,0:T(8,128)(2,1)} %get-tuple-element.50.q_ref, bf16[3584,128]{1,0:T(8,128)(2,1)} %get-tuple-element.47.kc_ref, bf16[3584,128]{1,0:T(8,128)(2,1)} %get-tuple-element.46.vc_ref, bf16[512,128]{1,0:T(8,128)(2,1)} %get-tuple-element.49.kn_ref, ...), custom_call_target="tpu_custom_call" | custom-call | tf_op jit(solution)/shard_map/pallas_call | solution.py:80
  86.0 3.0 %convolution_convert_fusion = bf16[512,2048]{1,0:T(8,128)(2,1)} fusion(bf16[512,128]{1,0:T(8,128)(2,1)} %shard_map.102, bf16[128,2048]{0,1:T(8,128)(2,1)S(1)} %bitcast.50), kind=kOutput, calls=%fused_computation.4 | convolution fusion | flops 269484032 | bytes 2752512 | tf_op jit(solution)/shard_map/dot_general | solution.py:152
  89.1 0.8 slice_reduce_fusion.2
  89.9 28.6 %all_to_all.29 = bf16[16,1,128]{2,1,0:T(2,128)(2,1)S(1)} all-to-all(bf16[16,1,128]{2,1,0:T(2,128)(2,1)S(1)} %copy.56), channel_id=1, replica_groups=mesh['y'=4,'zh'=2,'c'=2,'zl'=8,'x'=4] {'y','zh','c'}, dimensions={0} | all-to-all | bytes 8192 | tf_op jit(solution)/shard_map/all_to_all | solution.py:156
  119.1 5.0 %all-to-all-start.1 = ((bf16[32,1,128]{2,1,0:T(2,128)(2,1)}), bf16[32,1,128]{2,1,0:T(2,128)(2,1)S(1)}, u32[]{:S(2)}, u32[]{:S(2)}) async-start(bf16[32,1,128]{2,1,0:T(2,128)(2,1)} %broadcast_in_dim.6), calls=%async_computation.1 | async-start | bytes 32768 | tf_op jit(solution)/shard_map/all_to_all | solution.py:160
  124.2 11.3 %all-to-all-done.1 = bf16[32,1,128]{2,1,0:T(2,128)(2,1)S(1)} async-done(((bf16[32,1,128]{2,1,0:T(2,128)(2,1)}), bf16[32,1,128]{2,1,0:T(2,128)(2,1)S(1)}, u32[]{:S(2)}, u32[]{:S(2)}) %all-to-all-start.1) | async-done | bytes 8224 | tf_op jit(solution)/shard_map/all_to_all | solution.py:160
  136.1 0.9 all_to_all.22
  137.0 7.4 %all-to-all-start.2 = ((f32[16,2,2377]{2,1,0:T(2,128)}), f32[16,2,2377]{2,1,0:T(2,128)S(1)}, u32[]{:S(2)}, u32[]{:S(2)}) async-start(f32[16,2,2377]{2,1,0:T(2,128)} %all_to_all.22), calls=%async_computation.3 | async-start | bytes 622592 | tf_op jit(solution)/shard_map/all_to_all | solution.py:170
  144.5 1.8 copy.61
  146.3 15.1 %all-to-all-done.2 = f32[16,2,2377]{2,1,0:T(2,128)S(1)} async-done(((f32[16,2,2377]{2,1,0:T(2,128)}), f32[16,2,2377]{2,1,0:T(2,128)S(1)}, u32[]{:S(2)}, u32[]{:S(2)}) %all-to-all-start.2) | async-done | bytes 304288 | tf_op jit(solution)/shard_map/all_to_all | solution.py:170
  161.9 0.6 broadcast_in_dim.8
  162.5 13.8 %all-to-all-start.3 = ((f32[32,2,2]{2,1,0:T(2,128)}), f32[32,2,2]{2,1,0:T(2,128)S(1)}, u32[]{:S(2)}, u32[]{:S(2)}) async-start(f32[32,2,2]{2,1,0:T(2,128)} %broadcast_in_dim.8), calls=%async_computation.4 | async-start | bytes 65536 | tf_op jit(solution)/shard_map/all_to_all | solution.py:177
  176.4 1.0 copy.60
  177.4 11.3 %reduce-scatter.7.cloned.1.call-done = bf16[128,512]{1,0:T(8,128)(2,1)} async-done(((bf16[256,512]{1,0:T(8,128)(2,1)}), bf16[128,512]{1,0:T(8,128)(2,1)}) %reduce-scatter.7.cloned.1.call-update) | async-done | bytes 131088
  188.7 1.0 copy.62
  190.8 0.7 add_convert_fusion
  (44 shorter events, 4.3 us)
Async XLA Ops:
  7.2 128.5 %copy-start = (bf16[2376,128]{1,0:T(8,128)(2,1)S(1)}, bf16[2376,128]{1,0:T(8,128)(2,1)}, u32[]{:S(2)}) copy-start(bf16[2376,128]{1,0:T(8,128)(2,1)} %param.13) | copy-start | bytes 1824772
  7.2 63.4 %all-gather.2.cloned.1.call-start = ((), (), s32[]{:S(2)}) async-start(), calls=%async_computation.6 | async-start | bytes 2359296 | tf_op jit(solution)/shard_map/all_gather | solution.py:122
  27.6 108.5 %reduce-scatter.5.cloned.1.call-start = ((), (), s32[]{:S(2)}) async-start(), calls=%async_computation.7 | async-start | bytes 2359296 | tf_op jit(solution)/shard_map/reduce_scatter | solution.py:153
  27.7 2.9 %copy-start.2 = (bf16[1,3584,2,128]{3,2,1,0:T(2,128)(2,1)S(1)}, bf16[1,3584,2,128]{3,2,1,0:T(2,128)(2,1)}, u32[]{:S(2)}) copy-start(bf16[1,3584,2,128]{3,2,1,0:T(2,128)(2,1)} %param.10) | copy-start | bytes 5505028
  30.6 1.0 copy-start.4
  30.6 1.4 copy-start.5
  70.6 2.2 %copy-start.1 = (bf16[512,2048]{1,0:T(8,128)(2,1)S(1)}, bf16[512,2048]{1,0:T(8,128)(2,1)}, u32[]{:S(2)}) copy-start(bf16[512,2048]{1,0:T(8,128)(2,1)} %all-gather.2.cloned.1.call-done) | copy-start | bytes 6291460
  86.0 32.5 %copy-start.3 = (bf16[512,128]{1,0:T(8,128)(2,1)S(1)}, bf16[512,128]{1,0:T(8,128)(2,1)}, u32[]{:S(2)}) copy-start(bf16[512,128]{1,0:T(8,128)(2,1)} %param.7) | copy-start | bytes 393220
  86.0 38.1 %copy-start.6 = (bf16[128]{0:T(256)(128)(2,1)S(1)}, bf16[128]{0:T(256)(128)(2,1)}, u32[]{:S(2)}) copy-start(bf16[128]{0:T(256)(128)(2,1)} %param.12) | copy-start | bytes 772
  119.1 16.3 %all-to-all-start.1 = ((bf16[32,1,128]{2,1,0:T(2,128)(2,1)}), bf16[32,1,128]{2,1,0:T(2,128)(2,1)S(1)}, u32[]{:S(2)}, u32[]{:S(2)}) async-start(bf16[32,1,128]{2,1,0:T(2,128)(2,1)} %broadcast_in_dim.6), calls=%async_computation.1 | async-start | bytes 32768 | tf_op jit(solution)/shard_map/all_to_all | solution.py:160
  137.0 24.4 %all-to-all-start.2 = ((f32[16,2,2377]{2,1,0:T(2,128)}), f32[16,2,2377]{2,1,0:T(2,128)S(1)}, u32[]{:S(2)}, u32[]{:S(2)}) async-start(f32[16,2,2377]{2,1,0:T(2,128)} %all_to_all.22), calls=%async_computation.3 | async-start | bytes 622592 | tf_op jit(solution)/shard_map/all_to_all | solution.py:170
  144.4 44.3 %reduce-scatter.7.cloned.1.call-start = ((), (), s32[]{:S(2)}) async-start(), calls=%async_computation.8 | async-start | bytes 393216
  162.5 27.2 %all-to-all-start.3 = ((f32[32,2,2]{2,1,0:T(2,128)}), f32[32,2,2]{2,1,0:T(2,128)S(1)}, u32[]{:S(2)}, u32[]{:S(2)}) async-start(f32[32,2,2]{2,1,0:T(2,128)} %broadcast_in_dim.8), calls=%async_computation.4 | async-start | bytes 65536 | tf_op jit(solution)/shard_map/all_to_all | solution.py:177
Sparse Core Ops, SparseCore 0:
  27.8 42.7 all-gather.1
  89.2 39.3 reduce-scatter.4
  148.0 40.6 reduce-scatter.6
